TPU v7x, 128 devices: a whole 4x4x4 slice. The times are simulated.
128 devices in a mesh: freq: 8 (over z_hi, x), blk: 16 (over y, z_lo, core).
Axes of the slice: x: 4, y: 4, z: 4 (z_hi: 2, z_lo: 2; z = z_hi * 2 + z_lo), core: 2. Of those that a mesh axis runs over, the one named last changes fastest.
Arguments:
- traces: bfloat16 [2048, 2048, 256], P('blk', 'freq'), may hold values from -6 to 6
- signature: float32 [8, 2], P('freq'), may hold values from 0.5 to 1.5
Outputs:
- multiples: float32 [8, 2, 2048, 2048], P('freq', None, 'blk')
All inputs are finite; a program needn't handle non-finite values.
Results may differ from a plain program's by a relative error of at most 0.0035.
Values sent between devices are 32-bit elements; how exact they have to be, the bound alone decides.
No kernel may reach another device: no remote copies, remote signals or barrier semaphores. Data moves between devices by JAX's collectives and lax.ppermute only.
A program may use at most 256 MiB of HBM per device.

v0:
```python
import math

import jax
import jax.numpy as jnp
from jax import lax
from jax.sharding import PartitionSpec as P

BIN0 = 4
BINSTEP = 3


def make_table(freqs, samples):
    bins = BIN0 + BINSTEP * jnp.arange(freqs, dtype=jnp.int32)
    steps = jnp.arange(samples, dtype=jnp.int32)
    phase = steps[:, None] * bins[None, :] % samples
    angle = phase.astype(jnp.float32) * (2.0 * math.pi / samples)
    scale = 1.0 / math.sqrt(samples)
    table = jnp.concatenate([jnp.cos(angle) * scale, -jnp.sin(angle) * scale], axis=1)
    return table.astype(jnp.bfloat16)


def complex_dot(a_re, a_im, b_re, b_im):
    hp = lax.Precision.HIGHEST
    real_part = jnp.dot(a_re, b_re, precision=hp) - jnp.dot(a_im, b_im, precision=hp)
    imag_part = jnp.dot(a_re, b_im, precision=hp) + jnp.dot(a_im, b_re, precision=hp)
    return (real_part, imag_part)


def on_device(traces, signature):
    src_rows, rec_cols, samples = traces.shape
    freqs = lax.axis_size("freq")
    table = make_table(freqs, samples)
    projected = jnp.einsum("srt,tc->csr", traces, table, preferred_element_type=jnp.float32)
    projected = projected.reshape(2, freqs, src_rows, rec_cols)
    spectra = lax.all_to_all(projected, "freq", split_axis=1, concat_axis=3, tiled=True)
    own = spectra[:, 0]
    width = own.shape[2]
    own_re = own[0]
    own_im = own[1]
    full = lax.all_gather(own, "blk", axis=1, tiled=True)
    prod_re, prod_im = complex_dot(own_re, own_im, full[0], full[1])
    scale = 1.0 / math.sqrt(width)
    w_re = signature[0, 0]
    w_im = signature[0, 1]
    out_re = -(w_re * prod_re - w_im * prod_im) * scale
    out_im = -(w_re * prod_im + w_im * prod_re) * scale
    return jnp.stack([out_re, out_im], axis=0)[None]


def solution(mesh):
    return jax.shard_map(
        on_device,
        mesh=mesh,
        in_specs=(P("blk", "freq", None), P("freq", None)),
        out_specs=P("freq", None, "blk", None),
        check_vma=False,
    )
```

profile of v0, /device:TPU:1, one launch (start us, length us, event | category | flops | bytes accessed | tf_op | source)
XLA Modules:
  0.0 346.1 jit_solution(8752176337144553729)
XLA Ops:
  6.5 0.0 all-gather.2.cloned.1.call-start
  6.5 0.1 multiply_convert_fusion.1
  6.7 0.0 copy-start.1
  6.7 10.2 %convolution_bitcast_fusion = f32[2,8,128,256]{3,1,0,2:T(8,128)S(1)} fusion(bf16[128,256,256]{2,1,0:T(8,128)(2,1)} %param.2, bf16[256,8]{0,1:T(8,128)(2,1)S(1)} %get-tuple-element.14, bf16[256,8]{0,1:T(8,128)(2,1)S(1)} %get-tuple-element.13), kind=kOutput, calls=%fused_computation.15 | convolution fusion | flops 268451840 | bytes 18882560 | tf_op jit(solution)/shard_map/srt,tc->csr/dot_general | solution.py:33
  16.9 1.1 copy.4
  18.0 36.3 %all_to_all.15 = f32[2,8,128,256]{3,0,2,1:T(2,128)} all-to-all(f32[2,8,128,256]{3,0,2,1:T(2,128)S(1)} %copy.4), channel_id=1, replica_groups=mesh['freq'=8,'blk'=16] {'freq'}, dimensions={1} | all-to-all | bytes 4194304 | tf_op jit(solution)/shard_map/all_to_all | solution.py:35
  54.3 2.7 copy.5
  57.0 2.3 copy.6
  59.4 0.0 all-gather.2.cloned.1.call-update
  59.4 0.0 copy-done.1
  59.4 0.7 fusion.29
  60.1 1.1 fusion.28
  61.2 168.2 %all-gather.2.cloned.1.call-done = f32[2,2048,2048]{2,0,1:T(2,128)} async-done(((f32[2,128,2048]{2,0,1:T(2,128)}), f32[2,2048,2048]{2,0,1:T(2,128)}) %all-gather.2.cloned.1.call-update) | async-done | bytes 33554448 | tf_op jit(solution)/shard_map/all_gather | solution.py:40
  229.4 40.0 %fusion.27 = (f32[1,2048,2048]{2,0,1:T(1,128)}, f32[1,2048,2048]{2,0,1:T(1,128)}) fusion(f32[2,2048,2048]{2,0,1:T(2,128)} %all-gather.2.cloned.1.call-done), kind=kLoop, calls=%fused_computation.34 | loop fusion | bytes 67108864 | tf_op jit(solution)/shard_map/slice | solution.py:41
  269.4 0.0 copy-start
  269.4 0.0 slice-start
  269.4 0.0 slice-start.1
  269.4 18.8 %fusion.2 = f32[128,2048]{1,0:T(8,128)S(1)} fusion(f32[128,2048]{0,1:T(8,128)S(1)} %bitcast.45, f32[1,2048,2048]{2,0,1:T(1,128)} %get-tuple-element.6), kind=kOutput, calls=%fused_computation.2 | convolution fusion | flops 6442450944 | bytes 18874368 | tf_op jit(solution)/shard_map/dot_general | solution.py:24
  288.2 0.0 slice-start.2
  288.2 0.0 copy-done
  288.2 0.0 slice-start.3
  288.2 19.2 %fusion = f32[128,2048]{1,0:T(8,128)S(1)} fusion(f32[128,2048]{0,1:T(8,128)S(1)} %bitcast.47, f32[1,2048,2048]{2,0,1:T(1,128)} %get-tuple-element.6), kind=kOutput, calls=%fused_computation | convolution fusion | flops 6442450944 | bytes 18874368 | tf_op jit(solution)/shard_map/dot_general | solution.py:25
  307.4 0.0 slice-done
  307.5 0.0 slice-done.1
  307.5 0.0 slice-done.2
  307.5 0.0 slice-done.3
  307.5 14.1 %fusion.12 = f32[128,2048]{1,0:T(8,128)S(1)} fusion(f32[128,2048]{1,0:T(8,128)S(1)} %fusion.2, f32[128,2048]{0,1:T(8,128)S(1)} %bitcast.48, f32[1,2048,2048]{2,0,1:T(1,128)S(1)} %bitcast.42), kind=kOutput, calls=%fused_computation.12 | convolution fusion | flops 6442713088 | bytes 19922944 | tf_op jit(solution)/shard_map/dot_general | solution.py:24
  321.6 15.7 %multiply_bitcast_fusion.1 = (f32[1,128,2048]{2,1,0:T(8,128)S(1)}, f32[1,128,2048]{2,1,0:T(8,128)S(1)}) fusion(f32[128,2048]{1,0:T(8,128)S(1)} %fusion.12, f32[]{:T(128)} %bitcast.9, f32[]{:T(128)} %bitcast, f32[128,2048]{1,0:T(8,128)S(1)} %fusion, f32[128,2048]{0,1:T(8,128)S(1)} %bitcast.46, f32[1,2048,2048]{2,0,1:T(1,128)S(1)} %bitcast.42), kind=kOutput, calls=%fused_computation.17 | convolution fusion | flops 6445334528 | bytes 22020104 | tf_op jit(solution)/shard_map/dot_general | solution.py:25
  337.3 1.5 maximum_bitcast_fusion
  (2 shorter events, 0.0 us)
Async XLA Ops:
  6.5 222.8 %all-gather.2.cloned.1.call-start = ((), (), s32[]{:S(2)}) async-start(), calls=%async_computation.1 | async-start | bytes 35651584 | tf_op jit(solution)/shard_map/all_gather | solution.py:40
  6.7 52.7 %copy-start.1 = (f32[1,2]{1,0:T(1,128)S(1)}, f32[1,2]{1,0:T(1,128)}, u32[]{:S(2)}) copy-start(f32[1,2]{1,0:T(1,128)} %param.3) | copy-start | bytes 28
  269.4 18.9 %copy-start = (f32[1,1,128,8,256]{2,4,3,1,0:T(8,128)S(1)}, f32[1,1,128,8,256]{2,4,3,1,0:T(8,128)}, u32[]{:S(2)}) copy-start(f32[1,1,128,8,256]{2,4,3,1,0:T(8,128)} %get-tuple-element.9) | copy-start | bytes 3145732
  269.4 38.1 %slice-start = ((s8[16777216]{0:T(1024)(128)(4,1)}), s8[4194304]{0:T(1024)(128)(4,1)S(1)}, s32[]{:S(2)}) async-start(s8[16777216]{0:T(1024)(128)(4,1)} %bitcast.41), calls=%async_computation.2 | async-start | bytes 8388608
  269.4 38.1 %slice-start.1 = ((s8[16777216]{0:T(1024)(128)(4,1)}), s8[4194304]{0:T(1024)(128)(4,1)S(1)}, s32[]{:S(2)}) async-start(s8[16777216]{0:T(1024)(128)(4,1)} %bitcast.41), calls=%async_computation.3 | async-start | bytes 8388608
  288.2 19.3 %slice-start.2 = ((s8[16777216]{0:T(1024)(128)(4,1)}), s8[4194304]{0:T(1024)(128)(4,1)S(1)}, s32[]{:S(2)}) async-start(s8[16777216]{0:T(1024)(128)(4,1)} %bitcast.41), calls=%async_computation.4 | async-start | bytes 8388608
  288.2 19.3 %slice-start.3 = ((s8[16777216]{0:T(1024)(128)(4,1)}), s8[4194304]{0:T(1024)(128)(4,1)S(1)}, s32[]{:S(2)}) async-start(s8[16777216]{0:T(1024)(128)(4,1)} %bitcast.41), calls=%async_computation.5 | async-start | bytes 8388608
Sparse Core Ops, SparseCore 0:
  59.5 169.8 all-gather.1
where the time goes:
time: 349 us; the launch traced here: 346 us
  waiting for transfers between devices  168 us (48%)
  matrix products  78 us (22%)
  local copies, waits for them, and re-layouts  48 us (14%)
  blocking collectives  36.3 us (10%)
  between operations  14 us (4%)
    all_gather x1, waiting for transfers between devices, on_device(): full = lax.all_gather(own, 'blk', axis=1, tiled=True)  168 us
    slice x1, local copies, waits for them, and re-layouts, on_device(): prod_re, prod_im = complex_dot(own_re, own_im, full[0], full[1])  40 us
    all_to_all x1, blocking collectives, on_device(): lax.all_to_all(projected, 'freq', split_axis=1, concat_axis=3, tiled=True)  36.3 us
    dot_general x1, matrix products, complex_dot(): jnp.dot(a_re, b_im, precision=hp) + jnp.dot(a_im, b_re, precision=hp)  19.2 us
    dot_general x1, matrix products, complex_dot(): jnp.dot(a_im, b_im, precision=hp)  18.8 us
    dot_general x1, matrix products, complex_dot(): jnp.dot(a_im, b_re, precision=hp)  15.7 us
    dot_general x1, matrix products, complex_dot(): jnp.dot(a_re, b_re, precision=hp) - jnp.dot(a_im, b_im, precision=hp)  14.1 us
    dot_general x1, matrix products, on_device(): jnp.einsum('srt,tc->csr', traces, table, preferred_element_type=jnp.float32)  10.2 us
  transfers between devices with their start and end apart: 1, of which 1 were waited for; matrix products, arithmetic and copies ran while one was open for 1% of the time, Pallas kernels for 0%

commit v1 on v0

v1 whole, which is shorter than its diff:
```python
import math

import jax
import jax.numpy as jnp
from jax import lax
from jax.sharding import PartitionSpec as P

BIN0 = 4
BINSTEP = 3
GROUP = 4


def make_table(freqs, samples):
    bins = BIN0 + BINSTEP * jnp.arange(freqs, dtype=jnp.int32)
    steps = jnp.arange(samples, dtype=jnp.int32)
    phase = steps[:, None] * bins[None, :] % samples
    angle = phase.astype(jnp.float32) * (2.0 * math.pi / samples)
    scale = 1.0 / math.sqrt(samples)
    table = jnp.concatenate([jnp.cos(angle) * scale, -jnp.sin(angle) * scale], axis=1)
    return table.astype(jnp.bfloat16)


def xor_perm(n, m):
    return [(i, i ^ m) for i in range(n)]


def shift_perm(n, s):
    return [(i, (i + s) % n) for i in range(n)]


def on_device(traces, signature):
    src_rows, rec_cols, samples = traces.shape
    freqs = lax.axis_size("freq")
    nblk = lax.axis_size("blk")
    ny = nblk // GROUP
    assert ny == 4 and nblk % GROUP == 0
    table = make_table(freqs, samples)
    projected = jnp.einsum("srt,tc->csr", traces, table, preferred_element_type=jnp.float32)
    projected = projected.reshape(2, freqs, src_rows, rec_cols)
    spectra = lax.all_to_all(projected, "freq", split_axis=1, concat_axis=3, tiled=True)
    own = spectra[:, 0]
    n = own.shape[2]
    rb = src_rows
    gw = GROUP * rb
    cw = n // GROUP

    b = lax.axis_index("blk")
    p = b % GROUP
    y = b // GROUP

    q1 = lax.ppermute(own, "blk", xor_perm(nblk, 1))
    q2 = lax.ppermute(own, "blk", xor_perm(nblk, 2))
    q3 = lax.ppermute(q2, "blk", xor_perm(nblk, 1))
    rows = jnp.concatenate([own, q1, q2, q3], axis=1)

    piece = lax.dynamic_slice_in_dim(rows, p * cw, cw, axis=2)

    l5 = rows.reshape(2, gw, ny, GROUP, rb)
    lx = jnp.concatenate(
        [lax.dynamic_slice_in_dim(l5, p ^ m, 1, axis=3) for m in range(GROUP)], axis=3
    ).reshape(2, gw, n)

    def contrib(g, pc, lo, hi):
        lg = lax.dynamic_slice_in_dim(lx, g * gw + lo * rb, (hi - lo) * rb, axis=2)
        return jnp.einsum(
            "aik,bkj->abij", lg, pc,
            precision=lax.Precision.HIGH, preferred_element_type=jnp.float32,
        )

    up = shift_perm(nblk, GROUP)
    dn = shift_perm(nblk, -GROUP)
    r_up = lax.ppermute(piece, "blk", up)
    r_dn = lax.ppermute(piece, "blk", dn)
    half = gw // 2
    f_up = lax.ppermute(r_up[:, :half], "blk", up)
    f_dn = lax.ppermute(r_dn[:, half:], "blk", dn)

    t = contrib(y, piece, 0, GROUP)
    t = t + contrib((y - 1) % ny, r_up, 0, GROUP)
    t = t + contrib((y + 1) % ny, r_dn, 0, GROUP)
    t = t + contrib((y + 2) % ny, f_up, 0, GROUP // 2)
    t = t + contrib((y + 2) % ny, f_dn, GROUP // 2, GROUP)

    prod_re = t[0, 0] - t[1, 1]
    prod_im = t[0, 1] + t[1, 0]
    scale = 1.0 / math.sqrt(n)
    w_re = signature[0, 0]
    w_im = signature[0, 1]
    out_re = -(w_re * prod_re - w_im * prod_im) * scale
    out_im = -(w_re * prod_im + w_im * prod_re) * scale
    blk_out = jnp.stack([out_re, out_im], axis=0)

    parts = [blk_out[:, :rb]]
    for m in range(1, GROUP):
        parts.append(lax.ppermute(blk_out[:, m * rb:(m + 1) * rb], "blk", xor_perm(nblk, m)))
    stacked = jnp.stack(parts, axis=0)
    ordered = [lax.dynamic_index_in_dim(stacked, p ^ i, 0, keepdims=False) for i in range(GROUP)]
    out = jnp.concatenate(ordered, axis=2)
    return out[None]


def solution(mesh):
    return jax.shard_map(
        on_device,
        mesh=mesh,
        in_specs=(P("blk", "freq", None), P("freq", None)),
        out_specs=P("freq", None, "blk", None),
        check_vma=False,
    )
```

time: 349 us -> 227 us (0.65)
  waiting for transfers between devices: 168 us -> 120 us
  matrix products: 78 us -> 33.6 us
  local copies, waits for them, and re-layouts: 48 us -> 9.57 us
  starting transfers between devices: 0.01 us -> 15.2 us
  between operations: 14 us -> 0.18 us
  other arithmetic: 1.6 us -> 12.8 us
    all_gather x1 -> x0, waiting for transfers between devices: 168 us -> none  [on_device(): full = lax.all_gather(own, 'blk', axis=1, tiled=True)]
    ppermute x0 -> x10, waiting for transfers between devices: none -> 120 us  [the longest x1 42.8 us: on_device(): q2 = lax.ppermute(own, 'blk', xor_perm(nblk, 2))]
    dot_general x4 -> x5, matrix products: 67.8 us -> 23.4 us  [contrib(): jnp.einsum('aik,bkj->abij', lg, pc, precision=lax.Precision.HIGH, preferr...]
    slice x3, local copies, waits for them, and re-layouts: 41.8 us -> 3.2 us  [the longest x1 1.29 us: on_device(): f_dn = lax.ppermute(r_dn[:, half:], 'blk', dn)]
    ppermute x0 -> x10, starting transfers between devices: none -> 15.2 us  [the longest x3 4.04 us: on_device(): lax.ppermute(blk_out[:, m * rb:(m + 1) * rb], 'blk', xor_perm(nblk, m))]
    concatenate x0 -> x3, other arithmetic: none -> 7.2 us  [the longest x2 5.96 us: on_device(): rows = jnp.concatenate([own, q1, q2, q3], axis=1)]
    mul x0 -> x2, other arithmetic: none -> 3.62 us  [the longest x1 1.81 us: on_device(): out_im = -(w_re * prod_im + w_im * prod_re) * scale]
  transfers between devices with their start and end apart: 1 -> 10, of which waited for: 1 -> 6; matrix products, arithmetic and copies ran while one was open for 1% -> 9% of each run, Pallas kernels for 0% -> 0%
where the time goes in v1:
time: 227 us
  waiting for transfers between devices  120 us (53%)
  blocking collectives  35.7 us (16%)
  matrix products  33.6 us (15%)
  starting transfers between devices  15.2 us (7%)
  other arithmetic  12.8 us (6%)
  local copies, waits for them, and re-layouts  9.57 us (4%)
    ppermute x1, waiting for transfers between devices, on_device(): q2 = lax.ppermute(own, 'blk', xor_perm(nblk, 2))  42.8 us
    ppermute x1, waiting for transfers between devices, on_device(): r_up = lax.ppermute(piece, 'blk', up)  40.4 us
    all_to_all x1, blocking collectives, on_device(): lax.all_to_all(projected, 'freq', split_axis=1, concat_axis=3, tiled=True)  35.7 us
    dot_general x5, matrix products, contrib(): jnp.einsum('aik,bkj->abij', lg, pc, precision=lax.Precision.HIGH, preferr...  23.4 us
    ppermute x3, waiting for transfers between devices, on_device(): lax.ppermute(blk_out[:, m * rb:(m + 1) * rb], 'blk', xor_perm(nblk, m))  23.2 us
    dot_general x1, matrix products, on_device(): jnp.einsum('srt,tc->csr', traces, table, preferred_element_type=jnp.float32)  10.2 us
    ppermute x1, waiting for transfers between devices, on_device(): f_up = lax.ppermute(r_up[:, :half], 'blk', up)  9.13 us
    concatenate x2, other arithmetic, on_device(): rows = jnp.concatenate([own, q1, q2, q3], axis=1)  5.96 us
  transfers between devices with their start and end apart: 10, of which 6 were waited for; matrix products, arithmetic and copies ran while one was open for 9% of the time, Pallas kernels for 0%

profile of v1, /device:TPU:1, one launch (start us, length us, event | category | flops | bytes accessed | tf_op | source)
XLA Modules:
  0.0 226.6 jit_solution(9673138914343612404)
XLA Ops:
  0.0 0.1 multiply_convert_fusion.1
  0.1 10.2 %convolution_bitcast_fusion = f32[2,8,128,256]{3,1,0,2:T(8,128)S(1)} fusion(bf16[128,256,256]{2,1,0:T(8,128)(2,1)} %param.2, bf16[256,8]{0,1:T(8,128)(2,1)S(1)} %get-tuple-element.18, bf16[256,8]{0,1:T(8,128)(2,1)S(1)} %get-tuple-element.17), kind=kOutput, calls=%fused_computation.29 | convolution fusion | flops 268451840 | bytes 18882560 | tf_op jit(solution)/shard_map/srt,tc->csr/dot_general | solution.py:38
  10.4 1.1 copy.44
  11.5 35.7 %all_to_all.15 = f32[2,8,128,256]{3,0,2,1:T(2,128)} all-to-all(f32[2,8,128,256]{3,0,2,1:T(2,128)S(1)} %copy.44), channel_id=1, replica_groups=mesh['freq'=8,'blk'=16] {'freq'}, dimensions={1} | all-to-all | bytes 4194304 | tf_op jit(solution)/shard_map/all_to_all | solution.py:40
  47.2 2.7 %copy.45 = f32[2,8,128,256]{2,3,1,0:T(8,128)S(1)} copy(f32[2,8,128,256]{3,0,2,1:T(2,128)} %all_to_all.15) | data formatting | bytes 4194304 | tf_op jit(solution)/shard_map/all_to_all | solution.py:40
  49.9 0.8 collective-permute-start.1
  50.7 2.0 collective-permute-start
  52.8 42.8 %collective-permute-done.1 = f32[2,128,2048]{1,2,0:T(8,128)} collective-permute-done((f32[2,128,2048]{1,2,0:T(8,128)S(1)}, f32[2,128,2048]{1,2,0:T(8,128)}, u32[]{:S(2)}, u32[]{:S(2)}) %collective-permute-start.1) | collective-permute-done | bytes 2097184 | tf_op jit(solution)/shard_map/ppermute | solution.py:52
  95.5 2.6 %collective-permute-start.2 = (f32[2,128,2048]{1,2,0:T(8,128)}, f32[2,128,2048]{1,2,0:T(8,128)}, u32[]{:S(2)}, u32[]{:S(2)}) collective-permute-start(f32[2,128,2048]{1,2,0:T(8,128)} %collective-permute-done.1), channel_id=1, source_target_pairs={{0,1},{1,0},{2,3},{3,2},{4,5},{5,4},{6,7},{7,6},{8,9},{9,8},{10,11... | collective-permute-start | bytes 6291464 | tf_op jit(solution)/shard_map/ppermute | solution.py:53
  98.1 0.0 collective-permute-done
  98.1 4.1 %collective-permute-done.2 = f32[2,128,2048]{1,2,0:T(8,128)} collective-permute-done((f32[2,128,2048]{1,2,0:T(8,128)}, f32[2,128,2048]{1,2,0:T(8,128)}, u32[]{:S(2)}, u32[]{:S(2)}) %collective-permute-start.2) | collective-permute-done | bytes 2097184 | tf_op jit(solution)/shard_map/ppermute | solution.py:53
  102.3 2.8 %fusion.2 = f32[2,512,512]{1,2,0:T(8,128)} fusion(s32[]{:T(128)S(6)} %select_n.70, f32[2,128,2048]{1,2,0:T(8,128)S(1)} %bitcast.124, f32[2,128,2048]{1,2,0:T(8,128)} %collective-permute-done, f32[2,128,2048]{1,2,0:T(8,128)} %collective-permute-done.1, f32[2,128,2048]{1,2,0:T(8,128)} %collective-permute-done.2), kind=kLoop, calls=%fused_computation.15 | loop fusion | flops 1572864 | bytes 10485764 | tf_op jit(solution)/shard_map/concatenate | solution.py:54
  105.1 1.3 collective-permute-start.3
  106.4 1.4 collective-permute-start.4
  107.8 0.0 copy-done
  107.8 0.6 fusion.48
  108.4 3.1 %pad_maximum_fusion = f32[2,512,4,4,128]{1,4,3,2,0:T(8,128)S(1)} fusion(f32[2,128,4,4,128]{1,4,3,2,0:T(8,128)} %bitcast.13, f32[2,128,4,4,128]{1,4,3,2,0:T(8,128)} %bitcast.12, f32[2,128,4,4,128]{1,4,3,2,0:T(8,128)} %bitcast.11, f32[2,128,4,4,128]{1,4,3,2,0:T(8,128)S(1)} %bitcast.125), kind=kLoop, calls=%fused_computation.4 | loop fusion | flops 6291456 | bytes 16777216 | tf_op jit(solution)/shard_map/concatenate | solution.py:54
  111.6 1.6 constant_dynamic-slice_fusion.7
  113.2 40.4 %collective-permute-done.3 = f32[2,512,512]{1,2,0:T(8,128)} collective-permute-done((f32[2,512,512]{1,2,0:T(8,128)}, f32[2,512,512]{1,2,0:T(8,128)}, u32[]{:S(2)}, u32[]{:S(2)}) %collective-permute-start.3) | collective-permute-done | bytes 2097184 | tf_op jit(solution)/shard_map/ppermute | solution.py:72
  153.5 1.3 slice.48
  154.8 0.1 collective-permute-start.5
  154.9 1.2 pad_maximum_fusion.1
  156.2 0.0 collective-permute-done.4
  156.2 1.3 slice.49
  157.5 2.9 %collective-permute-start.6 = (f32[2,256,512]{1,2,0:T(8,128)S(1)}, f32[2,256,512]{1,2,0:T(8,128)S(1)}, u32[]{:S(2)}, u32[]{:S(2)}) collective-permute-start(f32[2,256,512]{1,2,0:T(8,128)S(1)} %slice.49), channel_id=1, source_target_pairs={{0,12},{1,13},{2,14},{3,15},{4,0},{5,1},{6,2},{7,3},{8,4},{9,5},{1... | collective-permute-start | bytes 3145736 | tf_op jit(solution)/shard_map/ppermute | solution.py:76
  160.4 5.1 %fusion.5 = f32[2,512,2,512]{3,1,2,0:T(8,128)S(1)} fusion(f32[2,512,512]{1,2,0:T(8,128)} %collective-permute-done.3, f32[2,512,2048]{1,2,0:T(8,128)S(1)} %bitcast.117, s32[]{:T(128)S(6)} %select_n.78), kind=kOutput, calls=%fused_computation.20 | convolution fusion | flops 3221225472 | bytes 8388612 | tf_op jit(solution)/shard_map/aik,bkj->abij/dot_general | solution.py:65
  165.5 5.1 %fusion.3 = f32[2,512,2,512]{3,1,2,0:T(8,128)S(1)} fusion(f32[2,512,512]{1,2,0:T(8,128)} %collective-permute-done.4, f32[2,512,2048]{1,2,0:T(8,128)S(1)} %bitcast.118, s32[]{:T(128)S(6)} %select_n.80), kind=kOutput, calls=%fused_computation.18 | convolution fusion | flops 3221225472 | bytes 8388612 | tf_op jit(solution)/shard_map/aik,bkj->abij/dot_general | solution.py:65
  170.5 9.1 %collective-permute-done.5 = f32[2,256,512]{1,2,0:T(8,128)S(1)} collective-permute-done((f32[2,256,512]{1,2,0:T(8,128)S(1)}, f32[2,256,512]{1,2,0:T(8,128)S(1)}, u32[]{:S(2)}, u32[]{:S(2)}) %collective-permute-start.5) | collective-permute-done | bytes 1048608 | tf_op jit(solution)/shard_map/ppermute | solution.py:75
  179.7 1.8 fusion.17
  181.5 0.0 collective-permute-done.6
  181.5 3.8 %fusion.15 = f32[2,512,2,512]{3,1,2,0:T(8,128)} fusion(f32[2,256,512]{1,2,0:T(8,128)S(1)} %collective-permute-done.6, f32[2,512,2048]{1,2,0:T(8,128)S(1)} %bitcast.120, s32[]{:T(128)S(6)} %select_n.83), kind=kOutput, calls=%fused_computation.34 | convolution fusion | flops 1610612736 | bytes 6291460 | tf_op jit(solution)/shard_map/aik,bkj->abij/dot_general | solution.py:65
  185.3 7.7 %add_bitcast_fusion = f32[2,2,512,512]{2,3,0,1:T(8,128)S(1)} fusion(f32[2,512,2,512]{3,1,2,0:T(8,128)} %fusion.15, f32[2,512,2,512]{3,1,2,0:T(8,128)S(1)} %fusion.17, f32[2,512,2,512]{3,1,2,0:T(8,128)S(1)} %fusion.3, f32[2,512,2,512]{3,1,2,0:T(8,128)S(1)} %fusion.5, f32[2,512,512]{1,2,0:T(8,128)} %fusion.2, f32[2,512,2048]{1,2,0:T(8,128)S(1)} %bitcast.121, ...), kind=kOutput, calls=%fused_computation.6 | convolution fusion | flops 3225419776 | bytes 25165828 | tf_op jit(solution)/shard_map/aik,bkj->abij/dot_general | solution.py:65
  193.0 1.8 fusion.23
  194.8 1.8 fusion.27
  196.6 0.2 fusion.32
  196.8 2.3 %collective-permute-start.7 = (f32[2,128,512]{1,2,0:T(8,128)S(1)}, f32[2,128,512]{1,2,0:T(8,128)S(1)}, u32[]{:S(2)}, u32[]{:S(2)}) collective-permute-start(f32[2,128,512]{1,2,0:T(8,128)S(1)} %get-tuple-element.14), channel_id=1, source_target_pairs={{0,1},{1,0},{2,3},{3,2},{4,5},{5,4},{6,7},{7,6},{8,9},{9,8},{10,11... | collective-permute-start | bytes 1572872 | tf_op jit(solution)/shard_map/ppermute | solution.py:95
  199.1 0.7 collective-permute-start.8
  199.8 1.0 collective-permute-start.9
  200.8 0.0 collective-permute-done.7
  200.8 11.7 %collective-permute-done.8 = f32[2,128,512]{1,2,0:T(8,128)S(1)} collective-permute-done((f32[2,128,512]{1,2,0:T(8,128)S(1)}, f32[2,128,512]{1,2,0:T(8,128)S(1)}, u32[]{:S(2)}, u32[]{:S(2)}) %collective-permute-start.8) | collective-permute-done | bytes 524320 | tf_op jit(solution)/shard_map/ppermute | solution.py:95
  212.5 11.5 %collective-permute-done.9 = f32[2,128,512]{1,2,0:T(8,128)S(1)} collective-permute-done((f32[2,128,512]{1,2,0:T(8,128)S(1)}, f32[2,128,512]{1,2,0:T(8,128)S(1)}, u32[]{:S(2)}, u32[]{:S(2)}) %collective-permute-start.9) | collective-permute-done | bytes 524320 | tf_op jit(solution)/shard_map/ppermute | solution.py:95
  224.0 0.2 pad_maximum_fusion.2
  224.1 0.2 constant_dynamic-slice_fusion.3
  224.3 0.2 copy.53
  224.5 0.2 copy.54
  224.7 0.2 copy.55
  224.9 0.2 copy.56
  225.1 1.5 maximum_bitcast_fusion
  (2 shorter events, 0.0 us)
Async XLA Ops:
  49.9 45.6 %collective-permute-start.1 = (f32[2,128,2048]{1,2,0:T(8,128)S(1)}, f32[2,128,2048]{1,2,0:T(8,128)}, u32[]{:S(2)}, u32[]{:S(2)}) collective-permute-start(f32[2,128,2048]{1,2,0:T(8,128)S(1)} %bitcast.122), channel_id=1, source_target_pairs={{0,2},{1,3},{2,0},{3,1},{4,6},{5,7},{6,4},{7,5},{8,10},{9,11},{10,... | collective-permute-start | bytes 6291464 | tf_op jit(solution)/shard_map/ppermute | solution.py:52
  50.7 47.4 %collective-permute-start = (f32[2,128,2048]{1,2,0:T(8,128)S(1)}, f32[2,128,2048]{1,2,0:T(8,128)}, u32[]{:S(2)}, u32[]{:S(2)}) collective-permute-start(f32[2,128,2048]{1,2,0:T(8,128)S(1)} %bitcast.123), channel_id=1, source_target_pairs={{0,1},{1,0},{2,3},{3,2},{4,5},{5,4},{6,7},{7,6},{8,9},{9,8},{10,11... | collective-permute-start | bytes 6291464 | tf_op jit(solution)/shard_map/ppermute | solution.py:51
  95.5 6.7 %collective-permute-start.2 = (f32[2,128,2048]{1,2,0:T(8,128)}, f32[2,128,2048]{1,2,0:T(8,128)}, u32[]{:S(2)}, u32[]{:S(2)}) collective-permute-start(f32[2,128,2048]{1,2,0:T(8,128)} %collective-permute-done.1), channel_id=1, source_target_pairs={{0,1},{1,0},{2,3},{3,2},{4,5},{5,4},{6,7},{7,6},{8,9},{9,8},{10,11... | collective-permute-start | bytes 6291464 | tf_op jit(solution)/shard_map/ppermute | solution.py:53
  98.1 9.7 %copy-start = (f32[1,2]{1,0:T(1,128)S(1)}, f32[1,2]{1,0:T(1,128)}, u32[]{:S(2)}) copy-start(f32[1,2]{1,0:T(1,128)} %param.3) | copy-start | bytes 28
  105.1 48.5 %collective-permute-start.3 = (f32[2,512,512]{1,2,0:T(8,128)}, f32[2,512,512]{1,2,0:T(8,128)}, u32[]{:S(2)}, u32[]{:S(2)}) collective-permute-start(f32[2,512,512]{1,2,0:T(8,128)} %fusion.2), channel_id=1, source_target_pairs={{0,4},{1,5},{2,6},{3,7},{4,8},{5,9},{6,10},{7,11},{8,12},{9,13},{1... | collective-permute-start | bytes 6291464 | tf_op jit(solution)/shard_map/ppermute | solution.py:72
  106.4 49.8 %collective-permute-start.4 = (f32[2,512,512]{1,2,0:T(8,128)}, f32[2,512,512]{1,2,0:T(8,128)}, u32[]{:S(2)}, u32[]{:S(2)}) collective-permute-start(f32[2,512,512]{1,2,0:T(8,128)} %fusion.2), channel_id=1, source_target_pairs={{0,12},{1,13},{2,14},{3,15},{4,0},{5,1},{6,2},{7,3},{8,4},{9,5},{1... | collective-permute-start | bytes 6291464 | tf_op jit(solution)/shard_map/ppermute | solution.py:73
  154.8 24.8 %collective-permute-start.5 = (f32[2,256,512]{1,2,0:T(8,128)S(1)}, f32[2,256,512]{1,2,0:T(8,128)S(1)}, u32[]{:S(2)}, u32[]{:S(2)}) collective-permute-start(f32[2,256,512]{1,2,0:T(8,128)S(1)} %slice.48), channel_id=1, source_target_pairs={{0,4},{1,5},{2,6},{3,7},{4,8},{5,9},{6,10},{7,11},{8,12},{9,13},{1... | collective-permute-start | bytes 3145736 | tf_op jit(solution)/shard_map/ppermute | solution.py:75
  157.5 24.0 %collective-permute-start.6 = (f32[2,256,512]{1,2,0:T(8,128)S(1)}, f32[2,256,512]{1,2,0:T(8,128)S(1)}, u32[]{:S(2)}, u32[]{:S(2)}) collective-permute-start(f32[2,256,512]{1,2,0:T(8,128)S(1)} %slice.49), channel_id=1, source_target_pairs={{0,12},{1,13},{2,14},{3,15},{4,0},{5,1},{6,2},{7,3},{8,4},{9,5},{1... | collective-permute-start | bytes 3145736 | tf_op jit(solution)/shard_map/ppermute | solution.py:76
  196.8 4.0 %collective-permute-start.7 = (f32[2,128,512]{1,2,0:T(8,128)S(1)}, f32[2,128,512]{1,2,0:T(8,128)S(1)}, u32[]{:S(2)}, u32[]{:S(2)}) collective-permute-start(f32[2,128,512]{1,2,0:T(8,128)S(1)} %get-tuple-element.14), channel_id=1, source_target_pairs={{0,1},{1,0},{2,3},{3,2},{4,5},{5,4},{6,7},{7,6},{8,9},{9,8},{10,11... | collective-permute-start | bytes 1572872 | tf_op jit(solution)/shard_map/ppermute | solution.py:95
  199.1 13.4 %collective-permute-start.8 = (f32[2,128,512]{1,2,0:T(8,128)S(1)}, f32[2,128,512]{1,2,0:T(8,128)S(1)}, u32[]{:S(2)}, u32[]{:S(2)}) collective-permute-start(f32[2,128,512]{1,2,0:T(8,128)S(1)} %get-tuple-element.16), channel_id=1, source_target_pairs={{0,2},{1,3},{2,0},{3,1},{4,6},{5,7},{6,4},{7,5},{8,10},{9,11},{10,... | collective-permute-start | bytes 1572872 | tf_op jit(solution)/shard_map/ppermute | solution.py:95
  199.8 24.1 %collective-permute-start.9 = (f32[2,128,512]{1,2,0:T(8,128)S(1)}, f32[2,128,512]{1,2,0:T(8,128)S(1)}, u32[]{:S(2)}, u32[]{:S(2)}) collective-permute-start(f32[2,128,512]{1,2,0:T(8,128)S(1)} %get-tuple-element.15), channel_id=1, source_target_pairs={{0,3},{1,2},{2,1},{3,0},{4,7},{5,6},{6,5},{7,4},{8,11},{9,10},{10,... | collective-permute-start | bytes 1572872 | tf_op jit(solution)/shard_map/ppermute | solution.py:95

commit v2 on v1

--- a/solution.py
+++ b/solution.py
@@ -48,12 +48,20 @@
     p = b % GROUP
     y = b // GROUP
 
+    def cols(x, i):
+        return lax.dynamic_slice_in_dim(x, i * cw, cw, axis=2)
+
     q1 = lax.ppermute(own, "blk", xor_perm(nblk, 1))
-    q2 = lax.ppermute(own, "blk", xor_perm(nblk, 2))
+    c2 = lax.ppermute(cols(own, p ^ 2), "blk", xor_perm(nblk, 2))
+    c3 = lax.ppermute(cols(own, p ^ 3), "blk", xor_perm(nblk, 3))
+    rest = jnp.concatenate([cols(own, p ^ 2 ^ m) for m in range(1, GROUP)], axis=2)
+    rest = lax.ppermute(rest, "blk", xor_perm(nblk, 2))
+    q2 = jnp.zeros_like(own)
+    q2 = lax.dynamic_update_slice_in_dim(q2, c2, p * cw, axis=2)
+    for m in range(1, GROUP):
+        q2 = lax.dynamic_update_slice_in_dim(q2, rest[:, :, (m - 1) * cw:m * cw], (p ^ m) * cw, axis=2)
     q3 = lax.ppermute(q2, "blk", xor_perm(nblk, 1))
     rows = jnp.concatenate([own, q1, q2, q3], axis=1)
-
-    piece = lax.dynamic_slice_in_dim(rows, p * cw, cw, axis=2)
 
     l5 = rows.reshape(2, gw, ny, GROUP, rb)
     lx = jnp.concatenate(
@@ -67,19 +75,22 @@
             precision=lax.Precision.HIGH, preferred_element_type=jnp.float32,
         )
 
+    part_a = jnp.concatenate([cols(own, p), cols(q1, p)], axis=1)
+    part_b = jnp.concatenate([c2, c3], axis=1)
     up = shift_perm(nblk, GROUP)
     dn = shift_perm(nblk, -GROUP)
-    r_up = lax.ppermute(piece, "blk", up)
-    r_dn = lax.ppermute(piece, "blk", dn)
-    half = gw // 2
-    f_up = lax.ppermute(r_up[:, :half], "blk", up)
-    f_dn = lax.ppermute(r_dn[:, half:], "blk", dn)
+    ua = lax.ppermute(part_a, "blk", up)
+    da = lax.ppermute(part_a, "blk", dn)
+    ub = lax.ppermute(part_b, "blk", up)
+    db = lax.ppermute(part_b, "blk", dn)
+    fa = lax.ppermute(ua, "blk", up)
+    fb = lax.ppermute(db, "blk", dn)
 
-    t = contrib(y, piece, 0, GROUP)
-    t = t + contrib((y - 1) % ny, r_up, 0, GROUP)
-    t = t + contrib((y + 1) % ny, r_dn, 0, GROUP)
-    t = t + contrib((y + 2) % ny, f_up, 0, GROUP // 2)
-    t = t + contrib((y + 2) % ny, f_dn, GROUP // 2, GROUP)
+    half = GROUP // 2
+    t = contrib(y, part_a, 0, half) + contrib(y, part_b, half, GROUP)
+    t = t + contrib((y - 1) % ny, ua, 0, half) + contrib((y + 1) % ny, da, 0, half)
+    t = t + contrib((y - 1) % ny, ub, half, GROUP) + contrib((y + 1) % ny, db, half, GROUP)
+    t = t + contrib((y + 2) % ny, fa, 0, half) + contrib((y + 2) % ny, fb, half, GROUP)
 
     prod_re = t[0, 0] - t[1, 1]
     prod_im = t[0, 1] + t[1, 0]

time: 227 us -> 259 us (1.14)
  blocking collectives: 35.7 us -> 0 us
  waiting for transfers between devices: 120 us -> 147 us
  matrix products: 33.6 us -> 53.2 us
  local copies, waits for them, and re-layouts: 9.57 us -> 23 us
  starting transfers between devices: 15.2 us -> 22.7 us
    all_to_all x1 -> x0, blocking collectives: 35.7 us -> none  [on_device(): lax.all_to_all(projected, 'freq', split_axis=1, concat_axis=3, tiled=True)]
    all_to_all x0 -> x1, waiting for transfers between devices: none -> 28.7 us  [on_device(): lax.all_to_all(projected, 'freq', split_axis=1, concat_axis=3, tiled=True)]
    dot_general x5 -> x8, matrix products: 23.4 us -> 43 us  [contrib(): jnp.einsum('aik,bkj->abij', lg, pc, precision=lax.Precision.HIGH, preferr...]
    all_to_all x0 -> x1, starting transfers between devices: none -> 8.15 us  [on_device(): lax.all_to_all(projected, 'freq', split_axis=1, concat_axis=3, tiled=True)]
    dynamic_update_slice x0 -> x3, local copies, waits for them, and re-layouts: none -> 5.61 us  [on_device(): lax.dynamic_update_slice_in_dim(q2, rest[:, :, (m - 1) * cw:m * cw], (p ^...]
    ppermute x1, waiting for transfers between devices: 4.12 us -> 0.01 us  [on_device(): q3 = lax.ppermute(q2, 'blk', xor_perm(nblk, 1))]
    dynamic_slice x5, local copies, waits for them, and re-layouts: 0.94 us -> 4.01 us  [on_device(): lax.dynamic_index_in_dim(stacked, p ^ i, 0, keepdims=False)]
    concatenate x2 -> x1, other arithmetic: 5.96 us -> 3.15 us  [on_device(): rows = jnp.concatenate([own, q1, q2, q3], axis=1)]
  transfers between devices with their start and end apart: 10 -> 15, of which waited for: 6 -> 9; matrix products, arithmetic and copies ran while one was open for 9% -> 19% of each run, Pallas kernels for 0% -> 0%
where the time goes in v2:
time: 259 us; the launch traced here: 258 us
  waiting for transfers between devices  147 us (57%)
  matrix products  53.2 us (21%)
  local copies, waits for them, and re-layouts  23 us (9%)
  starting transfers between devices  22.7 us (9%)
  other arithmetic  12.3 us (5%)
    ppermute x1, waiting for transfers between devices, on_device(): c2 = lax.ppermute(cols(own, p ^ 2), 'blk', xor_perm(nblk, 2))  43.9 us
    dot_general x8, matrix products, contrib(): jnp.einsum('aik,bkj->abij', lg, pc, precision=lax.Precision.HIGH, preferr...  43 us
    all_to_all x1, waiting for transfers between devices, on_device(): lax.all_to_all(projected, 'freq', split_axis=1, concat_axis=3, tiled=True)  28.7 us
    ppermute x3, waiting for transfers between devices, on_device(): lax.ppermute(blk_out[:, m * rb:(m + 1) * rb], 'blk', xor_perm(nblk, m))  23.1 us
    ppermute x1, waiting for transfers between devices, on_device(): db = lax.ppermute(part_b, 'blk', dn)  20 us
    ppermute x1, waiting for transfers between devices, on_device(): da = lax.ppermute(part_a, 'blk', dn)  16.2 us
    ppermute x1, waiting for transfers between devices, on_device(): c3 = lax.ppermute(cols(own, p ^ 3), 'blk', xor_perm(nblk, 3))  12.9 us
    dot_general x1, matrix products, on_device(): jnp.einsum('srt,tc->csr', traces, table, preferred_element_type=jnp.float32)  10.2 us
  transfers between devices with their start and end apart: 15, of which 9 were waited for; matrix products, arithmetic and copies ran while one was open for 19% of the time, Pallas kernels for 0%

profile of v2, /device:TPU:1, one launch (start us, length us, event | category | flops | bytes accessed | tf_op | source)
XLA Modules:
  0.0 258.0 jit_solution(12633397025815402862)
XLA Ops:
  0.1 10.2 %convolution_bitcast_fusion = f32[2,8,128,256]{3,1,0,2:T(8,128)S(1)} fusion(bf16[128,256,256]{2,1,0:T(8,128)(2,1)} %param.2, bf16[256,8]{0,1:T(8,128)(2,1)S(1)} %get-tuple-element.26, bf16[256,8]{0,1:T(8,128)(2,1)S(1)} %get-tuple-element.25), kind=kOutput, calls=%fused_computation.11 | convolution fusion | flops 268451840 | bytes 18882560 | tf_op jit(solution)/shard_map/srt,tc->csr/dot_general | solution.py:38
  10.4 2.4 copy.50
  12.8 8.2 %all-to-all-start = ((f32[2,8,128,256]{3,0,2,1:T(2,128)}), f32[2,8,128,256]{3,0,2,1:T(2,128)}, u32[]{:S(2)}, u32[]{:S(2)}) async-start(f32[2,8,128,256]{3,0,2,1:T(2,128)} %copy.50), calls=%async_computation | async-start | bytes 4194304 | tf_op jit(solution)/shard_map/all_to_all | solution.py:40
  20.9 28.7 %all-to-all-done = f32[2,8,128,256]{3,0,2,1:T(2,128)} async-done(((f32[2,8,128,256]{3,0,2,1:T(2,128)}), f32[2,8,128,256]{3,0,2,1:T(2,128)}, u32[]{:S(2)}, u32[]{:S(2)}) %all-to-all-start) | async-done | bytes 2097184 | tf_op jit(solution)/shard_map/all_to_all | solution.py:40
  49.6 2.7 %copy.51 = f32[2,8,128,256]{2,3,1,0:T(8,128)S(1)} copy(f32[2,8,128,256]{3,0,2,1:T(2,128)} %all-to-all-done) | data formatting | bytes 4194304 | tf_op jit(solution)/shard_map/all_to_all | solution.py:40
  52.4 1.0 constant_dynamic-slice_fusion.4
  53.4 1.2 pad_maximum_fusion.3
  54.7 0.7 collective-permute-start.2
  55.4 0.7 collective-permute-start.1
  56.1 1.4 collective-permute-start
  57.5 43.9 %collective-permute-done.1 = f32[2,128,512]{1,2,0:T(8,128)} collective-permute-done((f32[2,128,512]{1,2,0:T(8,128)}, f32[2,128,512]{1,2,0:T(8,128)}, u32[]{:S(2)}, u32[]{:S(2)}) %collective-permute-start.1) | collective-permute-done | bytes 524320 | tf_op jit(solution)/shard_map/ppermute | solution.py:55
  101.4 1.5 broadcast_in_dim.8
  102.8 2.1 constant_dynamic-update-slice_fusion.2
  104.9 1.9 slice_dynamic-update-slice_fusion.2
  106.8 1.9 slice_dynamic-update-slice_fusion.1
  108.6 1.9 slice_dynamic-update-slice_fusion
  110.5 1.6 collective-permute-start.3
  112.8 12.9 %collective-permute-done.4 = f32[2,128,512]{1,2,0:T(8,128)S(1)} collective-permute-done((f32[2,128,512]{1,2,0:T(8,128)S(1)}, f32[2,128,512]{1,2,0:T(8,128)S(1)}, u32[]{:S(2)}, u32[]{:S(2)}) %collective-permute-start.4) | collective-permute-done | bytes 524320 | tf_op jit(solution)/shard_map/ppermute | solution.py:56
  125.7 0.9 constant_dynamic-update-slice_fusion.1
  126.6 2.7 %collective-permute-start.8 = (f32[2,256,512]{1,2,0:T(8,128)}, f32[2,256,512]{1,2,0:T(8,128)}, u32[]{:S(2)}, u32[]{:S(2)}) collective-permute-start(f32[2,256,512]{1,2,0:T(8,128)} %constant_dynamic-update-slice_fusion.1), channel_id=1, source_target_pairs={{0,12},{1,13},{2,14},{3,15},{4,0},{5,1},{6,2},{7,3},{8,4},{9,5},{1... | collective-permute-start | bytes 3145736 | tf_op jit(solution)/shard_map/ppermute | solution.py:85
  129.4 1.1 constant_dynamic-slice_fusion.13
  130.4 1.1 pad_maximum_fusion.4
  132.1 20.0 %collective-permute-done.8 = f32[2,256,512]{1,2,0:T(8,128)} collective-permute-done((f32[2,256,512]{1,2,0:T(8,128)}, f32[2,256,512]{1,2,0:T(8,128)}, u32[]{:S(2)}, u32[]{:S(2)}) %collective-permute-start.8) | collective-permute-done | bytes 1048608 | tf_op jit(solution)/shard_map/ppermute | solution.py:85
  152.2 3.4 %collective-permute-start.10 = (f32[2,256,512]{1,2,0:T(8,128)}, f32[2,256,512]{1,2,0:T(8,128)}, u32[]{:S(2)}, u32[]{:S(2)}) collective-permute-start(f32[2,256,512]{1,2,0:T(8,128)} %collective-permute-done.8), channel_id=1, source_target_pairs={{0,12},{1,13},{2,14},{3,15},{4,0},{5,1},{6,2},{7,3},{8,4},{9,5},{1... | collective-permute-start | bytes 3145736 | tf_op jit(solution)/shard_map/ppermute | solution.py:87
  155.6 1.8 collective-permute-done.5
  157.5 3.2 %pad_maximum_fusion = f32[2,512,4,4,128]{1,4,3,2,0:T(8,128)S(1)} fusion(f32[2,128,4,4,128]{1,4,3,2,0:T(8,128)} %bitcast.13, f32[2,128,4,4,128]{1,4,3,2,0:T(8,128)} %bitcast.12, f32[2,128,4,4,128]{1,4,3,2,0:T(8,128)} %bitcast.11, f32[2,128,4,4,128]{1,4,3,2,0:T(8,128)S(1)} %bitcast.156), kind=kLoop, calls=%fused_computation | loop fusion | flops 6291456 | bytes 16777216 | tf_op jit(solution)/shard_map/concatenate | solution.py:64
  160.6 1.0 constant_dynamic-slice_fusion.8
  161.7 1.4 pad_maximum_fusion.1
  163.1 1.9 fusion.17
  165.0 5.0 %fusion.15 = f32[2,512,2,512]{3,1,2,0:T(8,128)} fusion(f32[2,256,512]{1,2,0:T(8,128)} %constant_dynamic-update-slice_fusion.1, f32[2,512,2048]{1,2,0:T(8,128)S(1)} %bitcast.147, s32[]{:T(128)S(6)} %select_n.118), kind=kOutput, calls=%fused_computation.30 | convolution fusion | flops 1610612736 | bytes 6291460 | tf_op jit(solution)/shard_map/aik,bkj->abij/dot_general | solution.py:73
  170.0 5.0 %fusion.7 = f32[2,512,2,512]{3,1,2,0:T(8,128)} fusion(f32[2,256,512]{1,2,0:T(8,128)} %collective-permute-done.8, f32[2,512,2048]{1,2,0:T(8,128)S(1)} %bitcast.148, s32[]{:T(128)S(6)} %select_n.124), kind=kOutput, calls=%fused_computation.22 | convolution fusion | flops 1610612736 | bytes 6291460 | tf_op jit(solution)/shard_map/aik,bkj->abij/dot_general | solution.py:73
  175.0 5.1 %fusion.13 = f32[2,512,2,512]{3,1,2,0:T(8,128)} fusion(f32[2,256,512]{1,2,0:T(8,128)} %collective-permute-done.5, f32[2,512,2048]{1,2,0:T(8,128)S(1)} %bitcast.149, s32[]{:T(128)S(6)} %select_n.120), kind=kOutput, calls=%fused_computation.28 | convolution fusion | flops 1610612736 | bytes 6291460 | tf_op jit(solution)/shard_map/aik,bkj->abij/dot_general | solution.py:73
  180.1 3.8 %fusion.9 = f32[2,512,2,512]{3,1,2,0:T(8,128)} fusion(f32[2,256,512]{1,2,0:T(8,128)S(1)} %collective-permute-done.7, f32[2,512,2048]{1,2,0:T(8,128)S(1)} %bitcast.150, s32[]{:T(128)S(6)} %select_n.123), kind=kOutput, calls=%fused_computation.24 | convolution fusion | flops 1610612736 | bytes 6291460 | tf_op jit(solution)/shard_map/aik,bkj->abij/dot_general | solution.py:73
  183.8 16.2 %collective-permute-done.6 = f32[2,256,512]{1,2,0:T(8,128)} collective-permute-done((f32[2,256,512]{1,2,0:T(8,128)}, f32[2,256,512]{1,2,0:T(8,128)}, u32[]{:S(2)}, u32[]{:S(2)}) %collective-permute-start.6) | collective-permute-done | bytes 1048608 | tf_op jit(solution)/shard_map/ppermute | solution.py:83
  200.1 5.0 %fusion.11 = f32[2,512,2,512]{3,1,2,0:T(8,128)} fusion(f32[2,256,512]{1,2,0:T(8,128)} %collective-permute-done.6, f32[2,512,2048]{1,2,0:T(8,128)S(1)} %bitcast.151, s32[]{:T(128)S(6)} %select_n.122), kind=kOutput, calls=%fused_computation.26 | convolution fusion | flops 1610612736 | bytes 6291460 | tf_op jit(solution)/shard_map/aik,bkj->abij/dot_general | solution.py:73
  205.0 5.3 %fusion.5 = f32[2,512,2,512]{3,1,2,0:T(8,128)} fusion(f32[2,256,512]{1,2,0:T(8,128)} %collective-permute-done.9, f32[2,512,2048]{1,2,0:T(8,128)S(1)} %bitcast.152, s32[]{:T(128)S(6)} %select_n.126), kind=kOutput, calls=%fused_computation.20 | convolution fusion | flops 1610612736 | bytes 6291460 | tf_op jit(solution)/shard_map/aik,bkj->abij/dot_general | solution.py:73
  210.3 12.0 %add_bitcast_fusion = f32[2,2,512,512]{2,3,0,1:T(8,128)S(1)} fusion(f32[2,512,2,512]{3,1,2,0:T(8,128)} %fusion.5, f32[2,512,2,512]{3,1,2,0:T(8,128)} %fusion.7, f32[2,512,2,512]{3,1,2,0:T(8,128)} %fusion.9, f32[2,512,2,512]{3,1,2,0:T(8,128)} %fusion.11, f32[2,512,2,512]{3,1,2,0:T(8,128)} %fusion.13, f32[2,512,2,512]{3,1,2,0:T(8,128)S(1)} %fusion.17, ...), kind=kOutput, calls=%fused_computation.2 | convolution fusion | flops 1617952768 | bytes 35651588 | tf_op jit(solution)/shard_map/aik,bkj->abij/dot_general | solution.py:73
  222.3 1.8 fusion.29
  224.1 1.8 fusion.33
  226.0 1.8 collective-permute-start.11
  227.8 0.7 collective-permute-start.13
  228.5 0.7 collective-permute-start.12
  229.3 12.7 %collective-permute-done.13 = f32[2,128,512]{1,2,0:T(8,128)S(1)} collective-permute-done((f32[2,128,512]{1,2,0:T(8,128)S(1)}, f32[2,128,512]{1,2,0:T(8,128)S(1)}, u32[]{:S(2)}, u32[]{:S(2)}) %collective-permute-start.13) | collective-permute-done | bytes 524320 | tf_op jit(solution)/shard_map/ppermute | solution.py:106
  242.0 10.3 %collective-permute-done.12 = f32[2,128,512]{1,2,0:T(8,128)S(1)} collective-permute-done((f32[2,128,512]{1,2,0:T(8,128)S(1)}, f32[2,128,512]{1,2,0:T(8,128)S(1)}, u32[]{:S(2)}, u32[]{:S(2)}) %collective-permute-start.12) | collective-permute-done | bytes 524320 | tf_op jit(solution)/shard_map/ppermute | solution.py:106
  252.5 1.1 constant_dynamic-slice_fusion.3
  253.6 1.2 copy.59
  254.9 1.2 copy.62
  256.5 1.5 maximum_bitcast_fusion
  (21 shorter events, 2.2 us)
Async XLA Ops:
  12.8 36.9 %all-to-all-start = ((f32[2,8,128,256]{3,0,2,1:T(2,128)}), f32[2,8,128,256]{3,0,2,1:T(2,128)}, u32[]{:S(2)}, u32[]{:S(2)}) async-start(f32[2,8,128,256]{3,0,2,1:T(2,128)} %copy.50), calls=%async_computation | async-start | bytes 4194304 | tf_op jit(solution)/shard_map/all_to_all | solution.py:40
  54.7 50.2 %collective-permute-start.2 = (f32[2,128,1536]{1,2,0:T(8,128)}, f32[2,128,1536]{1,2,0:T(8,128)}, u32[]{:S(2)}, u32[]{:S(2)}) collective-permute-start(f32[2,128,1536]{1,2,0:T(8,128)} %pad_maximum_fusion.3), channel_id=1, source_target_pairs={{0,2},{1,3},{2,0},{3,1},{4,6},{5,7},{6,4},{7,5},{8,10},{9,11},{10,... | collective-permute-start | bytes 4718600 | tf_op jit(solution)/shard_map/ppermute | solution.py:58
  55.4 46.0 %collective-permute-start.1 = (f32[2,128,512]{1,2,0:T(8,128)}, f32[2,128,512]{1,2,0:T(8,128)}, u32[]{:S(2)}, u32[]{:S(2)}) collective-permute-start(f32[2,128,512]{1,2,0:T(8,128)} %get-tuple-element.21), channel_id=1, source_target_pairs={{0,2},{1,3},{2,0},{3,1},{4,6},{5,7},{6,4},{7,5},{8,10},{9,11},{10,... | collective-permute-start | bytes 1572872 | tf_op jit(solution)/shard_map/ppermute | solution.py:55
  56.1 73.2 %collective-permute-start = (f32[2,128,2048]{1,2,0:T(8,128)S(1)}, f32[2,128,2048]{1,2,0:T(8,128)}, u32[]{:S(2)}, u32[]{:S(2)}) collective-permute-start(f32[2,128,2048]{1,2,0:T(8,128)S(1)} %bitcast.155), channel_id=1, source_target_pairs={{0,1},{1,0},{2,3},{3,2},{4,5},{5,4},{6,7},{7,6},{8,9},{9,8},{10,11... | collective-permute-start | bytes 6291464 | tf_op jit(solution)/shard_map/ppermute | solution.py:54
  110.5 46.9 %collective-permute-start.3 = (f32[2,128,2048]{1,2,0:T(8,128)}, f32[2,128,2048]{1,2,0:T(8,128)}, u32[]{:S(2)}, u32[]{:S(2)}) collective-permute-start(f32[2,128,2048]{1,2,0:T(8,128)} %slice_dynamic-update-slice_fusion), channel_id=1, source_target_pairs={{0,1},{1,0},{2,3},{3,2},{4,5},{5,4},{6,7},{7,6},{8,9},{9,8},{10,11... | collective-permute-start | bytes 6291464 | tf_op jit(solution)/shard_map/ppermute | solution.py:63
  112.2 13.5 %collective-permute-start.4 = (f32[2,128,512]{1,2,0:T(8,128)S(1)}, f32[2,128,512]{1,2,0:T(8,128)S(1)}, u32[]{:S(2)}, u32[]{:S(2)}) collective-permute-start(f32[2,128,512]{1,2,0:T(8,128)S(1)} %get-tuple-element.17), channel_id=1, source_target_pairs={{0,3},{1,2},{2,1},{3,0},{4,7},{5,6},{6,5},{7,4},{8,11},{9,10},{10,... | collective-permute-start | bytes 1572872 | tf_op jit(solution)/shard_map/ppermute | solution.py:56
  125.7 5.8 %copy-start = (f32[1,2]{1,0:T(1,128)S(1)}, f32[1,2]{1,0:T(1,128)}, u32[]{:S(2)}) copy-start(f32[1,2]{1,0:T(1,128)} %param.3) | copy-start | bytes 28
  126.6 25.6 %collective-permute-start.8 = (f32[2,256,512]{1,2,0:T(8,128)}, f32[2,256,512]{1,2,0:T(8,128)}, u32[]{:S(2)}, u32[]{:S(2)}) collective-permute-start(f32[2,256,512]{1,2,0:T(8,128)} %constant_dynamic-update-slice_fusion.1), channel_id=1, source_target_pairs={{0,12},{1,13},{2,14},{3,15},{4,0},{5,1},{6,2},{7,3},{8,4},{9,5},{1... | collective-permute-start | bytes 3145736 | tf_op jit(solution)/shard_map/ppermute | solution.py:85
  131.5 26.0 %collective-permute-start.5 = (f32[2,256,512]{1,2,0:T(8,128)}, f32[2,256,512]{1,2,0:T(8,128)}, u32[]{:S(2)}, u32[]{:S(2)}) collective-permute-start(f32[2,256,512]{1,2,0:T(8,128)} %pad_maximum_fusion.4), channel_id=1, source_target_pairs={{0,4},{1,5},{2,6},{3,7},{4,8},{5,9},{6,10},{7,11},{8,12},{9,13},{1... | collective-permute-start | bytes 3145736 | tf_op jit(solution)/shard_map/ppermute | solution.py:82
  132.1 47.9 %collective-permute-start.7 = (f32[2,256,512]{1,2,0:T(8,128)}, f32[2,256,512]{1,2,0:T(8,128)S(1)}, u32[]{:S(2)}, u32[]{:S(2)}) collective-permute-start(f32[2,256,512]{1,2,0:T(8,128)} %constant_dynamic-update-slice_fusion.1), channel_id=1, source_target_pairs={{0,4},{1,5},{2,6},{3,7},{4,8},{5,9},{6,10},{7,11},{8,12},{9,13},{1... | collective-permute-start | bytes 3145736 | tf_op jit(solution)/shard_map/ppermute | solution.py:84
  152.2 58.1 %collective-permute-start.10 = (f32[2,256,512]{1,2,0:T(8,128)}, f32[2,256,512]{1,2,0:T(8,128)}, u32[]{:S(2)}, u32[]{:S(2)}) collective-permute-start(f32[2,256,512]{1,2,0:T(8,128)} %collective-permute-done.8), channel_id=1, source_target_pairs={{0,12},{1,13},{2,14},{3,15},{4,0},{5,1},{6,2},{7,3},{8,4},{9,5},{1... | collective-permute-start | bytes 3145736 | tf_op jit(solution)/shard_map/ppermute | solution.py:87
  155.6 44.4 %collective-permute-start.6 = (f32[2,256,512]{1,2,0:T(8,128)}, f32[2,256,512]{1,2,0:T(8,128)}, u32[]{:S(2)}, u32[]{:S(2)}) collective-permute-start(f32[2,256,512]{1,2,0:T(8,128)} %pad_maximum_fusion.4), channel_id=1, source_target_pairs={{0,12},{1,13},{2,14},{3,15},{4,0},{5,1},{6,2},{7,3},{8,4},{9,5},{1... | collective-permute-start | bytes 3145736 | tf_op jit(solution)/shard_map/ppermute | solution.py:83
  157.5 47.6 %collective-permute-start.9 = (f32[2,256,512]{1,2,0:T(8,128)}, f32[2,256,512]{1,2,0:T(8,128)}, u32[]{:S(2)}, u32[]{:S(2)}) collective-permute-start(f32[2,256,512]{1,2,0:T(8,128)} %collective-permute-done.5), channel_id=1, source_target_pairs={{0,4},{1,5},{2,6},{3,7},{4,8},{5,9},{6,10},{7,11},{8,12},{9,13},{1... | collective-permute-start | bytes 3145736 | tf_op jit(solution)/shard_map/ppermute | solution.py:86
  226.0 3.3 %collective-permute-start.11 = (f32[2,128,512]{1,2,0:T(8,128)S(1)}, f32[2,128,512]{1,2,0:T(8,128)S(1)}, u32[]{:S(2)}, u32[]{:S(2)}) collective-permute-start(f32[2,128,512]{1,2,0:T(8,128)S(1)} %get-tuple-element.14), channel_id=1, source_target_pairs={{0,1},{1,0},{2,3},{3,2},{4,5},{5,4},{6,7},{7,6},{8,9},{9,8},{10,11... | collective-permute-start | bytes 1572872 | tf_op jit(solution)/shard_map/ppermute | solution.py:106
  227.8 14.2 %collective-permute-start.13 = (f32[2,128,512]{1,2,0:T(8,128)S(1)}, f32[2,128,512]{1,2,0:T(8,128)S(1)}, u32[]{:S(2)}, u32[]{:S(2)}) collective-permute-start(f32[2,128,512]{1,2,0:T(8,128)S(1)} %get-tuple-element.15), channel_id=1, source_target_pairs={{0,3},{1,2},{2,1},{3,0},{4,7},{5,6},{6,5},{7,4},{8,11},{9,10},{10,... | collective-permute-start | bytes 1572872 | tf_op jit(solution)/shard_map/ppermute | solution.py:106
  228.5 23.8 %collective-permute-start.12 = (f32[2,128,512]{1,2,0:T(8,128)S(1)}, f32[2,128,512]{1,2,0:T(8,128)S(1)}, u32[]{:S(2)}, u32[]{:S(2)}) collective-permute-start(f32[2,128,512]{1,2,0:T(8,128)S(1)} %get-tuple-element.16), channel_id=1, source_target_pairs={{0,2},{1,3},{2,0},{3,1},{4,6},{5,7},{6,4},{7,5},{8,10},{9,11},{10,... | collective-permute-start | bytes 1572872 | tf_op jit(solution)/shard_map/ppermute | solution.py:106

commit v3 on v2

--- a/solution.py
+++ b/solution.py
@@ -4,6 +4,7 @@
 import jax.numpy as jnp
 from jax import lax
 from jax.sharding import PartitionSpec as P
+
 
 BIN0 = 4
 BINSTEP = 3
@@ -26,6 +27,10 @@
 
 def shift_perm(n, s):
     return [(i, (i + s) % n) for i in range(n)]
+
+
+def send(x, perm):
+    return lax.ppermute(x, "blk", perm)
 
 
 def on_device(traces, signature):
@@ -51,16 +56,17 @@
     def cols(x, i):
         return lax.dynamic_slice_in_dim(x, i * cw, cw, axis=2)
 
-    q1 = lax.ppermute(own, "blk", xor_perm(nblk, 1))
-    c2 = lax.ppermute(cols(own, p ^ 2), "blk", xor_perm(nblk, 2))
-    c3 = lax.ppermute(cols(own, p ^ 3), "blk", xor_perm(nblk, 3))
+    q1 = send(own, xor_perm(nblk, 1))
+    c2 = send(cols(own, p ^ 2), xor_perm(nblk, 2))
+    c3 = send(cols(own, p ^ 3), xor_perm(nblk, 3))
     rest = jnp.concatenate([cols(own, p ^ 2 ^ m) for m in range(1, GROUP)], axis=2)
-    rest = lax.ppermute(rest, "blk", xor_perm(nblk, 2))
+    rest, _, _ = lax.optimization_barrier((rest, c2, c3))
+    rest = send(rest, xor_perm(nblk, 2))
     q2 = jnp.zeros_like(own)
     q2 = lax.dynamic_update_slice_in_dim(q2, c2, p * cw, axis=2)
     for m in range(1, GROUP):
         q2 = lax.dynamic_update_slice_in_dim(q2, rest[:, :, (m - 1) * cw:m * cw], (p ^ m) * cw, axis=2)
-    q3 = lax.ppermute(q2, "blk", xor_perm(nblk, 1))
+    q3 = send(q2, xor_perm(nblk, 1))
     rows = jnp.concatenate([own, q1, q2, q3], axis=1)
 
     l5 = rows.reshape(2, gw, ny, GROUP, rb)
@@ -79,12 +85,12 @@
     part_b = jnp.concatenate([c2, c3], axis=1)
     up = shift_perm(nblk, GROUP)
     dn = shift_perm(nblk, -GROUP)
-    ua = lax.ppermute(part_a, "blk", up)
-    da = lax.ppermute(part_a, "blk", dn)
-    ub = lax.ppermute(part_b, "blk", up)
-    db = lax.ppermute(part_b, "blk", dn)
-    fa = lax.ppermute(ua, "blk", up)
-    fb = lax.ppermute(db, "blk", dn)
+    ua = send(part_a, up)
+    da = send(part_a, dn)
+    ub = send(part_b, up)
+    db = send(part_b, dn)
+    fa = send(ua, up)
+    fb = send(db, dn)
 
     half = GROUP // 2
     t = contrib(y, part_a, 0, half) + contrib(y, part_b, half, GROUP)
@@ -103,7 +109,7 @@
 
     parts = [blk_out[:, :rb]]
     for m in range(1, GROUP):
-        parts.append(lax.ppermute(blk_out[:, m * rb:(m + 1) * rb], "blk", xor_perm(nblk, m)))
+        parts.append(send(blk_out[:, m * rb:(m + 1) * rb], xor_perm(nblk, m)))
     stacked = jnp.stack(parts, axis=0)
     ordered = [lax.dynamic_index_in_dim(stacked, p ^ i, 0, keepdims=False) for i in range(GROUP)]
     out = jnp.concatenate(ordered, axis=2)

time: 259 us -> 261 us (level)
  waiting for transfers between devices: 147 us -> 150 us
    ppermute x14, waiting for transfers between devices: 118 us -> 122 us  [send(): return lax.ppermute(x, 'blk', perm)]
  transfers between devices with their start and end apart: 15 -> 15, of which waited for: 9 -> 10; matrix products, arithmetic and copies ran while one was open for 19% -> 19% of each run, Pallas kernels for 0% -> 0%
where the time goes in v3:
time: 261 us; the launch traced here: 260 us
  waiting for transfers between devices  150 us (57%)
  matrix products  53.2 us (20%)
  local copies, waits for them, and re-layouts  21.9 us (8%)
  starting transfers between devices  21.9 us (8%)
  other arithmetic  12.4 us (5%)
    ppermute x14, waiting for transfers between devices, send(): return lax.ppermute(x, 'blk', perm)  122 us
    dot_general x8, matrix products, contrib(): jnp.einsum('aik,bkj->abij', lg, pc, precision=lax.Precision.HIGH, preferr...  43 us
    all_to_all x1, waiting for transfers between devices, on_device(): lax.all_to_all(projected, 'freq', split_axis=1, concat_axis=3, tiled=True)  28.7 us
    ppermute x14, starting transfers between devices, send(): return lax.ppermute(x, 'blk', perm)  13.7 us
    dot_general x1, matrix products, on_device(): jnp.einsum('srt,tc->csr', traces, table, preferred_element_type=jnp.float32)  10.2 us
    all_to_all x1, starting transfers between devices, on_device(): lax.all_to_all(projected, 'freq', split_axis=1, concat_axis=3, tiled=True)  8.15 us
    dynamic_update_slice x3, local copies, waits for them, and re-layouts, on_device(): lax.dynamic_update_slice_in_dim(q2, rest[:, :, (m - 1) * cw:m * cw], (p ^...  5.61 us
  transfers between devices with their start and end apart: 15, of which 10 were waited for; matrix products, arithmetic and copies ran while one was open for 19% of the time, Pallas kernels for 0%

profile of v3, /device:TPU:1, one launch (start us, length us, event | category | flops | bytes accessed | tf_op | source)
XLA Modules:
  0.0 259.8 jit_solution(12964207345551581365)
XLA Ops:
  0.1 10.2 %convolution_bitcast_fusion = f32[2,8,128,256]{3,1,0,2:T(8,128)S(1)} fusion(bf16[128,256,256]{2,1,0:T(8,128)(2,1)} %param.2, bf16[256,8]{0,1:T(8,128)(2,1)S(1)} %get-tuple-element.28, bf16[256,8]{0,1:T(8,128)(2,1)S(1)} %get-tuple-element.27), kind=kOutput, calls=%fused_computation.11 | convolution fusion | flops 268451840 | bytes 18882560 | tf_op jit(solution)/shard_map/srt,tc->csr/dot_general | solution.py:43
  10.4 2.4 copy.50
  12.8 8.2 %all-to-all-start = ((f32[2,8,128,256]{3,0,2,1:T(2,128)}), f32[2,8,128,256]{3,0,2,1:T(2,128)}, u32[]{:S(2)}, u32[]{:S(2)}) async-start(f32[2,8,128,256]{3,0,2,1:T(2,128)} %copy.50), calls=%async_computation | async-start | bytes 4194304 | tf_op jit(solution)/shard_map/all_to_all | solution.py:45
  20.9 28.7 %all-to-all-done = f32[2,8,128,256]{3,0,2,1:T(2,128)} async-done(((f32[2,8,128,256]{3,0,2,1:T(2,128)}), f32[2,8,128,256]{3,0,2,1:T(2,128)}, u32[]{:S(2)}, u32[]{:S(2)}) %all-to-all-start) | async-done | bytes 2097184 | tf_op jit(solution)/shard_map/all_to_all | solution.py:45
  49.6 2.7 %copy.51 = f32[2,8,128,256]{2,3,1,0:T(8,128)S(1)} copy(f32[2,8,128,256]{3,0,2,1:T(2,128)} %all-to-all-done) | data formatting | bytes 4194304 | tf_op jit(solution)/shard_map/all_to_all | solution.py:45
  52.6 1.5 collective-permute-start.2
  54.1 0.7 collective-permute-start.1
  54.9 1.2 pad_maximum_fusion.3
  56.1 11.0 %collective-permute-done.2 = f32[2,128,512]{1,2,0:T(8,128)S(1)} collective-permute-done((f32[2,128,512]{1,2,0:T(8,128)S(1)}, f32[2,128,512]{1,2,0:T(8,128)S(1)}, u32[]{:S(2)}, u32[]{:S(2)}) %collective-permute-start.2) | collective-permute-done | bytes 524320 | tf_op jit(solution)/shard_map/ppermute | solution.py:33
  67.1 11.2 %collective-permute-done.1 = f32[2,128,512]{1,2,0:T(8,128)S(1)} collective-permute-done((f32[2,128,512]{1,2,0:T(8,128)S(1)}, f32[2,128,512]{1,2,0:T(8,128)S(1)}, u32[]{:S(2)}, u32[]{:S(2)}) %collective-permute-start.1) | collective-permute-done | bytes 524320 | tf_op jit(solution)/shard_map/ppermute | solution.py:33
  78.4 0.8 copy-done
  79.2 0.7 collective-permute-start.3
  80.6 1.5 broadcast_in_dim.8
  82.0 1.0 constant_dynamic-update-slice_fusion.2
  83.1 32.0 %collective-permute-done.3 = f32[2,128,1536]{1,2,0:T(8,128)} collective-permute-done((f32[2,128,1536]{1,2,0:T(8,128)}, f32[2,128,1536]{1,2,0:T(8,128)}, u32[]{:S(2)}, u32[]{:S(2)}) %collective-permute-start.3) | collective-permute-done | bytes 1572896 | tf_op jit(solution)/shard_map/ppermute | solution.py:33
  115.0 1.9 slice_dynamic-update-slice_fusion.2
  116.9 1.9 slice_dynamic-update-slice_fusion.1
  118.8 1.9 slice_dynamic-update-slice_fusion
  120.6 1.3 collective-permute-start.4
  121.9 0.9 constant_dynamic-update-slice_fusion.1
  122.8 2.7 %collective-permute-start.8 = (f32[2,256,512]{1,2,0:T(8,128)}, f32[2,256,512]{1,2,0:T(8,128)}, u32[]{:S(2)}, u32[]{:S(2)}) collective-permute-start(f32[2,256,512]{1,2,0:T(8,128)} %constant_dynamic-update-slice_fusion.1), channel_id=1, source_target_pairs={{0,12},{1,13},{2,14},{3,15},{4,0},{5,1},{6,2},{7,3},{8,4},{9,5},{1... | collective-permute-start | bytes 3145736 | tf_op jit(solution)/shard_map/ppermute | solution.py:33
  125.5 1.1 constant_dynamic-slice_fusion.13
  126.6 1.1 pad_maximum_fusion.4
  128.4 20.0 %collective-permute-done.8 = f32[2,256,512]{1,2,0:T(8,128)} collective-permute-done((f32[2,256,512]{1,2,0:T(8,128)}, f32[2,256,512]{1,2,0:T(8,128)}, u32[]{:S(2)}, u32[]{:S(2)}) %collective-permute-start.8) | collective-permute-done | bytes 1048608 | tf_op jit(solution)/shard_map/ppermute | solution.py:33
  148.4 3.4 %collective-permute-start.10 = (f32[2,256,512]{1,2,0:T(8,128)}, f32[2,256,512]{1,2,0:T(8,128)}, u32[]{:S(2)}, u32[]{:S(2)}) collective-permute-start(f32[2,256,512]{1,2,0:T(8,128)} %collective-permute-done.8), channel_id=1, source_target_pairs={{0,12},{1,13},{2,14},{3,15},{4,0},{5,1},{6,2},{7,3},{8,4},{9,5},{1... | collective-permute-start | bytes 3145736 | tf_op jit(solution)/shard_map/ppermute | solution.py:33
  151.8 1.9 collective-permute-done.5
  153.7 3.2 %pad_maximum_fusion = f32[2,512,4,4,128]{1,4,3,2,0:T(8,128)S(1)} fusion(f32[2,128,4,4,128]{1,4,3,2,0:T(8,128)} %bitcast.13, f32[2,128,4,4,128]{1,4,3,2,0:T(8,128)} %bitcast.12, f32[2,128,4,4,128]{1,4,3,2,0:T(8,128)} %bitcast.11, f32[2,128,4,4,128]{1,4,3,2,0:T(8,128)S(1)} %bitcast.156), kind=kLoop, calls=%fused_computation | loop fusion | flops 6291456 | bytes 16777216 | tf_op jit(solution)/shard_map/concatenate | solution.py:70
  156.8 1.0 constant_dynamic-slice_fusion.7
  157.9 1.4 pad_maximum_fusion.1
  159.3 1.9 fusion.17
  161.2 5.0 %fusion.15 = f32[2,512,2,512]{3,1,2,0:T(8,128)} fusion(f32[2,256,512]{1,2,0:T(8,128)} %constant_dynamic-update-slice_fusion.1, f32[2,512,2048]{1,2,0:T(8,128)S(1)} %bitcast.147, s32[]{:T(128)S(6)} %select_n.118), kind=kOutput, calls=%fused_computation.30 | convolution fusion | flops 1610612736 | bytes 6291460 | tf_op jit(solution)/shard_map/aik,bkj->abij/dot_general | solution.py:79
  166.2 5.0 %fusion.7 = f32[2,512,2,512]{3,1,2,0:T(8,128)} fusion(f32[2,256,512]{1,2,0:T(8,128)} %collective-permute-done.8, f32[2,512,2048]{1,2,0:T(8,128)S(1)} %bitcast.148, s32[]{:T(128)S(6)} %select_n.124), kind=kOutput, calls=%fused_computation.22 | convolution fusion | flops 1610612736 | bytes 6291460 | tf_op jit(solution)/shard_map/aik,bkj->abij/dot_general | solution.py:79
  171.2 5.1 %fusion.13 = f32[2,512,2,512]{3,1,2,0:T(8,128)} fusion(f32[2,256,512]{1,2,0:T(8,128)} %collective-permute-done.5, f32[2,512,2048]{1,2,0:T(8,128)S(1)} %bitcast.149, s32[]{:T(128)S(6)} %select_n.120), kind=kOutput, calls=%fused_computation.28 | convolution fusion | flops 1610612736 | bytes 6291460 | tf_op jit(solution)/shard_map/aik,bkj->abij/dot_general | solution.py:79
  176.3 22.3 %collective-permute-done.9 = f32[2,256,512]{1,2,0:T(8,128)} collective-permute-done((f32[2,256,512]{1,2,0:T(8,128)}, f32[2,256,512]{1,2,0:T(8,128)}, u32[]{:S(2)}, u32[]{:S(2)}) %collective-permute-start.9) | collective-permute-done | bytes 1048608 | tf_op jit(solution)/shard_map/ppermute | solution.py:33
  198.6 5.0 %fusion.5 = f32[2,512,2,512]{3,1,2,0:T(8,128)} fusion(f32[2,256,512]{1,2,0:T(8,128)} %collective-permute-done.9, f32[2,512,2048]{1,2,0:T(8,128)S(1)} %bitcast.150, s32[]{:T(128)S(6)} %select_n.126), kind=kOutput, calls=%fused_computation.20 | convolution fusion | flops 1610612736 | bytes 6291460 | tf_op jit(solution)/shard_map/aik,bkj->abij/dot_general | solution.py:79
  203.6 3.8 %fusion.9 = f32[2,512,2,512]{3,1,2,0:T(8,128)} fusion(f32[2,256,512]{1,2,0:T(8,128)S(1)} %collective-permute-done.7, f32[2,512,2048]{1,2,0:T(8,128)S(1)} %bitcast.151, s32[]{:T(128)S(6)} %select_n.123), kind=kOutput, calls=%fused_computation.24 | convolution fusion | flops 1610612736 | bytes 6291460 | tf_op jit(solution)/shard_map/aik,bkj->abij/dot_general | solution.py:79
  207.4 5.3 %fusion.11 = f32[2,512,2,512]{3,1,2,0:T(8,128)} fusion(f32[2,256,512]{1,2,0:T(8,128)} %collective-permute-done.6, f32[2,512,2048]{1,2,0:T(8,128)S(1)} %bitcast.152, s32[]{:T(128)S(6)} %select_n.122), kind=kOutput, calls=%fused_computation.26 | convolution fusion | flops 1610612736 | bytes 6291460 | tf_op jit(solution)/shard_map/aik,bkj->abij/dot_general | solution.py:79
  212.7 12.0 %add_bitcast_fusion = f32[2,2,512,512]{2,3,0,1:T(8,128)S(1)} fusion(f32[2,512,2,512]{3,1,2,0:T(8,128)} %fusion.5, f32[2,512,2,512]{3,1,2,0:T(8,128)} %fusion.7, f32[2,512,2,512]{3,1,2,0:T(8,128)} %fusion.9, f32[2,512,2,512]{3,1,2,0:T(8,128)} %fusion.11, f32[2,512,2,512]{3,1,2,0:T(8,128)} %fusion.13, f32[2,512,2,512]{3,1,2,0:T(8,128)S(1)} %fusion.17, ...), kind=kOutput, calls=%fused_computation.2 | convolution fusion | flops 1617952768 | bytes 35651588 | tf_op jit(solution)/shard_map/aik,bkj->abij/dot_general | solution.py:79
  224.6 1.8 fusion.29
  226.4 1.8 fusion.33
  228.4 1.2 collective-permute-start.11
  230.3 0.7 collective-permute-start.12
  231.1 12.7 %collective-permute-done.13 = f32[2,128,512]{1,2,0:T(8,128)S(1)} collective-permute-done((f32[2,128,512]{1,2,0:T(8,128)S(1)}, f32[2,128,512]{1,2,0:T(8,128)S(1)}, u32[]{:S(2)}, u32[]{:S(2)}) %collective-permute-start.13) | collective-permute-done | bytes 524320 | tf_op jit(solution)/shard_map/ppermute | solution.py:33
  243.8 10.3 %collective-permute-done.12 = f32[2,128,512]{1,2,0:T(8,128)S(1)} collective-permute-done((f32[2,128,512]{1,2,0:T(8,128)S(1)}, f32[2,128,512]{1,2,0:T(8,128)S(1)}, u32[]{:S(2)}, u32[]{:S(2)}) %collective-permute-start.12) | collective-permute-done | bytes 524320 | tf_op jit(solution)/shard_map/ppermute | solution.py:33
  254.3 1.1 constant_dynamic-slice_fusion.3
  255.4 1.2 copy.59
  256.7 1.2 copy.62
  258.3 1.5 maximum_bitcast_fusion
  (25 shorter events, 3.3 us)
Async XLA Ops:
  12.8 36.9 %all-to-all-start = ((f32[2,8,128,256]{3,0,2,1:T(2,128)}), f32[2,8,128,256]{3,0,2,1:T(2,128)}, u32[]{:S(2)}, u32[]{:S(2)}) async-start(f32[2,8,128,256]{3,0,2,1:T(2,128)} %copy.50), calls=%async_computation | async-start | bytes 4194304 | tf_op jit(solution)/shard_map/all_to_all | solution.py:45
  52.6 14.5 %collective-permute-start.2 = (f32[2,128,512]{1,2,0:T(8,128)S(1)}, f32[2,128,512]{1,2,0:T(8,128)S(1)}, u32[]{:S(2)}, u32[]{:S(2)}) collective-permute-start(f32[2,128,512]{1,2,0:T(8,128)S(1)} %get-tuple-element.19), channel_id=1, source_target_pairs={{0,3},{1,2},{2,1},{3,0},{4,7},{5,6},{6,5},{7,4},{8,11},{9,10},{10,... | collective-permute-start | bytes 1572872 | tf_op jit(solution)/shard_map/ppermute | solution.py:33
  54.1 24.2 %collective-permute-start.1 = (f32[2,128,512]{1,2,0:T(8,128)S(1)}, f32[2,128,512]{1,2,0:T(8,128)S(1)}, u32[]{:S(2)}, u32[]{:S(2)}) collective-permute-start(f32[2,128,512]{1,2,0:T(8,128)S(1)} %get-tuple-element.23), channel_id=1, source_target_pairs={{0,2},{1,3},{2,0},{3,1},{4,6},{5,7},{6,4},{7,5},{8,10},{9,11},{10,... | collective-permute-start | bytes 1572872 | tf_op jit(solution)/shard_map/ppermute | solution.py:33
  78.4 0.8 copy-start
  79.2 35.9 %collective-permute-start.3 = (f32[2,128,1536]{1,2,0:T(8,128)}, f32[2,128,1536]{1,2,0:T(8,128)}, u32[]{:S(2)}, u32[]{:S(2)}) collective-permute-start(f32[2,128,1536]{1,2,0:T(8,128)} %pad_maximum_fusion.3), channel_id=1, source_target_pairs={{0,2},{1,3},{2,0},{3,1},{4,6},{5,7},{6,4},{7,5},{8,10},{9,11},{10,... | collective-permute-start | bytes 4718600 | tf_op jit(solution)/shard_map/ppermute | solution.py:33
  79.9 45.7 %collective-permute-start = (f32[2,128,2048]{1,2,0:T(8,128)S(1)}, f32[2,128,2048]{1,2,0:T(8,128)}, u32[]{:S(2)}, u32[]{:S(2)}) collective-permute-start(f32[2,128,2048]{1,2,0:T(8,128)S(1)} %bitcast.155), channel_id=1, source_target_pairs={{0,1},{1,0},{2,3},{3,2},{4,5},{5,4},{6,7},{7,6},{8,9},{9,8},{10,11... | collective-permute-start | bytes 6291464 | tf_op jit(solution)/shard_map/ppermute | solution.py:33
  80.6 1.5 copy-start.1
  120.6 33.0 %collective-permute-start.4 = (f32[2,128,2048]{1,2,0:T(8,128)}, f32[2,128,2048]{1,2,0:T(8,128)}, u32[]{:S(2)}, u32[]{:S(2)}) collective-permute-start(f32[2,128,2048]{1,2,0:T(8,128)} %slice_dynamic-update-slice_fusion), channel_id=1, source_target_pairs={{0,1},{1,0},{2,3},{3,2},{4,5},{5,4},{6,7},{7,6},{8,9},{9,8},{10,11... | collective-permute-start | bytes 6291464 | tf_op jit(solution)/shard_map/ppermute | solution.py:33
  121.9 5.8 %copy-start.2 = (f32[1,2]{1,0:T(1,128)S(1)}, f32[1,2]{1,0:T(1,128)}, u32[]{:S(2)}) copy-start(f32[1,2]{1,0:T(1,128)} %param.3) | copy-start | bytes 28
  122.8 25.6 %collective-permute-start.8 = (f32[2,256,512]{1,2,0:T(8,128)}, f32[2,256,512]{1,2,0:T(8,128)}, u32[]{:S(2)}, u32[]{:S(2)}) collective-permute-start(f32[2,256,512]{1,2,0:T(8,128)} %constant_dynamic-update-slice_fusion.1), channel_id=1, source_target_pairs={{0,12},{1,13},{2,14},{3,15},{4,0},{5,1},{6,2},{7,3},{8,4},{9,5},{1... | collective-permute-start | bytes 3145736 | tf_op jit(solution)/shard_map/ppermute | solution.py:33
  127.7 26.0 %collective-permute-start.5 = (f32[2,256,512]{1,2,0:T(8,128)}, f32[2,256,512]{1,2,0:T(8,128)}, u32[]{:S(2)}, u32[]{:S(2)}) collective-permute-start(f32[2,256,512]{1,2,0:T(8,128)} %pad_maximum_fusion.4), channel_id=1, source_target_pairs={{0,4},{1,5},{2,6},{3,7},{4,8},{5,9},{6,10},{7,11},{8,12},{9,13},{1... | collective-permute-start | bytes 3145736 | tf_op jit(solution)/shard_map/ppermute | solution.py:33
  128.4 75.2 %collective-permute-start.7 = (f32[2,256,512]{1,2,0:T(8,128)}, f32[2,256,512]{1,2,0:T(8,128)S(1)}, u32[]{:S(2)}, u32[]{:S(2)}) collective-permute-start(f32[2,256,512]{1,2,0:T(8,128)} %constant_dynamic-update-slice_fusion.1), channel_id=1, source_target_pairs={{0,4},{1,5},{2,6},{3,7},{4,8},{5,9},{6,10},{7,11},{8,12},{9,13},{1... | collective-permute-start | bytes 3145736 | tf_op jit(solution)/shard_map/ppermute | solution.py:33
  148.4 64.3 %collective-permute-start.10 = (f32[2,256,512]{1,2,0:T(8,128)}, f32[2,256,512]{1,2,0:T(8,128)}, u32[]{:S(2)}, u32[]{:S(2)}) collective-permute-start(f32[2,256,512]{1,2,0:T(8,128)} %collective-permute-done.8), channel_id=1, source_target_pairs={{0,12},{1,13},{2,14},{3,15},{4,0},{5,1},{6,2},{7,3},{8,4},{9,5},{1... | collective-permute-start | bytes 3145736 | tf_op jit(solution)/shard_map/ppermute | solution.py:33
  151.8 55.6 %collective-permute-start.6 = (f32[2,256,512]{1,2,0:T(8,128)}, f32[2,256,512]{1,2,0:T(8,128)}, u32[]{:S(2)}, u32[]{:S(2)}) collective-permute-start(f32[2,256,512]{1,2,0:T(8,128)} %pad_maximum_fusion.4), channel_id=1, source_target_pairs={{0,12},{1,13},{2,14},{3,15},{4,0},{5,1},{6,2},{7,3},{8,4},{9,5},{1... | collective-permute-start | bytes 3145736 | tf_op jit(solution)/shard_map/ppermute | solution.py:33
  153.7 44.9 %collective-permute-start.9 = (f32[2,256,512]{1,2,0:T(8,128)}, f32[2,256,512]{1,2,0:T(8,128)}, u32[]{:S(2)}, u32[]{:S(2)}) collective-permute-start(f32[2,256,512]{1,2,0:T(8,128)} %collective-permute-done.5), channel_id=1, source_target_pairs={{0,4},{1,5},{2,6},{3,7},{4,8},{5,9},{6,10},{7,11},{8,12},{9,13},{1... | collective-permute-start | bytes 3145736 | tf_op jit(solution)/shard_map/ppermute | solution.py:33
  228.4 2.8 %collective-permute-start.11 = (f32[2,128,512]{1,2,0:T(8,128)S(1)}, f32[2,128,512]{1,2,0:T(8,128)S(1)}, u32[]{:S(2)}, u32[]{:S(2)}) collective-permute-start(f32[2,128,512]{1,2,0:T(8,128)S(1)} %get-tuple-element.16), channel_id=1, source_target_pairs={{0,1},{1,0},{2,3},{3,2},{4,5},{5,4},{6,7},{7,6},{8,9},{9,8},{10,11... | collective-permute-start | bytes 1572872 | tf_op jit(solution)/shard_map/ppermute | solution.py:33
  229.6 14.2 %collective-permute-start.13 = (f32[2,128,512]{1,2,0:T(8,128)S(1)}, f32[2,128,512]{1,2,0:T(8,128)S(1)}, u32[]{:S(2)}, u32[]{:S(2)}) collective-permute-start(f32[2,128,512]{1,2,0:T(8,128)S(1)} %get-tuple-element.17), channel_id=1, source_target_pairs={{0,3},{1,2},{2,1},{3,0},{4,7},{5,6},{6,5},{7,4},{8,11},{9,10},{10,... | collective-permute-start | bytes 1572872 | tf_op jit(solution)/shard_map/ppermute | solution.py:33
  230.3 23.8 %collective-permute-start.12 = (f32[2,128,512]{1,2,0:T(8,128)S(1)}, f32[2,128,512]{1,2,0:T(8,128)S(1)}, u32[]{:S(2)}, u32[]{:S(2)}) collective-permute-start(f32[2,128,512]{1,2,0:T(8,128)S(1)} %get-tuple-element.18), channel_id=1, source_target_pairs={{0,2},{1,3},{2,0},{3,1},{4,6},{5,7},{6,4},{7,5},{8,10},{9,11},{10,... | collective-permute-start | bytes 1572872 | tf_op jit(solution)/shard_map/ppermute | solution.py:33

commit v4 on v3

--- a/solution.py
+++ b/solution.py
@@ -67,17 +67,16 @@
     for m in range(1, GROUP):
         q2 = lax.dynamic_update_slice_in_dim(q2, rest[:, :, (m - 1) * cw:m * cw], (p ^ m) * cw, axis=2)
     q3 = send(q2, xor_perm(nblk, 1))
-    rows = jnp.concatenate([own, q1, q2, q3], axis=1)
 
-    l5 = rows.reshape(2, gw, ny, GROUP, rb)
-    lx = jnp.concatenate(
-        [lax.dynamic_slice_in_dim(l5, p ^ m, 1, axis=3) for m in range(GROUP)], axis=3
-    ).reshape(2, gw, n)
+    def reorder(r):
+        l5 = r.reshape(2, r.shape[1], ny, GROUP, rb)
+        return jnp.concatenate(
+            [lax.dynamic_slice_in_dim(l5, p ^ m, 1, axis=3) for m in range(GROUP)], axis=3
+        ).reshape(2, r.shape[1], n)
 
-    def contrib(g, pc, lo, hi):
-        lg = lax.dynamic_slice_in_dim(lx, g * gw + lo * rb, (hi - lo) * rb, axis=2)
+    def mm(lhs, rhs):
         return jnp.einsum(
-            "aik,bkj->abij", lg, pc,
+            "aik,bkj->abij", lhs, rhs,
             precision=lax.Precision.HIGH, preferred_element_type=jnp.float32,
         )
 
@@ -93,10 +92,27 @@
     fb = send(db, dn)
 
     half = GROUP // 2
-    t = contrib(y, part_a, 0, half) + contrib(y, part_b, half, GROUP)
-    t = t + contrib((y - 1) % ny, ua, 0, half) + contrib((y + 1) % ny, da, 0, half)
-    t = t + contrib((y - 1) % ny, ub, half, GROUP) + contrib((y + 1) % ny, db, half, GROUP)
-    t = t + contrib((y + 2) % ny, fa, 0, half) + contrib((y + 2) % ny, fb, half, GROUP)
+    hk = half * rb
+    pieces = [
+        (y, 0, part_a), (y, 1, part_b),
+        ((y - 1) % ny, 0, ua), ((y + 1) % ny, 0, da),
+        ((y - 1) % ny, 1, ub), ((y + 1) % ny, 1, db),
+        ((y + 2) % ny, 0, fa), ((y + 2) % ny, 1, fb),
+    ]
+
+    early = reorder(jnp.concatenate([own, q1], axis=1))
+    t_early = None
+    for g, h, pc in pieces:
+        lhs = lax.dynamic_slice_in_dim(early, g * gw + h * hk, hk, axis=2)
+        term = mm(lhs, pc)
+        t_early = term if t_early is None else t_early + term
+
+    right = jnp.zeros((2, n, cw), jnp.float32)
+    for g, h, pc in pieces:
+        right = lax.dynamic_update_slice_in_dim(right, pc, g * gw + h * hk, axis=1)
+    late = reorder(jnp.concatenate([q2, q3], axis=1))
+    t_late = mm(late, right)
+    t = jnp.concatenate([t_early, t_late], axis=2)
 
     prod_re = t[0, 0] - t[1, 1]
     prod_im = t[0, 1] + t[1, 0]

time: 261 us -> 258 us (0.989)
  waiting for transfers between devices: 150 us -> 73.9 us
  local copies, waits for them, and re-layouts: 21.9 us -> 63.7 us
  blocking collectives: 0 us -> 35.6 us
  matrix products: 53.2 us -> 43.8 us
  other arithmetic: 12.4 us -> 21.2 us
  starting transfers between devices: 21.9 us -> 18.8 us
    ppermute x14, waiting for transfers between devices: 122 us -> 73.9 us  [send(): return lax.ppermute(x, 'blk', perm)]
    all_to_all x0 -> x1, blocking collectives: none -> 35.6 us  [on_device(): lax.all_to_all(projected, 'freq', split_axis=1, concat_axis=3, tiled=True)]
    all_to_all x1 -> x0, waiting for transfers between devices: 28.7 us -> none  [on_device(): lax.all_to_all(projected, 'freq', split_axis=1, concat_axis=3, tiled=True)]
    dynamic_update_slice x0 -> x7, local copies, waits for them, and re-layouts: none -> 14.1 us  [on_device(): right = lax.dynamic_update_slice_in_dim(right, pc, g * gw + h * hk, axis=1)]
    reshape x0 -> x2, local copies, waits for them, and re-layouts: none -> 11.5 us  [the longest x1 6.02 us: reorder(): l5 = r.reshape(2, r.shape[1], ny, GROUP, rb)]
    dot_general x8 -> x9, matrix products: 43 us -> 33.5 us  [mm(): jnp.einsum('aik,bkj->abij', lhs, rhs, precision=lax.Precision.HIGH, prefe...]
    concatenate x2 -> x4, other arithmetic: 4.56 us -> 13.3 us  [the longest x2 6.8 us: reorder(): jnp.concatenate([lax.dynamic_slice_in_dim(l5, p ^ m, 1, axis=3) for m in...]
    all_to_all x1 -> x0, starting transfers between devices: 8.15 us -> none  [on_device(): lax.all_to_all(projected, 'freq', split_axis=1, concat_axis=3, tiled=True)]
  transfers between devices with their start and end apart: 15 -> 14, of which waited for: 10 -> 6; matrix products, arithmetic and copies ran while one was open for 19% -> 34% of each run, Pallas kernels for 0% -> 0%
where the time goes in v4:
time: 258 us; the launch traced here: 257 us
  waiting for transfers between devices  73.9 us (29%)
  local copies, waits for them, and re-layouts  63.7 us (25%)
  matrix products  43.8 us (17%)
  blocking collectives  35.6 us (14%)
  other arithmetic  21.2 us (8%)
  starting transfers between devices  18.8 us (7%)
    ppermute x14, waiting for transfers between devices, send(): return lax.ppermute(x, 'blk', perm)  73.9 us
    all_to_all x1, blocking collectives, on_device(): lax.all_to_all(projected, 'freq', split_axis=1, concat_axis=3, tiled=True)  35.6 us
    dot_general x9, matrix products, mm(): jnp.einsum('aik,bkj->abij', lhs, rhs, precision=lax.Precision.HIGH, prefe...  33.5 us
    ppermute x14, starting transfers between devices, send(): return lax.ppermute(x, 'blk', perm)  18.8 us
    dynamic_update_slice x7, local copies, waits for them, and re-layouts, on_device(): right = lax.dynamic_update_slice_in_dim(right, pc, g * gw + h * hk, axis=1)  14.1 us
    dynamic_slice x1, local copies, waits for them, and re-layouts, reorder(): lax.dynamic_slice_in_dim(l5, p ^ m, 1, axis=3)  11.5 us
    dot_general x1, matrix products, on_device(): jnp.einsum('srt,tc->csr', traces, table, preferred_element_type=jnp.float32)  10.2 us
    concatenate x2, other arithmetic, reorder(): jnp.concatenate([lax.dynamic_slice_in_dim(l5, p ^ m, 1, axis=3) for m in...  6.8 us
  transfers between devices with their start and end apart: 14, of which 6 were waited for; matrix products, arithmetic and copies ran while one was open for 34% of the time, Pallas kernels for 0%

profile of v4, /device:TPU:1, one launch (start us, length us, event | category | flops | bytes accessed | tf_op | source)
XLA Modules:
  0.0 257.3 jit_solution(11199708942037492192)
XLA Ops:
  0.1 10.2 %convolution_bitcast_fusion = f32[2,8,128,256]{3,1,0,2:T(8,128)S(1)} fusion(bf16[128,256,256]{2,1,0:T(8,128)(2,1)} %param.2, bf16[256,8]{0,1:T(8,128)(2,1)S(1)} %get-tuple-element.37, bf16[256,8]{0,1:T(8,128)(2,1)S(1)} %get-tuple-element.36), kind=kOutput, calls=%fused_computation.30 | convolution fusion | flops 268451840 | bytes 18882560 | tf_op jit(solution)/shard_map/srt,tc->csr/dot_general | solution.py:43
  10.4 1.1 copy.19
  11.5 35.6 %all_to_all.15 = f32[2,8,128,256]{3,0,2,1:T(2,128)S(1)} all-to-all(f32[2,8,128,256]{3,0,2,1:T(2,128)S(1)} %copy.19), channel_id=1, replica_groups=mesh['freq'=8,'blk'=16] {'freq'}, dimensions={1} | all-to-all | bytes 4194304 | tf_op jit(solution)/shard_map/all_to_all | solution.py:45
  47.1 2.5 copy.53
  49.6 2.7 %squeeze.27 = f32[2,128,2048]{2,1,0:T(8,128)} reshape(f32[2,1,128,8,256]{4,3,2,0,1:T(8,128)} %bitcast.167) | data formatting | bytes 4194304 | tf_op jit(solution)/shard_map/squeeze | solution.py:46
  52.3 1.8 collective-permute-start
  54.1 3.0 %constant_dynamic-slice_fusion.10 = (f32[2,128,512]{2,1,0:T(8,128)}, f32[2,128,512]{2,1,0:T(8,128)S(1)}, f32[2,128,512]{2,1,0:T(8,128)S(1)}, f32[2,128,512]{2,1,...) fusion(f32[2,128,2048]{2,1,0:T(8,128)} %squeeze.27, s32[]{:T(128)S(6)} %select_n.117, ...), kind=kLoop, calls=%fused_computation.128 | loop fusion | bytes 6291480 | tf_op jit(solution)/shard_map/dynamic_slice | solution.py:57
  58.7 1.2 pad_maximum_fusion.4
  59.9 10.6 %collective-permute-done.1 = f32[2,128,512]{2,1,0:T(8,128)S(1)} collective-permute-done((f32[2,128,512]{2,1,0:T(8,128)S(1)}, f32[2,128,512]{2,1,0:T(8,128)S(1)}, u32[]{:S(2)}, u32[]{:S(2)}) %collective-permute-start.1) | collective-permute-done | bytes 524320 | tf_op jit(solution)/shard_map/ppermute | solution.py:33
  70.5 11.4 %collective-permute-done.2 = f32[2,128,512]{2,1,0:T(8,128)S(1)} collective-permute-done((f32[2,128,512]{2,1,0:T(8,128)S(1)}, f32[2,128,512]{2,1,0:T(8,128)S(1)}, u32[]{:S(2)}, u32[]{:S(2)}) %collective-permute-start.2) | collective-permute-done | bytes 524320 | tf_op jit(solution)/shard_map/ppermute | solution.py:33
  82.7 1.6 broadcast_in_dim.12
  85.2 2.8 %collective-permute-start.6 = (f32[2,256,512]{2,1,0:T(8,128)S(1)}, f32[2,256,512]{2,1,0:T(8,128)}, u32[]{:S(2)}, u32[]{:S(2)}) collective-permute-start(f32[2,256,512]{2,1,0:T(8,128)S(1)} %constant_dynamic-update-slice_fusion.9), channel_id=1, source_target_pairs={{0,12},{1,13},{2,14},{3,15},{4,0},{5,1},{6,2},{7,3},{8,4},{9,5},{1... | collective-permute-start | bytes 3145736 | tf_op jit(solution)/shard_map/ppermute | solution.py:33
  88.6 2.4 copy.20
  91.0 19.1 %collective-permute-done.6 = f32[2,256,512]{2,1,0:T(8,128)} collective-permute-done((f32[2,256,512]{2,1,0:T(8,128)S(1)}, f32[2,256,512]{2,1,0:T(8,128)}, u32[]{:S(2)}, u32[]{:S(2)}) %collective-permute-start.6) | collective-permute-done | bytes 1048608 | tf_op jit(solution)/shard_map/ppermute | solution.py:33
  110.0 3.5 %collective-permute-start.8 = (f32[2,256,512]{2,1,0:T(8,128)}, f32[2,256,512]{2,1,0:T(8,128)}, u32[]{:S(2)}, u32[]{:S(2)}) collective-permute-start(f32[2,256,512]{2,1,0:T(8,128)} %collective-permute-done.6), channel_id=1, source_target_pairs={{0,12},{1,13},{2,14},{3,15},{4,0},{5,1},{6,2},{7,3},{8,4},{9,5},{1... | collective-permute-start | bytes 3145736 | tf_op jit(solution)/shard_map/ppermute | solution.py:33
  115.9 1.2 pad_maximum_fusion.6
  117.1 2.7 %collective-permute-start.4 = (f32[2,256,512]{2,1,0:T(8,128)}, f32[2,256,512]{2,1,0:T(8,128)}, u32[]{:S(2)}, u32[]{:S(2)}) collective-permute-start(f32[2,256,512]{2,1,0:T(8,128)} %get-tuple-element.32), channel_id=1, source_target_pairs={{0,12},{1,13},{2,14},{3,15},{4,0},{5,1},{6,2},{7,3},{8,4},{9,5},{1... | collective-permute-start | bytes 3145736 | tf_op jit(solution)/shard_map/ppermute | solution.py:33
  119.8 2.0 slice_dynamic-update-slice_fusion.2
  121.8 1.9 slice_dynamic-update-slice_fusion.1
  123.7 1.9 slice_dynamic-update-slice_fusion
  125.5 2.1 collective-permute-start.10
  127.6 2.9 %copy.40 = f32[2,128,2048]{1,2,0:T(8,128)} copy(f32[2,128,2048]{2,1,0:T(8,128)} %collective-permute-done) | data formatting | bytes 4194304 | tf_op jit(solution)/shard_map/concatenate | solution.py:103
  130.5 1.8 fusion.13
  135.6 2.4 fusion.30
  138.0 3.7 %fusion.22 = f32[2,512,2,256]{1,3,2,0:T(8,128)} fusion(f32[2,256,512]{2,1,0:T(8,128)} %collective-permute-done.6, f32[2,256,2048]{1,2,0:T(8,128)S(1)} %bitcast.159, s32[]{:T(128)S(6)} %select_n.132), kind=kOutput, calls=%fused_computation.49 | convolution fusion | flops 805306368 | bytes 3670020 | tf_op jit(solution)/shard_map/aik,bkj->abij/dot_general | solution.py:78
  141.7 3.6 %fusion.24 = f32[2,512,2,256]{1,3,2,0:T(8,128)} fusion(f32[2,256,512]{2,1,0:T(8,128)} %collective-permute-done.5, f32[2,256,2048]{1,2,0:T(8,128)S(1)} %bitcast.160, s32[]{:T(128)S(6)} %select_n.131), kind=kOutput, calls=%fused_computation.51 | convolution fusion | flops 805306368 | bytes 3670020 | tf_op jit(solution)/shard_map/aik,bkj->abij/dot_general | solution.py:78
  145.3 2.3 constant_dynamic-update-slice_fusion.6
  147.6 9.9 %collective-permute-done.4 = f32[2,256,512]{2,1,0:T(8,128)} collective-permute-done((f32[2,256,512]{2,1,0:T(8,128)}, f32[2,256,512]{2,1,0:T(8,128)}, u32[]{:S(2)}, u32[]{:S(2)}) %collective-permute-start.4) | collective-permute-done | bytes 1048608 | tf_op jit(solution)/shard_map/ppermute | solution.py:33
  157.5 2.2 constant_dynamic-update-slice_fusion.5
  159.8 2.4 constant_dynamic-update-slice_fusion.4
  162.1 2.3 constant_dynamic-update-slice_fusion.3
  164.4 3.6 %fusion.26 = f32[2,512,2,256]{1,3,2,0:T(8,128)} fusion(f32[2,256,512]{2,1,0:T(8,128)} %collective-permute-done.4, f32[2,256,2048]{1,2,0:T(8,128)S(1)} %bitcast.161, s32[]{:T(128)S(6)} %select_n.130), kind=kOutput, calls=%fused_computation.53 | convolution fusion | flops 805306368 | bytes 3670020 | tf_op jit(solution)/shard_map/aik,bkj->abij/dot_general | solution.py:78
  168.0 3.6 %fusion.28 = f32[2,512,2,256]{1,3,2,0:T(8,128)} fusion(f32[2,256,512]{2,1,0:T(8,128)} %collective-permute-done.3, f32[2,256,2048]{1,2,0:T(8,128)S(1)} %bitcast.162, s32[]{:T(128)S(6)} %select_n.128), kind=kOutput, calls=%fused_computation.55 | convolution fusion | flops 805306368 | bytes 3670020 | tf_op jit(solution)/shard_map/aik,bkj->abij/dot_general | solution.py:78
  171.6 4.6 %pad_maximum_fusion.1 = f32[2,256,2048]{2,1,0:T(8,128)} fusion(f32[2,128,2048]{2,1,0:T(8,128)} %collective-permute-done.10, f32[2,128,2048]{2,1,0:T(8,128)} %slice_dynamic-update-slice_fusion), kind=kLoop, calls=%fused_computation.17 | loop fusion | flops 1048576 | bytes 8388608 | tf_op jit(solution)/shard_map/concatenate | solution.py:113
  176.2 6.0 %reshape.118 = f32[2,256,4,4,128]{4,3,2,1,0:T(4,128)} reshape(f32[2,256,2048]{2,1,0:T(8,128)} %pad_maximum_fusion.1) | data formatting | bytes 8388608 | tf_op jit(solution)/shard_map/reshape | solution.py:72
  182.2 11.5 %constant_dynamic-slice_fusion.3 = (f32[2,256,4,1,128]{4,3,2,1,0:T(1,128)S(1)}, f32[2,256,4,1,128]{4,3,2,1,0:T(1,128)S(1)}, f32[2,256,4,1,128]{4,3,2,1,0:T(1,128)S(1)}, f32[2,256,4,1,128]{4,3,2,1,0:T(1,128)}) fusion(f32[2,256,4,4,128]{4,3,2,1,0:T(4,128)} %reshape.118, s32[]{:T(128)S(6)} %select_n.118, s32[]{:T(128)S(6)} %select_n.121, s32[]{:T(128)S(6)} %select_n.120, ...), kind=kLoop, calls=%fused_computation.104 | loop fusion | bytes 8388624 | tf_op jit(solution)/shard_map/dynamic_slice | solution.py:74
  193.8 6.4 %pad_maximum_fusion.2 = f32[2,256,4,4,128]{4,3,2,1,0:T(4,128)} fusion(f32[2,256,4,1,128]{4,3,2,1,0:T(1,128)S(1)} %get-tuple-element.15, f32[2,256,4,1,128]{4,3,2,1,0:T(1,128)S(1)} %get-tuple-element.16, f32[2,256,4,1,128]{4,3,2,1,0:T(1,128)} %get-tuple-element.17, f32[2,256,4,1,128]{4,3,2,1,0:T(1,128)S(1)} %get-tuple-element.14), kind=kLoop, calls=%fused_computation.18 | loop fusion | flops 3145728 | bytes 8388608 | tf_op jit(solution)/shard_map/concatenate | solution.py:73
  200.1 5.5 %reshape.142 = f32[2,256,2048,1]{2,1,0,3:T(8,128)} reshape(f32[2,256,4,4,128]{4,3,2,1,0:T(4,128)} %pad_maximum_fusion.2) | data formatting | bytes 8388608 | tf_op jit(solution)/shard_map/reshape | solution.py:75
  206.6 2.8 %constant_dynamic-update-slice_fusion.1 = f32[2,2048,512]{2,1,0:T(8,128)} fusion(f32[2,2048,512]{2,1,0:T(8,128)} %constant_dynamic-update-slice_fusion.2, f32[2,256,512]{2,1,0:T(8,128)} %collective-permute-done.8, s32[]{:T(128)S(6)} %select_n.135), kind=kLoop, calls=%fused_computation.109 | loop fusion | bytes 2097156 | tf_op jit(solution)/shard_map/dynamic_update_slice | solution.py:112
  209.4 10.0 %fusion.2 = f32[2,2,256,512]{3,2,0,1:T(8,128)S(1)} fusion(f32[2,256,2048,1]{2,1,0,3:T(8,128)S(1)} %copy-done.12, f32[2,2048,512]{2,1,0:T(8,128)} %constant_dynamic-update-slice_fusion.1), kind=kOutput, calls=%fused_computation.29 | convolution fusion | flops 6442450944 | bytes 14680064 | tf_op jit(solution)/shard_map/aik,bkj->abij/dot_general | solution.py:78
  219.5 2.2 fusion.20
  221.8 3.4 %add_bitcast_fusion = f32[2,2,256,512]{3,2,0,1:T(8,128)S(1)} fusion(f32[2,512,2,256]{1,3,2,0:T(8,128)S(1)} %fusion.20, f32[2,512,2,256]{1,3,2,0:T(8,128)S(1)} %copy-done.4, f32[2,512,2,256]{1,3,2,0:T(8,128)S(1)} %copy-done.5, f32[2,512,2,256]{1,3,2,0:T(8,128)S(1)} %copy-done.6, f32[2,512,2,256]{1,3,2,0:T(8,128)S(1)} %copy-done.7, ...), kind=kOutput, calls=%fused_computation.28 | convolution fusion | flops 808976384 | bytes 18350084 | tf_op jit(solution)/shard_map/aik,bkj->abij/dot_general | solution.py:78
  225.2 1.8 fusion.40
  227.0 1.6 fusion.36
  228.8 2.8 %collective-permute-start.13 = (f32[2,128,512]{2,1,0:T(8,128)S(1)}, f32[2,128,512]{2,1,0:T(8,128)S(1)}, u32[]{:S(2)}, u32[]{:S(2)}) collective-permute-start(f32[2,128,512]{2,1,0:T(8,128)S(1)} %get-tuple-element.24), channel_id=1, source_target_pairs={{0,3},{1,2},{2,1},{3,0},{4,7},{5,6},{6,5},{7,4},{8,11},{9,10},{10,... | collective-permute-start | bytes 1572872 | tf_op jit(solution)/shard_map/ppermute | solution.py:33
  232.4 11.5 %collective-permute-done.13 = f32[2,128,512]{2,1,0:T(8,128)S(1)} collective-permute-done((f32[2,128,512]{2,1,0:T(8,128)S(1)}, f32[2,128,512]{2,1,0:T(8,128)S(1)}, u32[]{:S(2)}, u32[]{:S(2)}) %collective-permute-start.13) | collective-permute-done | bytes 524320 | tf_op jit(solution)/shard_map/ppermute | solution.py:33
  243.9 11.4 %collective-permute-done.12 = f32[2,128,512]{2,1,0:T(8,128)S(1)} collective-permute-done((f32[2,128,512]{2,1,0:T(8,128)S(1)}, f32[2,128,512]{2,1,0:T(8,128)S(1)}, u32[]{:S(2)}, u32[]{:S(2)}) %collective-permute-start.12) | collective-permute-done | bytes 524320 | tf_op jit(solution)/shard_map/ppermute | solution.py:33
  255.8 1.5 maximum_bitcast_fusion
  (58 shorter events, 12.1 us)
Async XLA Ops:
  52.3 61.2 %collective-permute-start = (f32[2,128,2048]{2,1,0:T(8,128)}, f32[2,128,2048]{2,1,0:T(8,128)}, u32[]{:S(2)}, u32[]{:S(2)}) collective-permute-start(f32[2,128,2048]{2,1,0:T(8,128)} %squeeze.27), channel_id=1, source_target_pairs={{0,1},{1,0},{2,3},{3,2},{4,5},{5,4},{6,7},{7,6},{8,9},{9,8},{10,11... | collective-permute-start | bytes 6291464 | tf_op jit(solution)/shard_map/ppermute | solution.py:33
  57.1 13.5 %collective-permute-start.1 = (f32[2,128,512]{2,1,0:T(8,128)S(1)}, f32[2,128,512]{2,1,0:T(8,128)S(1)}, u32[]{:S(2)}, u32[]{:S(2)}) collective-permute-start(f32[2,128,512]{2,1,0:T(8,128)S(1)} %get-tuple-element.31), channel_id=1, source_target_pairs={{0,2},{1,3},{2,0},{3,1},{4,6},{5,7},{6,4},{7,5},{8,10},{9,11},{10,... | collective-permute-start | bytes 1572872 | tf_op jit(solution)/shard_map/ppermute | solution.py:33
  57.8 24.2 %collective-permute-start.2 = (f32[2,128,512]{2,1,0:T(8,128)S(1)}, f32[2,128,512]{2,1,0:T(8,128)S(1)}, u32[]{:S(2)}, u32[]{:S(2)}) collective-permute-start(f32[2,128,512]{2,1,0:T(8,128)S(1)} %get-tuple-element.30), channel_id=1, source_target_pairs={{0,3},{1,2},{2,1},{3,0},{4,7},{5,6},{6,5},{7,4},{8,11},{9,10},{10,... | collective-permute-start | bytes 1572872 | tf_op jit(solution)/shard_map/ppermute | solution.py:33
  59.9 28.1 %copy-start.13 = (f32[1,2]{1,0:T(1,128)S(1)}, f32[1,2]{1,0:T(1,128)}, u32[]{:S(2)}) copy-start(f32[1,2]{1,0:T(1,128)} %param.3) | copy-start | bytes 28
  81.9 37.9 %collective-permute-start.9 = (f32[2,128,1536]{2,1,0:T(8,128)}, f32[2,128,1536]{2,1,0:T(8,128)}, u32[]{:S(2)}, u32[]{:S(2)}) collective-permute-start(f32[2,128,1536]{2,1,0:T(8,128)} %pad_maximum_fusion.4), channel_id=1, source_target_pairs={{0,2},{1,3},{2,0},{3,1},{4,6},{5,7},{6,4},{7,5},{8,10},{9,11},{10,... | collective-permute-start | bytes 4718600 | tf_op jit(solution)/shard_map/ppermute | solution.py:33
  85.2 24.9 %collective-permute-start.6 = (f32[2,256,512]{2,1,0:T(8,128)S(1)}, f32[2,256,512]{2,1,0:T(8,128)}, u32[]{:S(2)}, u32[]{:S(2)}) collective-permute-start(f32[2,256,512]{2,1,0:T(8,128)S(1)} %constant_dynamic-update-slice_fusion.9), channel_id=1, source_target_pairs={{0,12},{1,13},{2,14},{3,15},{4,0},{5,1},{6,2},{7,3},{8,4},{9,5},{1... | collective-permute-start | bytes 3145736 | tf_op jit(solution)/shard_map/ppermute | solution.py:33
  91.0 50.7 %collective-permute-start.5 = (f32[2,256,512]{2,1,0:T(8,128)S(1)}, f32[2,256,512]{2,1,0:T(8,128)}, u32[]{:S(2)}, u32[]{:S(2)}) collective-permute-start(f32[2,256,512]{2,1,0:T(8,128)S(1)} %constant_dynamic-update-slice_fusion.9), channel_id=1, source_target_pairs={{0,4},{1,5},{2,6},{3,7},{4,8},{5,9},{6,10},{7,11},{8,12},{9,13},{1... | collective-permute-start | bytes 3145736 | tf_op jit(solution)/shard_map/ppermute | solution.py:33
  110.0 96.6 %collective-permute-start.8 = (f32[2,256,512]{2,1,0:T(8,128)}, f32[2,256,512]{2,1,0:T(8,128)}, u32[]{:S(2)}, u32[]{:S(2)}) collective-permute-start(f32[2,256,512]{2,1,0:T(8,128)} %collective-permute-done.6), channel_id=1, source_target_pairs={{0,12},{1,13},{2,14},{3,15},{4,0},{5,1},{6,2},{7,3},{8,4},{9,5},{1... | collective-permute-start | bytes 3145736 | tf_op jit(solution)/shard_map/ppermute | solution.py:33
  114.6 1.1 copy-start.10
  114.7 1.2 copy-start.8
  117.1 6.5 %copy-start.2 = (f32[2,2048,512]{2,1,0:T(8,128)}, f32[2,2048,512]{2,1,0:T(8,128)S(1)}, u32[]{:S(2)}) copy-start(f32[2,2048,512]{2,1,0:T(8,128)S(1)} %get-tuple-element.33) | copy-start | bytes 25165828
  117.1 28.2 %collective-permute-start.3 = (f32[2,256,512]{2,1,0:T(8,128)}, f32[2,256,512]{2,1,0:T(8,128)}, u32[]{:S(2)}, u32[]{:S(2)}) collective-permute-start(f32[2,256,512]{2,1,0:T(8,128)} %get-tuple-element.32), channel_id=1, source_target_pairs={{0,4},{1,5},{2,6},{3,7},{4,8},{5,9},{6,10},{7,11},{8,12},{9,13},{1... | collective-permute-start | bytes 3145736 | tf_op jit(solution)/shard_map/ppermute | solution.py:33
  117.1 40.4 %collective-permute-start.4 = (f32[2,256,512]{2,1,0:T(8,128)}, f32[2,256,512]{2,1,0:T(8,128)}, u32[]{:S(2)}, u32[]{:S(2)}) collective-permute-start(f32[2,256,512]{2,1,0:T(8,128)} %get-tuple-element.32), channel_id=1, source_target_pairs={{0,12},{1,13},{2,14},{3,15},{4,0},{5,1},{6,2},{7,3},{8,4},{9,5},{1... | collective-permute-start | bytes 3145736 | tf_op jit(solution)/shard_map/ppermute | solution.py:33
  125.5 5.0 %copy-start.1 = (f32[2,8,128,256]{2,3,1,0:T(8,128)S(1)}, f32[2,8,128,256]{2,3,1,0:T(8,128)}, u32[]{:S(2)}) copy-start(f32[2,8,128,256]{2,3,1,0:T(8,128)} %copy.20) | copy-start | bytes 6291460
  125.5 46.0 %collective-permute-start.10 = (f32[2,128,2048]{2,1,0:T(8,128)}, f32[2,128,2048]{2,1,0:T(8,128)}, u32[]{:S(2)}, u32[]{:S(2)}) collective-permute-start(f32[2,128,2048]{2,1,0:T(8,128)} %slice_dynamic-update-slice_fusion), channel_id=1, source_target_pairs={{0,1},{1,0},{2,3},{3,2},{4,5},{5,4},{6,7},{7,6},{8,9},{9,8},{10,11... | collective-permute-start | bytes 6291464 | tf_op jit(solution)/shard_map/ppermute | solution.py:33
  132.3 1.0 copy-start.9
  132.3 1.2 copy-start.11
  132.8 35.2 %copy-start = (f32[2,256,4,4,128]{1,4,3,2,0:T(8,128)}, f32[2,256,4,4,128]{1,4,3,2,0:T(8,128)S(1)}, u32[]{:S(2)}) copy-start(f32[2,256,4,4,128]{1,4,3,2,0:T(8,128)S(1)} %pad_maximum_fusion) | copy-start | bytes 12582916
  145.3 60.3 %collective-permute-start.7 = (f32[2,256,512]{2,1,0:T(8,128)}, f32[2,256,512]{2,1,0:T(8,128)S(1)}, u32[]{:S(2)}, u32[]{:S(2)}) collective-permute-start(f32[2,256,512]{2,1,0:T(8,128)} %collective-permute-done.3), channel_id=1, source_target_pairs={{0,4},{1,5},{2,6},{3,7},{4,8},{5,9},{6,10},{7,11},{8,12},{9,13},{1... | collective-permute-start | bytes 3145736 | tf_op jit(solution)/shard_map/ppermute | solution.py:33
  205.6 3.9 %copy-start.12 = (f32[2,256,2048,1]{2,1,0,3:T(8,128)S(1)}, f32[2,256,2048,1]{2,1,0,3:T(8,128)}, u32[]{:S(2)}) copy-start(f32[2,256,2048,1]{2,1,0,3:T(8,128)} %reshape.142) | copy-start | bytes 12582916
  209.4 12.3 %copy-start.4 = (f32[2,512,2,256]{1,3,2,0:T(8,128)S(1)}, f32[2,512,2,256]{1,3,2,0:T(8,128)}, u32[]{:S(2)}) copy-start(f32[2,512,2,256]{1,3,2,0:T(8,128)} %fusion.22) | copy-start | bytes 6291460
  209.4 12.3 %copy-start.5 = (f32[2,512,2,256]{1,3,2,0:T(8,128)S(1)}, f32[2,512,2,256]{1,3,2,0:T(8,128)}, u32[]{:S(2)}) copy-start(f32[2,512,2,256]{1,3,2,0:T(8,128)} %fusion.24) | copy-start | bytes 6291460
  209.4 12.3 %copy-start.6 = (f32[2,512,2,256]{1,3,2,0:T(8,128)S(1)}, f32[2,512,2,256]{1,3,2,0:T(8,128)}, u32[]{:S(2)}) copy-start(f32[2,512,2,256]{1,3,2,0:T(8,128)} %fusion.26) | copy-start | bytes 6291460
  209.4 12.3 %copy-start.7 = (f32[2,512,2,256]{1,3,2,0:T(8,128)S(1)}, f32[2,512,2,256]{1,3,2,0:T(8,128)}, u32[]{:S(2)}) copy-start(f32[2,512,2,256]{1,3,2,0:T(8,128)} %fusion.28) | copy-start | bytes 6291460
  219.5 2.3 copy-start.3
  228.8 15.1 %collective-permute-start.13 = (f32[2,128,512]{2,1,0:T(8,128)S(1)}, f32[2,128,512]{2,1,0:T(8,128)S(1)}, u32[]{:S(2)}, u32[]{:S(2)}) collective-permute-start(f32[2,128,512]{2,1,0:T(8,128)S(1)} %get-tuple-element.24), channel_id=1, source_target_pairs={{0,3},{1,2},{2,1},{3,0},{4,7},{5,6},{6,5},{7,4},{8,11},{9,10},{10,... | collective-permute-start | bytes 1572872 | tf_op jit(solution)/shard_map/ppermute | solution.py:33
  231.6 23.7 %collective-permute-start.12 = (f32[2,128,512]{2,1,0:T(8,128)S(1)}, f32[2,128,512]{2,1,0:T(8,128)S(1)}, u32[]{:S(2)}, u32[]{:S(2)}) collective-permute-start(f32[2,128,512]{2,1,0:T(8,128)S(1)} %get-tuple-element.25), channel_id=1, source_target_pairs={{0,2},{1,3},{2,0},{3,1},{4,6},{5,7},{6,4},{7,5},{8,10},{9,11},{10,... | collective-permute-start | bytes 1572872 | tf_op jit(solution)/shard_map/ppermute | solution.py:33
  232.4 22.9 %collective-permute-start.11 = (f32[2,128,512]{2,1,0:T(8,128)S(1)}, f32[2,128,512]{2,1,0:T(8,128)S(1)}, u32[]{:S(2)}, u32[]{:S(2)}) collective-permute-start(f32[2,128,512]{2,1,0:T(8,128)S(1)} %get-tuple-element.23), channel_id=1, source_target_pairs={{0,1},{1,0},{2,3},{3,2},{4,5},{5,4},{6,7},{7,6},{8,9},{9,8},{10,11... | collective-permute-start | bytes 1572872 | tf_op jit(solution)/shard_map/ppermute | solution.py:33

commit v5 on v4

--- a/solution.py
+++ b/solution.py
@@ -46,7 +46,6 @@
     own = spectra[:, 0]
     n = own.shape[2]
     rb = src_rows
-    gw = GROUP * rb
     cw = n // GROUP
 
     b = lax.axis_index("blk")
@@ -68,12 +67,6 @@
         q2 = lax.dynamic_update_slice_in_dim(q2, rest[:, :, (m - 1) * cw:m * cw], (p ^ m) * cw, axis=2)
     q3 = send(q2, xor_perm(nblk, 1))
 
-    def reorder(r):
-        l5 = r.reshape(2, r.shape[1], ny, GROUP, rb)
-        return jnp.concatenate(
-            [lax.dynamic_slice_in_dim(l5, p ^ m, 1, axis=3) for m in range(GROUP)], axis=3
-        ).reshape(2, r.shape[1], n)
-
     def mm(lhs, rhs):
         return jnp.einsum(
             "aik,bkj->abij", lhs, rhs,
@@ -92,7 +85,6 @@
     fb = send(db, dn)
 
     half = GROUP // 2
-    hk = half * rb
     pieces = [
         (y, 0, part_a), (y, 1, part_b),
         ((y - 1) % ny, 0, ua), ((y + 1) % ny, 0, da),
@@ -100,17 +92,26 @@
         ((y + 2) % ny, 0, fa), ((y + 2) % ny, 1, fb),
     ]
 
-    early = reorder(jnp.concatenate([own, q1], axis=1))
+    def kblk(g, m):
+        return (GROUP * g + (p ^ m)) * rb
+
+    early = jnp.concatenate([own, q1], axis=1)
     t_early = None
     for g, h, pc in pieces:
-        lhs = lax.dynamic_slice_in_dim(early, g * gw + h * hk, hk, axis=2)
+        lhs = jnp.concatenate(
+            [lax.dynamic_slice_in_dim(early, kblk(g, half * h + i), rb, axis=2) for i in range(half)],
+            axis=2,
+        )
         term = mm(lhs, pc)
         t_early = term if t_early is None else t_early + term
 
     right = jnp.zeros((2, n, cw), jnp.float32)
     for g, h, pc in pieces:
-        right = lax.dynamic_update_slice_in_dim(right, pc, g * gw + h * hk, axis=1)
-    late = reorder(jnp.concatenate([q2, q3], axis=1))
+        for i in range(half):
+            right = lax.dynamic_update_slice_in_dim(
+                right, pc[:, i * rb:(i + 1) * rb], kblk(g, half * h + i), axis=1
+            )
+    late = jnp.concatenate([q2, q3], axis=1)
     t_late = mm(late, right)
     t = jnp.concatenate([t_early, t_late], axis=2)
 

time: 258 us -> 208 us (0.81)
  local copies, waits for them, and re-layouts: 63.7 us -> 31.5 us
  matrix products: 43.8 us -> 28.8 us
  other arithmetic: 21.2 us -> 7.59 us
  waiting for transfers between devices: 73.9 us -> 85.7 us
    dot_general x9, matrix products: 33.5 us -> 18.6 us  [mm(): jnp.einsum('aik,bkj->abij', lhs, rhs, precision=lax.Precision.HIGH, prefe...]
    dynamic_slice x3 -> x1, local copies, waits for them, and re-layouts: 15.6 us -> 0.6 us  [on_device(): lax.dynamic_slice_in_dim(early, kblk(g, half * h + i), rb, axis=2)]
    concatenate x4 -> x0, other arithmetic: 13.3 us -> none  [the longest x2 6.8 us: reorder(): jnp.concatenate([lax.dynamic_slice_in_dim(l5, p ^ m, 1, axis=3) for m in...]
    ppermute x14, waiting for transfers between devices: 73.9 us -> 85.7 us  [send(): return lax.ppermute(x, 'blk', perm)]
    reshape x2 -> x0, local copies, waits for them, and re-layouts: 11.5 us -> none  [the longest x1 6.02 us: reorder(): l5 = r.reshape(2, r.shape[1], ny, GROUP, rb)]
    broadcast_in_dim x1, local copies, waits for them, and re-layouts: 1.06 us -> 4.35 us  [on_device(): right = jnp.zeros((2, n, cw), jnp.float32)]
    dynamic_update_slice x7 -> x14, local copies, waits for them, and re-layouts: 14.1 us -> 13.1 us  [on_device(): lax.dynamic_update_slice_in_dim(right, pc[:, i * rb:(i + 1) * rb], kblk(g...]
  transfers between devices with their start and end apart: 14 -> 14, of which waited for: 6 -> 8; matrix products, arithmetic and copies ran while one was open for 34% -> 16% of each run, Pallas kernels for 0% -> 0%
where the time goes in v5:
time: 208 us; the launch traced here: 207 us
  waiting for transfers between devices  85.7 us (41%)
  blocking collectives  35.6 us (17%)
  local copies, waits for them, and re-layouts  31.5 us (15%)
  matrix products  28.8 us (14%)
  starting transfers between devices  18 us (9%)
  other arithmetic  7.59 us (4%)
    ppermute x14, waiting for transfers between devices, send(): return lax.ppermute(x, 'blk', perm)  85.7 us
    all_to_all x1, blocking collectives, on_device(): lax.all_to_all(projected, 'freq', split_axis=1, concat_axis=3, tiled=True)  35.6 us
    dot_general x9, matrix products, mm(): jnp.einsum('aik,bkj->abij', lhs, rhs, precision=lax.Precision.HIGH, prefe...  18.6 us
    ppermute x14, starting transfers between devices, send(): return lax.ppermute(x, 'blk', perm)  18 us
    dynamic_update_slice x14, local copies, waits for them, and re-layouts, on_device(): lax.dynamic_update_slice_in_dim(right, pc[:, i * rb:(i + 1) * rb], kblk(g...  13.1 us
    dot_general x1, matrix products, on_device(): jnp.einsum('srt,tc->csr', traces, table, preferred_element_type=jnp.float32)  10.2 us
    broadcast_in_dim x1, local copies, waits for them, and re-layouts, on_device(): right = jnp.zeros((2, n, cw), jnp.float32)  4.35 us
  transfers between devices with their start and end apart: 14, of which 8 were waited for; matrix products, arithmetic and copies ran while one was open for 16% of the time, Pallas kernels for 0%

profile of v5, /device:TPU:1, one launch (start us, length us, event | category | flops | bytes accessed | tf_op | source)
XLA Modules:
  0.0 207.4 jit_solution(9707245145305940137)
XLA Ops:
  0.1 10.2 %convolution_bitcast_fusion = f32[2,8,128,256]{3,1,0,2:T(8,128)S(1)} fusion(bf16[128,256,256]{2,1,0:T(8,128)(2,1)} %param.2, bf16[256,8]{0,1:T(8,128)(2,1)S(1)} %get-tuple-element.49, bf16[256,8]{0,1:T(8,128)(2,1)S(1)} %get-tuple-element.48), kind=kOutput, calls=%fused_computation.21 | convolution fusion | flops 268451840 | bytes 18882560 | tf_op jit(solution)/shard_map/srt,tc->csr/dot_general | solution.py:43
  10.4 1.1 copy.10
  11.5 35.6 %all_to_all.15 = f32[2,8,128,256]{3,0,2,1:T(2,128)S(1)} all-to-all(f32[2,8,128,256]{3,0,2,1:T(2,128)S(1)} %copy.10), channel_id=1, replica_groups=mesh['freq'=8,'blk'=16] {'freq'}, dimensions={1} | all-to-all | bytes 4194304 | tf_op jit(solution)/shard_map/all_to_all | solution.py:45
  47.1 2.5 %copy.11 = f32[2,1,128,8,256]{4,3,2,0,1:T(8,128)} copy(f32[2,1,128,8,256]{4,0,2,3,1:T(2,128)S(1)} %bitcast.146) | data formatting | bytes 4194304 | tf_op jit(solution)/shard_map/all_to_all | solution.py:45
  49.6 1.7 squeeze.27
  51.3 1.8 collective-permute-start
  53.2 4.3 %broadcast_in_dim.11 = f32[2,2048,512]{2,1,0:T(8,128)} broadcast(f32[]{:T(128)} %constant.92.clone.1), dimensions={} | broadcast | bytes 8388612 | tf_op jit(solution)/shard_map/broadcast_in_dim | solution.py:108
  57.5 1.2 constant_dynamic-update-slice_fusion.4
  59.4 1.0 collective-permute-start.2
  60.4 1.2 pad_maximum_fusion.1
  61.6 10.4 %collective-permute-done.1 = f32[2,128,512]{2,1,0:T(8,128)S(1)} collective-permute-done((f32[2,128,512]{2,1,0:T(8,128)S(1)}, f32[2,128,512]{2,1,0:T(8,128)S(1)}, u32[]{:S(2)}, u32[]{:S(2)}) %collective-permute-start.1) | collective-permute-done | bytes 524320 | tf_op jit(solution)/shard_map/ppermute | solution.py:33
  72.1 11.5 %collective-permute-done.2 = f32[2,128,512]{2,1,0:T(8,128)S(1)} collective-permute-done((f32[2,128,512]{2,1,0:T(8,128)S(1)}, f32[2,128,512]{2,1,0:T(8,128)S(1)}, u32[]{:S(2)}, u32[]{:S(2)}) %collective-permute-start.2) | collective-permute-done | bytes 524320 | tf_op jit(solution)/shard_map/ppermute | solution.py:33
  85.0 2.0 constant_dynamic-update-slice_fusion.3
  87.1 1.4 collective-permute-start.3
  88.4 1.6 collective-permute-start.4
  90.3 1.0 constant_dynamic-update-slice_fusion.8
  91.3 0.9 constant_dynamic-update-slice_fusion.7
  92.2 2.7 %collective-permute-start.6 = (f32[2,256,512]{2,1,0:T(8,128)S(1)}, f32[2,256,512]{2,1,0:T(8,128)S(1)}, u32[]{:S(2)}, u32[]{:S(2)}) collective-permute-start(f32[2,256,512]{2,1,0:T(8,128)S(1)} %get-tuple-element.43), channel_id=1, source_target_pairs={{0,12},{1,13},{2,14},{3,15},{4,0},{5,1},{6,2},{7,3},{8,4},{9,5},{1... | collective-permute-start | bytes 3145736 | tf_op jit(solution)/shard_map/ppermute | solution.py:33
  94.9 24.8 %collective-permute-done.9 = f32[2,128,1536]{2,1,0:T(8,128)} collective-permute-done((f32[2,128,1536]{2,1,0:T(8,128)}, f32[2,128,1536]{2,1,0:T(8,128)}, u32[]{:S(2)}, u32[]{:S(2)}) %collective-permute-start.9) | collective-permute-done | bytes 1572896 | tf_op jit(solution)/shard_map/ppermute | solution.py:33
  119.7 1.1 slice_dynamic-update-slice_fusion.2
  120.8 1.1 slice_dynamic-update-slice_fusion.1
  121.9 1.1 slice_dynamic-update-slice_fusion
  123.0 1.3 collective-permute-start.10
  124.2 1.7 constant_dynamic-update-slice_fusion.5
  126.6 1.0 fusion.28
  127.6 1.0 fusion.30
  128.7 1.4 collective-permute-start.7
  133.3 2.0 collective-permute-done.5
  135.4 0.9 slice_dynamic-update-slice_fusion.10
  136.3 0.9 slice_dynamic-update-slice_fusion.9
  137.1 1.2 collective-permute-start.8
  138.4 1.0 fusion.20
  139.4 1.0 fusion.22
  140.4 0.8 slice_dynamic-update-slice_fusion.8
  141.3 1.0 fusion.24
  143.1 1.0 fusion.26
  144.1 13.7 %collective-permute-done.7 = f32[2,256,512]{2,1,0:T(8,128)S(1)} collective-permute-done((f32[2,256,512]{2,1,0:T(8,128)S(1)}, f32[2,256,512]{2,1,0:T(8,128)S(1)}, u32[]{:S(2)}, u32[]{:S(2)}) %collective-permute-start.7) | collective-permute-done | bytes 1048608 | tf_op jit(solution)/shard_map/ppermute | solution.py:33
  161.6 9.3 %fusion.4 = f32[2,2,256,512]{3,2,0,1:T(8,128)S(1)} fusion(f32[2,128,2048]{2,1,0:T(8,128)S(1)} %collective-permute-done.10, f32[2,128,2048]{2,1,0:T(8,128)S(1)} %slice_dynamic-update-slice_fusion, f32[2,2048,512]{2,1,0:T(8,128)} %slice_dynamic-update-slice_fusion.3), kind=kOutput, calls=%fused_computation.20 | convolution fusion | flops 6443499520 | bytes 14680064 | tf_op jit(solution)/shard_map/aik,bkj->abij/dot_general | solution.py:71
  170.9 1.0 fusion.18
  171.9 2.1 add_bitcast_fusion
  174.0 1.8 fusion.38
  175.7 1.4 fusion.34
  177.4 3.3 %collective-permute-start.13 = (f32[2,128,512]{2,1,0:T(8,128)S(1)}, f32[2,128,512]{2,1,0:T(8,128)S(1)}, u32[]{:S(2)}, u32[]{:S(2)}) collective-permute-start(f32[2,128,512]{2,1,0:T(8,128)S(1)} %get-tuple-element.36), channel_id=1, source_target_pairs={{0,3},{1,2},{2,1},{3,0},{4,7},{5,6},{6,5},{7,4},{8,11},{9,10},{10,... | collective-permute-start | bytes 1572872 | tf_op jit(solution)/shard_map/ppermute | solution.py:33
  180.7 0.9 collective-permute-start.12
  181.6 11.2 %collective-permute-done.13 = f32[2,128,512]{2,1,0:T(8,128)S(1)} collective-permute-done((f32[2,128,512]{2,1,0:T(8,128)S(1)}, f32[2,128,512]{2,1,0:T(8,128)S(1)}, u32[]{:S(2)}, u32[]{:S(2)}) %collective-permute-start.13) | collective-permute-done | bytes 524320 | tf_op jit(solution)/shard_map/ppermute | solution.py:33
  192.9 11.6 %collective-permute-done.12 = f32[2,128,512]{2,1,0:T(8,128)S(1)} collective-permute-done((f32[2,128,512]{2,1,0:T(8,128)S(1)}, f32[2,128,512]{2,1,0:T(8,128)S(1)}, u32[]{:S(2)}, u32[]{:S(2)}) %collective-permute-start.12) | collective-permute-done | bytes 524320 | tf_op jit(solution)/shard_map/ppermute | solution.py:33
  204.4 1.2 pad_maximum_fusion
  205.9 1.5 maximum_bitcast_fusion.2
  (35 shorter events, 11.6 us)
Async XLA Ops:
  51.3 33.7 %collective-permute-start = (f32[2,128,2048]{2,1,0:T(8,128)S(1)}, f32[2,128,2048]{2,1,0:T(8,128)}, u32[]{:S(2)}, u32[]{:S(2)}) collective-permute-start(f32[2,128,2048]{2,1,0:T(8,128)S(1)} %squeeze.27), channel_id=1, source_target_pairs={{0,1},{1,0},{2,3},{3,2},{4,5},{5,4},{6,7},{7,6},{8,9},{9,8},{10,11... | collective-permute-start | bytes 6291464 | tf_op jit(solution)/shard_map/ppermute | solution.py:33
  58.7 25.6 %copy-start.2 = (f32[1,2]{1,0:T(1,128)S(1)}, f32[1,2]{1,0:T(1,128)}, u32[]{:S(2)}) copy-start(f32[1,2]{1,0:T(1,128)} %param.3) | copy-start | bytes 28
  58.7 13.4 %collective-permute-start.1 = (f32[2,128,512]{2,1,0:T(8,128)S(1)}, f32[2,128,512]{2,1,0:T(8,128)S(1)}, u32[]{:S(2)}, u32[]{:S(2)}) collective-permute-start(f32[2,128,512]{2,1,0:T(8,128)S(1)} %get-tuple-element.42), channel_id=1, source_target_pairs={{0,2},{1,3},{2,0},{3,1},{4,6},{5,7},{6,4},{7,5},{8,10},{9,11},{10,... | collective-permute-start | bytes 1572872 | tf_op jit(solution)/shard_map/ppermute | solution.py:33
  59.4 24.1 %collective-permute-start.2 = (f32[2,128,512]{2,1,0:T(8,128)S(1)}, f32[2,128,512]{2,1,0:T(8,128)S(1)}, u32[]{:S(2)}, u32[]{:S(2)}) collective-permute-start(f32[2,128,512]{2,1,0:T(8,128)S(1)} %get-tuple-element.41), channel_id=1, source_target_pairs={{0,3},{1,2},{2,1},{3,0},{4,7},{5,6},{6,5},{7,4},{8,11},{9,10},{10,... | collective-permute-start | bytes 1572872 | tf_op jit(solution)/shard_map/ppermute | solution.py:33
  72.1 11.5 %copy-start = (f32[2,128,512]{2,1,0:T(8,128)}, f32[2,128,512]{2,1,0:T(8,128)S(1)}, u32[]{:S(2)}) copy-start(f32[2,128,512]{2,1,0:T(8,128)S(1)} %collective-permute-done.1) | copy-start | bytes 1572868
  83.6 36.1 %collective-permute-start.9 = (f32[2,128,1536]{2,1,0:T(8,128)}, f32[2,128,1536]{2,1,0:T(8,128)}, u32[]{:S(2)}, u32[]{:S(2)}) collective-permute-start(f32[2,128,1536]{2,1,0:T(8,128)} %pad_maximum_fusion.1), channel_id=1, source_target_pairs={{0,2},{1,3},{2,0},{3,1},{4,6},{5,7},{6,4},{7,5},{8,10},{9,11},{10,... | collective-permute-start | bytes 4718600 | tf_op jit(solution)/shard_map/ppermute | solution.py:33
  87.0 3.3 %copy-start.1 = (f32[2,128,512]{2,1,0:T(8,128)S(1)}, f32[2,128,512]{2,1,0:T(8,128)}, u32[]{:S(2)}) copy-start(f32[2,128,512]{2,1,0:T(8,128)} %copy-done) | copy-start | bytes 1572868
  87.1 41.6 %collective-permute-start.3 = (f32[2,256,512]{2,1,0:T(8,128)S(1)}, f32[2,256,512]{2,1,0:T(8,128)S(1)}, u32[]{:S(2)}, u32[]{:S(2)}) collective-permute-start(f32[2,256,512]{2,1,0:T(8,128)S(1)} %pad_maximum_fusion.3), channel_id=1, source_target_pairs={{0,4},{1,5},{2,6},{3,7},{4,8},{5,9},{6,10},{7,11},{8,12},{9,13},{1... | collective-permute-start | bytes 3145736 | tf_op jit(solution)/shard_map/ppermute | solution.py:33
  88.4 43.2 %collective-permute-start.4 = (f32[2,256,512]{2,1,0:T(8,128)S(1)}, f32[2,256,512]{2,1,0:T(8,128)S(1)}, u32[]{:S(2)}, u32[]{:S(2)}) collective-permute-start(f32[2,256,512]{2,1,0:T(8,128)S(1)} %pad_maximum_fusion.3), channel_id=1, source_target_pairs={{0,12},{1,13},{2,14},{3,15},{4,0},{5,1},{6,2},{7,3},{8,4},{9,5},{1... | collective-permute-start | bytes 3145736 | tf_op jit(solution)/shard_map/ppermute | solution.py:33
  92.2 43.2 %collective-permute-start.5 = (f32[2,256,512]{2,1,0:T(8,128)S(1)}, f32[2,256,512]{2,1,0:T(8,128)S(1)}, u32[]{:S(2)}, u32[]{:S(2)}) collective-permute-start(f32[2,256,512]{2,1,0:T(8,128)S(1)} %get-tuple-element.43), channel_id=1, source_target_pairs={{0,4},{1,5},{2,6},{3,7},{4,8},{5,9},{6,10},{7,11},{8,12},{9,13},{1... | collective-permute-start | bytes 3145736 | tf_op jit(solution)/shard_map/ppermute | solution.py:33
  92.2 44.9 %collective-permute-start.6 = (f32[2,256,512]{2,1,0:T(8,128)S(1)}, f32[2,256,512]{2,1,0:T(8,128)S(1)}, u32[]{:S(2)}, u32[]{:S(2)}) collective-permute-start(f32[2,256,512]{2,1,0:T(8,128)S(1)} %get-tuple-element.43), channel_id=1, source_target_pairs={{0,12},{1,13},{2,14},{3,15},{4,0},{5,1},{6,2},{7,3},{8,4},{9,5},{1... | collective-permute-start | bytes 3145736 | tf_op jit(solution)/shard_map/ppermute | solution.py:33
  123.0 38.6 %collective-permute-start.10 = (f32[2,128,2048]{2,1,0:T(8,128)S(1)}, f32[2,128,2048]{2,1,0:T(8,128)S(1)}, u32[]{:S(2)}, u32[]{:S(2)}) collective-permute-start(f32[2,128,2048]{2,1,0:T(8,128)S(1)} %slice_dynamic-update-slice_fusion), channel_id=1, source_target_pairs={{0,1},{1,0},{2,3},{3,2},{4,5},{5,4},{6,7},{7,6},{8,9},{9,8},{10,11... | collective-permute-start | bytes 6291464 | tf_op jit(solution)/shard_map/ppermute | solution.py:33
  128.7 29.2 %collective-permute-start.7 = (f32[2,256,512]{2,1,0:T(8,128)S(1)}, f32[2,256,512]{2,1,0:T(8,128)S(1)}, u32[]{:S(2)}, u32[]{:S(2)}) collective-permute-start(f32[2,256,512]{2,1,0:T(8,128)S(1)} %collective-permute-done.3), channel_id=1, source_target_pairs={{0,4},{1,5},{2,6},{3,7},{4,8},{5,9},{6,10},{7,11},{8,12},{9,13},{1... | collective-permute-start | bytes 3145736 | tf_op jit(solution)/shard_map/ppermute | solution.py:33
  137.1 22.8 %collective-permute-start.8 = (f32[2,256,512]{2,1,0:T(8,128)S(1)}, f32[2,256,512]{2,1,0:T(8,128)S(1)}, u32[]{:S(2)}, u32[]{:S(2)}) collective-permute-start(f32[2,256,512]{2,1,0:T(8,128)S(1)} %collective-permute-done.6), channel_id=1, source_target_pairs={{0,12},{1,13},{2,14},{3,15},{4,0},{5,1},{6,2},{7,3},{8,4},{9,5},{1... | collective-permute-start | bytes 3145736 | tf_op jit(solution)/shard_map/ppermute | solution.py:33
  177.4 15.5 %collective-permute-start.13 = (f32[2,128,512]{2,1,0:T(8,128)S(1)}, f32[2,128,512]{2,1,0:T(8,128)S(1)}, u32[]{:S(2)}, u32[]{:S(2)}) collective-permute-start(f32[2,128,512]{2,1,0:T(8,128)S(1)} %get-tuple-element.36), channel_id=1, source_target_pairs={{0,3},{1,2},{2,1},{3,0},{4,7},{5,6},{6,5},{7,4},{8,11},{9,10},{10,... | collective-permute-start | bytes 1572872 | tf_op jit(solution)/shard_map/ppermute | solution.py:33
  180.7 23.7 %collective-permute-start.12 = (f32[2,128,512]{2,1,0:T(8,128)S(1)}, f32[2,128,512]{2,1,0:T(8,128)S(1)}, u32[]{:S(2)}, u32[]{:S(2)}) collective-permute-start(f32[2,128,512]{2,1,0:T(8,128)S(1)} %get-tuple-element.37), channel_id=1, source_target_pairs={{0,2},{1,3},{2,0},{3,1},{4,6},{5,7},{6,4},{7,5},{8,10},{9,11},{10,... | collective-permute-start | bytes 1572872 | tf_op jit(solution)/shard_map/ppermute | solution.py:33
  181.6 22.8 %collective-permute-start.11 = (f32[2,128,512]{2,1,0:T(8,128)S(1)}, f32[2,128,512]{2,1,0:T(8,128)}, u32[]{:S(2)}, u32[]{:S(2)}) collective-permute-start(f32[2,128,512]{2,1,0:T(8,128)S(1)} %get-tuple-element.35), channel_id=1, source_target_pairs={{0,1},{1,0},{2,3},{3,2},{4,5},{5,4},{6,7},{7,6},{8,9},{9,8},{10,11... | collective-permute-start | bytes 1572872 | tf_op jit(solution)/shard_map/ppermute | solution.py:33

commit v6 on v5

--- a/solution.py
+++ b/solution.py
@@ -58,14 +58,24 @@
     q1 = send(own, xor_perm(nblk, 1))
     c2 = send(cols(own, p ^ 2), xor_perm(nblk, 2))
     c3 = send(cols(own, p ^ 3), xor_perm(nblk, 3))
-    rest = jnp.concatenate([cols(own, p ^ 2 ^ m) for m in range(1, GROUP)], axis=2)
+    rest = jnp.concatenate([cols(own, p), cols(own, p ^ 1)], axis=2)
     rest, _, _ = lax.optimization_barrier((rest, c2, c3))
     rest = send(rest, xor_perm(nblk, 2))
-    q2 = jnp.zeros_like(own)
-    q2 = lax.dynamic_update_slice_in_dim(q2, c2, p * cw, axis=2)
-    for m in range(1, GROUP):
-        q2 = lax.dynamic_update_slice_in_dim(q2, rest[:, :, (m - 1) * cw:m * cw], (p ^ m) * cw, axis=2)
-    q3 = send(q2, xor_perm(nblk, 1))
+    r_c = send(jnp.concatenate([c2, c3], axis=2), xor_perm(nblk, 1))
+    r_rest = send(rest, xor_perm(nblk, 1))
+
+    def assemble(blocks):
+        out = jnp.zeros_like(own)
+        for m, blk in blocks:
+            out = lax.dynamic_update_slice_in_dim(out, blk, (p ^ m) * cw, axis=2)
+        return out
+
+    q2 = assemble([
+        (0, c2), (1, r_c[:, :, cw:]), (2, rest[:, :, :cw]), (3, rest[:, :, cw:]),
+    ])
+    q3 = assemble([
+        (0, c3), (1, r_c[:, :, :cw]), (3, r_rest[:, :, :cw]), (2, r_rest[:, :, cw:]),
+    ])
 
     def mm(lhs, rhs):
         return jnp.einsum(
@@ -111,23 +121,23 @@
             right = lax.dynamic_update_slice_in_dim(
                 right, pc[:, i * rb:(i + 1) * rb], kblk(g, half * h + i), axis=1
             )
-    late = jnp.concatenate([q2, q3], axis=1)
-    t_late = mm(late, right)
-    t = jnp.concatenate([t_early, t_late], axis=2)
-
-    prod_re = t[0, 0] - t[1, 1]
-    prod_im = t[0, 1] + t[1, 0]
     scale = 1.0 / math.sqrt(n)
     w_re = signature[0, 0]
     w_im = signature[0, 1]
-    out_re = -(w_re * prod_re - w_im * prod_im) * scale
-    out_im = -(w_re * prod_im + w_im * prod_re) * scale
-    blk_out = jnp.stack([out_re, out_im], axis=0)
 
-    parts = [blk_out[:, :rb]]
-    for m in range(1, GROUP):
-        parts.append(send(blk_out[:, m * rb:(m + 1) * rb], xor_perm(nblk, m)))
-    stacked = jnp.stack(parts, axis=0)
+    def finish(t):
+        prod_re = t[0, 0] - t[1, 1]
+        prod_im = t[0, 1] + t[1, 0]
+        out_re = -(w_re * prod_re - w_im * prod_im) * scale
+        out_im = -(w_re * prod_im + w_im * prod_re) * scale
+        return jnp.stack([out_re, out_im], axis=0)
+
+    out_early = finish(t_early)
+    out_2 = send(finish(mm(q2, right)), xor_perm(nblk, 2))
+    out_3 = send(finish(mm(q3, right)), xor_perm(nblk, 3))
+    out_1 = send(out_early[:, rb:], xor_perm(nblk, 1))
+
+    stacked = jnp.stack([out_early[:, :rb], out_1, out_2, out_3], axis=0)
     ordered = [lax.dynamic_index_in_dim(stacked, p ^ i, 0, keepdims=False) for i in range(GROUP)]
     out = jnp.concatenate(ordered, axis=2)
     return out[None]

time: 208 us -> 266 us (1.28)
  local copies, waits for them, and re-layouts: 31.5 us -> 83.7 us
  blocking collectives: 35.6 us -> 0 us
  matrix products: 28.8 us -> 49.2 us
  waiting for transfers between devices: 85.7 us -> 95.6 us
  starting transfers between devices: 18 us -> 24.7 us
  other arithmetic: 7.59 us -> 11.3 us
    all_to_all x1 -> x0, blocking collectives: 35.6 us -> none  [on_device(): lax.all_to_all(projected, 'freq', split_axis=1, concat_axis=3, tiled=True)]
    all_to_all x0 -> x1, waiting for transfers between devices: none -> 28.6 us  [on_device(): lax.all_to_all(projected, 'freq', split_axis=1, concat_axis=3, tiled=True)]
    slice x0 -> x18, local copies, waits for them, and re-layouts: none -> 27 us  [on_device(): pc[:, i * rb:(i + 1) * rb]]
    dot_general x9 -> x10, matrix products: 18.6 us -> 38.9 us  [mm(): jnp.einsum('aik,bkj->abij', lhs, rhs, precision=lax.Precision.HIGH, prefe...]
    ppermute x14 -> x15, waiting for transfers between devices: 85.7 us -> 67 us  [send(): return lax.ppermute(x, 'blk', perm)]
    all_to_all x0 -> x1, starting transfers between devices: none -> 8.15 us  [on_device(): lax.all_to_all(projected, 'freq', split_axis=1, concat_axis=3, tiled=True)]
    dynamic_update_slice x3 -> x6, local copies, waits for them, and re-layouts: 3.25 us -> 10.8 us  [assemble(): out = lax.dynamic_update_slice_in_dim(out, blk, (p ^ m) * cw, axis=2)]
    dynamic_slice x0 -> x9, local copies, waits for them, and re-layouts: none -> 5.07 us  [the longest x4 4.12 us: cols(): return lax.dynamic_slice_in_dim(x, i * cw, cw, axis=2)]
  transfers between devices with their start and end apart: 14 -> 16, of which waited for: 8 -> 7; matrix products, arithmetic and copies ran while one was open for 16% -> 38% of each run, Pallas kernels for 0% -> 0%
where the time goes in v6:
time: 266 us; the launch traced here: 265 us
  waiting for transfers between devices  95.6 us (36%)
  local copies, waits for them, and re-layouts  83.7 us (31%)
  matrix products  49.2 us (18%)
  starting transfers between devices  24.7 us (9%)
  other arithmetic  11.3 us (4%)
    ppermute x15, waiting for transfers between devices, send(): return lax.ppermute(x, 'blk', perm)  67 us
    dot_general x10, matrix products, mm(): jnp.einsum('aik,bkj->abij', lhs, rhs, precision=lax.Precision.HIGH, prefe...  38.9 us
    all_to_all x1, waiting for transfers between devices, on_device(): lax.all_to_all(projected, 'freq', split_axis=1, concat_axis=3, tiled=True)  28.6 us
    slice x18, local copies, waits for them, and re-layouts, on_device(): pc[:, i * rb:(i + 1) * rb]  27 us
    ppermute x15, starting transfers between devices, send(): return lax.ppermute(x, 'blk', perm)  16.5 us
    dynamic_update_slice x16, local copies, waits for them, and re-layouts, on_device(): lax.dynamic_update_slice_in_dim(right, pc[:, i * rb:(i + 1) * rb], kblk(g...  15.3 us
    dynamic_update_slice x6, local copies, waits for them, and re-layouts, assemble(): out = lax.dynamic_update_slice_in_dim(out, blk, (p ^ m) * cw, axis=2)  10.8 us
    dot_general x1, matrix products, on_device(): jnp.einsum('srt,tc->csr', traces, table, preferred_element_type=jnp.float32)  10.2 us
  transfers between devices with their start and end apart: 16, of which 7 were waited for; matrix products, arithmetic and copies ran while one was open for 38% of the time, Pallas kernels for 0%

profile of v6, /device:TPU:1, one launch (start us, length us, event | category | flops | bytes accessed | tf_op | source)
XLA Modules:
  0.0 264.9 jit_solution(5178939772595294454)
XLA Ops:
  0.1 10.2 %convolution_bitcast_fusion = f32[2,8,128,256]{3,1,0,2:T(8,128)S(1)} fusion(bf16[128,256,256]{2,1,0:T(8,128)(2,1)} %param.2, bf16[256,8]{0,1:T(8,128)(2,1)S(1)} %get-tuple-element.56, bf16[256,8]{0,1:T(8,128)(2,1)S(1)} %get-tuple-element.55), kind=kOutput, calls=%fused_computation.9 | convolution fusion | flops 268451840 | bytes 18882560 | tf_op jit(solution)/shard_map/srt,tc->csr/dot_general | solution.py:43
  10.4 2.4 copy.73
  12.8 8.2 %all-to-all-start = ((f32[2,8,128,256]{3,0,2,1:T(2,128)}), f32[2,8,128,256]{3,0,2,1:T(2,128)S(1)}, u32[]{:S(2)}, u32[]{:S(2)}) async-start(f32[2,8,128,256]{3,0,2,1:T(2,128)} %copy.73), calls=%async_computation | async-start | bytes 4194304 | tf_op jit(solution)/shard_map/all_to_all | solution.py:45
  20.9 28.6 %all-to-all-done = f32[2,8,128,256]{3,0,2,1:T(2,128)S(1)} async-done(((f32[2,8,128,256]{3,0,2,1:T(2,128)}), f32[2,8,128,256]{3,0,2,1:T(2,128)S(1)}, u32[]{:S(2)}, u32[]{:S(2)}) %all-to-all-start) | async-done | bytes 2097184 | tf_op jit(solution)/shard_map/all_to_all | solution.py:45
  49.5 2.5 copy.74
  52.1 1.7 squeeze.35
  55.6 1.7 collective-permute-start.2
  57.3 10.3 %collective-permute-done.1 = f32[2,128,512]{2,1,0:T(8,128)S(1)} collective-permute-done((f32[2,128,512]{2,1,0:T(8,128)S(1)}, f32[2,128,512]{2,1,0:T(8,128)S(1)}, u32[]{:S(2)}, u32[]{:S(2)}) %collective-permute-start.1) | collective-permute-done | bytes 524320 | tf_op jit(solution)/shard_map/ppermute | solution.py:33
  68.7 11.0 %collective-permute-done.2 = f32[2,128,512]{2,1,0:T(8,128)S(1)} collective-permute-done((f32[2,128,512]{2,1,0:T(8,128)S(1)}, f32[2,128,512]{2,1,0:T(8,128)S(1)}, u32[]{:S(2)}, u32[]{:S(2)}) %collective-permute-start.2) | collective-permute-done | bytes 524320 | tf_op jit(solution)/shard_map/ppermute | solution.py:33
  82.1 2.7 %collective-permute-start.6 = (f32[2,256,512]{2,1,0:T(8,128)}, f32[2,256,512]{2,1,0:T(8,128)}, u32[]{:S(2)}, u32[]{:S(2)}) collective-permute-start(f32[2,256,512]{2,1,0:T(8,128)} %get-tuple-element.53), channel_id=1, source_target_pairs={{0,12},{1,13},{2,14},{3,15},{4,0},{5,1},{6,2},{7,3},{8,4},{9,5},{1... | collective-permute-start | bytes 3145736 | tf_op jit(solution)/shard_map/ppermute | solution.py:33
  85.0 2.2 pad_maximum_fusion.3
  91.3 4.4 %broadcast_in_dim.8 = f32[2,2048,512]{1,2,0:T(8,128)} broadcast(f32[]{:T(128)} %constant.94.clone.1), dimensions={} | broadcast | bytes 8388612 | tf_op jit(solution)/shard_map/broadcast_in_dim | solution.py:118
  97.9 2.1 copy.92
  101.1 7.0 %collective-permute-done.6 = f32[2,256,512]{2,1,0:T(8,128)} collective-permute-done((f32[2,256,512]{2,1,0:T(8,128)}, f32[2,256,512]{2,1,0:T(8,128)}, u32[]{:S(2)}, u32[]{:S(2)}) %collective-permute-start.6) | collective-permute-done | bytes 1048608 | tf_op jit(solution)/shard_map/ppermute | solution.py:33
  108.1 2.1 fusion.79
  110.2 2.1 copy.100
  113.3 2.1 fusion.80
  115.4 2.0 copy.98
  118.4 3.3 %collective-permute-start.8 = (f32[2,256,512]{2,1,0:T(8,128)}, f32[2,256,512]{2,1,0:T(8,128)}, u32[]{:S(2)}, u32[]{:S(2)}) collective-permute-start(f32[2,256,512]{2,1,0:T(8,128)} %collective-permute-done.6), channel_id=1, source_target_pairs={{0,12},{1,13},{2,14},{3,15},{4,0},{5,1},{6,2},{7,3},{8,4},{9,5},{1... | collective-permute-start | bytes 3145736 | tf_op jit(solution)/shard_map/ppermute | solution.py:33
  122.4 2.3 slice_dynamic-update-slice_fusion.5
  124.7 1.9 slice_dynamic-update-slice_fusion.4
  126.5 1.9 slice_dynamic-update-slice_fusion.3
  131.5 2.7 %collective-permute-start.4 = (f32[2,256,512]{2,1,0:T(8,128)}, f32[2,256,512]{2,1,0:T(8,128)}, u32[]{:S(2)}, u32[]{:S(2)}) collective-permute-start(f32[2,256,512]{2,1,0:T(8,128)} %pad_maximum_fusion.1), channel_id=1, source_target_pairs={{0,12},{1,13},{2,14},{3,15},{4,0},{5,1},{6,2},{7,3},{8,4},{9,5},{1... | collective-permute-start | bytes 3145736 | tf_op jit(solution)/shard_map/ppermute | solution.py:33
  134.2 3.2 %constant_dynamic-update-slice_fusion.18 = f32[2,256,2048]{2,1,0:T(8,128)} fusion(f32[2,256,2048]{2,1,0:T(8,128)} %constant_dynamic-update-slice_fusion.19, f32[2,128,2048]{2,1,0:T(8,128)} %collective-permute-done), kind=kLoop, calls=%fused_computation.135 | loop fusion | bytes 4194304 | tf_op jit(solution)/shard_map/concatenate | solution.py:108
  137.4 3.5 %constant_dynamic-slice_fusion.6 = (f32[2,256,128]{2,1,0:T(8,128)S(1)}, f32[2,256,128]{2,1,0:T(8,128)}, f32[2,256,128]{2,1,0:T(8,128)}, f32[2,256,128]{2,1,0:T(8...) fusion(f32[2,256,2048]{2,1,0:T(8,128)} %constant_dynamic-update, ...), kind=kLoop, calls=%fused_computation.113 | loop fusion | bytes 8388672 | tf_op jit(solution)/shard_map/dynamic_slice | solution.py:112
  140.9 3.0 %fusion.30 = f32[2,512,2,256]{3,1,2,0:T(8,128)S(1)} fusion(f32[2,256,512]{2,1,0:T(8,128)} %get-tuple-element.53, f32[2,256,128]{2,1,0:T(8,128)S(1)} %get-tuple-element.19, f32[2,256,128]{2,1,0:T(8,128)S(1)} %get-tuple-element.20), kind=kOutput, calls=%fused_computation.29 | convolution fusion | flops 805437440 | bytes 3670016 | tf_op jit(solution)/shard_map/aik,bkj->abij/dot_general | solution.py:81
  143.9 4.4 %fusion.22 = f32[2,512,2,256]{3,1,2,0:T(8,128)} fusion(f32[2,256,512]{2,1,0:T(8,128)} %collective-permute-done.6, f32[2,256,128]{2,1,0:T(8,128)S(1)} %get-tuple-element.11, f32[2,256,128]{2,1,0:T(8,128)S(1)} %get-tuple-element.12), kind=kOutput, calls=%fused_computation.21 | convolution fusion | flops 805437440 | bytes 3670016 | tf_op jit(solution)/shard_map/aik,bkj->abij/dot_general | solution.py:81
  150.1 4.4 %fusion.24 = f32[2,512,2,256]{3,1,2,0:T(8,128)} fusion(f32[2,256,512]{2,1,0:T(8,128)} %collective-permute-done.5, f32[2,256,128]{2,1,0:T(8,128)S(1)} %get-tuple-element.13, f32[2,256,128]{2,1,0:T(8,128)S(1)} %get-tuple-element.14), kind=kOutput, calls=%fused_computation.23 | convolution fusion | flops 805437440 | bytes 3670016 | tf_op jit(solution)/shard_map/aik,bkj->abij/dot_general | solution.py:81
  154.5 3.1 %fusion.32 = f32[2,512,2,256]{3,1,2,0:T(8,128)} fusion(f32[2,256,128]{2,1,0:T(8,128)S(1)} %get-tuple-element.21, f32[2,256,128]{2,1,0:T(8,128)S(1)} %get-tuple-element.22, f32[2,128,512]{2,1,0:T(8,128)S(1)} %constant_dynamic-slice_fusion.23, f32[2,128,512]{2,1,0:T(8,128)S(1)} %get-tuple-element.27), kind=kOutput, calls=%fused_computation.31 | convolution fusion | flops 805699584 | bytes 3670016 | tf_op jit(solution)/shard_map/aik,bkj->abij/dot_general | solution.py:81
  158.5 2.1 fusion.77
  162.8 1.9 slice_dynamic-update-slice_fusion.1
  164.7 1.9 slice_dynamic-update-slice_fusion
  166.6 2.3 fusion.82
  170.1 2.1 copy.93
  172.2 2.3 fusion.81
  174.4 2.1 copy.96
  176.5 2.0 copy.95
  178.6 2.0 constant_dynamic-update-slice_fusion.13
  186.9 3.1 %fusion.26 = f32[2,512,2,256]{3,1,2,0:T(8,128)S(1)} fusion(f32[2,256,512]{2,1,0:T(8,128)} %collective-permute-done.4, f32[2,256,128]{2,1,0:T(8,128)S(1)} %copy-done.26, f32[2,256,128]{2,1,0:T(8,128)S(1)} %copy-done.27), kind=kOutput, calls=%fused_computation.25 | convolution fusion | flops 805437440 | bytes 3670016 | tf_op jit(solution)/shard_map/aik,bkj->abij/dot_general | solution.py:81
  190.0 3.2 %fusion.28 = f32[2,512,2,256]{3,1,2,0:T(8,128)S(1)} fusion(f32[2,256,512]{2,1,0:T(8,128)} %collective-permute-done.3, f32[2,256,128]{2,1,0:T(8,128)S(1)} %copy-done.24, f32[2,256,128]{2,1,0:T(8,128)S(1)} %copy-done.25), kind=kOutput, calls=%fused_computation.27 | convolution fusion | flops 805437440 | bytes 3670016 | tf_op jit(solution)/shard_map/aik,bkj->abij/dot_general | solution.py:81
  193.3 15.6 %collective-permute-done.7 = f32[2,256,512]{2,1,0:T(8,128)S(1)} collective-permute-done((f32[2,256,512]{2,1,0:T(8,128)}, f32[2,256,512]{2,1,0:T(8,128)S(1)}, u32[]{:S(2)}, u32[]{:S(2)}) %collective-permute-start.7) | collective-permute-done | bytes 1048608 | tf_op jit(solution)/shard_map/ppermute | solution.py:33
  208.9 1.8 fusion.20
  210.7 3.7 %add_bitcast_fusion = f32[2,2,256,512]{2,3,0,1:T(8,128)S(1)} fusion(f32[2,512,2,256]{3,1,2,0:T(8,128)S(1)} %fusion.20, f32[2,512,2,256]{3,1,2,0:T(8,128)S(1)} %copy-done, f32[2,512,2,256]{3,1,2,0:T(8,128)S(1)} %copy-done.1, f32[2,512,2,256]{3,1,2,0:T(8,128)S(1)} %fusion.26, f32[2,512,2,256]{3,1,2,0:T(8,128)S(1)} %fusion.28, ...), kind=kOutput, calls=%fused_computation.8 | convolution fusion | flops 809107456 | bytes 18350080 | tf_op jit(solution)/shard_map/aik,bkj->abij/dot_general | solution.py:81
  223.8 6.1 %fusion.11 = f32[2,2,128,512]{2,3,1,0:T(8,128)S(1)} fusion(f32[2,128,2048]{2,1,0:T(8,128)S(1)} %copy-done.4, f32[2,2048,512]{1,2,0:T(8,128)} %constant_dynamic-update-slice_fusion.2), kind=kOutput, calls=%fused_computation.11 | convolution fusion | flops 3221225472 | bytes 11534336 | tf_op jit(solution)/shard_map/aik,bkj->abij/dot_general | solution.py:81
  229.9 5.9 %fusion.6 = f32[2,2,128,512]{2,3,1,0:T(8,128)S(1)} fusion(f32[2,128,2048]{2,1,0:T(8,128)S(1)} %copy-done.6, f32[2,2048,512]{1,2,0:T(8,128)} %constant_dynamic-update-slice_fusion.2), kind=kOutput, calls=%fused_computation.10 | convolution fusion | flops 3221225472 | bytes 11534336 | tf_op jit(solution)/shard_map/aik,bkj->abij/dot_general | solution.py:81
  239.1 11.7 %collective-permute-done.12 = f32[2,128,512]{1,2,0:T(8,128)S(1)} collective-permute-done((f32[2,128,512]{1,2,0:T(8,128)S(1)}, f32[2,128,512]{1,2,0:T(8,128)S(1)}, u32[]{:S(2)}, u32[]{:S(2)}) %collective-permute-start.12) | collective-permute-done | bytes 524320 | tf_op jit(solution)/shard_map/ppermute | solution.py:33
  250.8 11.4 %collective-permute-done.14 = f32[2,128,512]{1,2,0:T(8,128)S(1)} collective-permute-done((f32[2,128,512]{1,2,0:T(8,128)S(1)}, f32[2,128,512]{1,2,0:T(8,128)S(1)}, u32[]{:S(2)}, u32[]{:S(2)}) %collective-permute-start.14) | collective-permute-done | bytes 524320 | tf_op jit(solution)/shard_map/ppermute | solution.py:33
  263.4 1.5 maximum_bitcast_fusion
  (128 shorter events, 44.8 us)
Async XLA Ops:
  12.8 36.8 %all-to-all-start = ((f32[2,8,128,256]{3,0,2,1:T(2,128)}), f32[2,8,128,256]{3,0,2,1:T(2,128)S(1)}, u32[]{:S(2)}, u32[]{:S(2)}) async-start(f32[2,8,128,256]{3,0,2,1:T(2,128)} %copy.73), calls=%async_computation | async-start | bytes 4194304 | tf_op jit(solution)/shard_map/all_to_all | solution.py:45
  54.8 12.7 %collective-permute-start.1 = (f32[2,128,512]{2,1,0:T(8,128)S(1)}, f32[2,128,512]{2,1,0:T(8,128)S(1)}, u32[]{:S(2)}, u32[]{:S(2)}) collective-permute-start(f32[2,128,512]{2,1,0:T(8,128)S(1)} %get-tuple-element.30), channel_id=1, source_target_pairs={{0,2},{1,3},{2,0},{3,1},{4,6},{5,7},{6,4},{7,5},{8,10},{9,11},{10,... | collective-permute-start | bytes 1572872 | tf_op jit(solution)/shard_map/ppermute | solution.py:33
  55.6 24.1 %collective-permute-start.2 = (f32[2,128,512]{2,1,0:T(8,128)S(1)}, f32[2,128,512]{2,1,0:T(8,128)S(1)}, u32[]{:S(2)}, u32[]{:S(2)}) collective-permute-start(f32[2,128,512]{2,1,0:T(8,128)S(1)} %get-tuple-element.29), channel_id=1, source_target_pairs={{0,3},{1,2},{2,1},{3,0},{4,7},{5,6},{6,5},{7,4},{8,11},{9,10},{10,... | collective-permute-start | bytes 1572872 | tf_op jit(solution)/shard_map/ppermute | solution.py:33
  68.7 11.0 %copy-start.5 = (f32[2,128,2048]{2,1,0:T(8,128)}, f32[2,128,2048]{2,1,0:T(8,128)S(1)}, u32[]{:S(2)}) copy-start(f32[2,128,2048]{2,1,0:T(8,128)S(1)} %get-tuple-element.51) | copy-start | bytes 6291460
  79.7 5.2 %copy-start.7 = (f32[2,128,512]{2,1,0:T(8,128)}, f32[2,128,512]{2,1,0:T(8,128)S(1)}, u32[]{:S(2)}) copy-start(f32[2,128,512]{2,1,0:T(8,128)S(1)} %collective-permute-done.2) | copy-start | bytes 1572868
  80.8 1.3 copy-start.3
  82.1 25.9 %collective-permute-start.6 = (f32[2,256,512]{2,1,0:T(8,128)}, f32[2,256,512]{2,1,0:T(8,128)}, u32[]{:S(2)}, u32[]{:S(2)}) collective-permute-start(f32[2,256,512]{2,1,0:T(8,128)} %get-tuple-element.53), channel_id=1, source_target_pairs={{0,12},{1,13},{2,14},{3,15},{4,0},{5,1},{6,2},{7,3},{8,4},{9,5},{1... | collective-permute-start | bytes 3145736 | tf_op jit(solution)/shard_map/ppermute | solution.py:33
  84.9 43.5 %collective-permute-start = (f32[2,128,2048]{2,1,0:T(8,128)S(1)}, f32[2,128,2048]{2,1,0:T(8,128)}, u32[]{:S(2)}, u32[]{:S(2)}) collective-permute-start(f32[2,128,2048]{2,1,0:T(8,128)S(1)} %squeeze.35), channel_id=1, source_target_pairs={{0,1},{1,0},{2,3},{3,2},{4,5},{5,4},{6,7},{7,6},{8,9},{9,8},{10,11... | collective-permute-start | bytes 6291464 | tf_op jit(solution)/shard_map/ppermute | solution.py:33
  84.9 3.0 %copy-start.8 = (f32[2,128,512]{2,1,0:T(8,128)S(1)}, f32[2,128,512]{2,1,0:T(8,128)}, u32[]{:S(2)}) copy-start(f32[2,128,512]{2,1,0:T(8,128)} %copy-done.7) | copy-start | bytes 1572868
  84.9 28.4 %collective-permute-start.5 = (f32[2,256,512]{2,1,0:T(8,128)}, f32[2,256,512]{2,1,0:T(8,128)}, u32[]{:S(2)}, u32[]{:S(2)}) collective-permute-start(f32[2,256,512]{2,1,0:T(8,128)} %get-tuple-element.53), channel_id=1, source_target_pairs={{0,4},{1,5},{2,6},{3,7},{4,8},{5,9},{6,10},{7,11},{8,12},{9,13},{1... | collective-permute-start | bytes 3145736 | tf_op jit(solution)/shard_map/ppermute | solution.py:33
  85.0 4.7 %copy-start.28 = (f32[1,2]{1,0:T(1,128)S(1)}, f32[1,2]{1,0:T(1,128)}, u32[]{:S(2)}) copy-start(f32[1,2]{1,0:T(1,128)} %param.3) | copy-start | bytes 28
  87.2 34.5 %collective-permute-start.11 = (f32[2,128,1024]{2,1,0:T(8,128)}, f32[2,128,1024]{2,1,0:T(8,128)}, u32[]{:S(2)}, u32[]{:S(2)}) collective-permute-start(f32[2,128,1024]{2,1,0:T(8,128)} %pad_maximum_fusion.3), channel_id=1, source_target_pairs={{0,2},{1,3},{2,0},{3,1},{4,6},{5,7},{6,4},{7,5},{8,10},{9,11},{10,... | collective-permute-start | bytes 3145736 | tf_op jit(solution)/shard_map/ppermute | solution.py:33
  89.0 33.4 %collective-permute-start.10 = (f32[2,128,1024]{2,1,0:T(8,128)}, f32[2,128,1024]{2,1,0:T(8,128)}, u32[]{:S(2)}, u32[]{:S(2)}) collective-permute-start(f32[2,128,1024]{2,1,0:T(8,128)} %pad_maximum_fusion.2), channel_id=1, source_target_pairs={{0,1},{1,0},{2,3},{3,2},{4,5},{5,4},{6,7},{7,6},{8,9},{9,8},{10,11... | collective-permute-start | bytes 3145736 | tf_op jit(solution)/shard_map/ppermute | solution.py:33
  91.3 4.4 %copy-start.19 = (f32[2,128,512]{1,2,0:T(8,128)S(1)}, f32[2,128,512]{1,2,0:T(8,128)}, u32[]{:S(2)}) copy-start(f32[2,128,512]{1,2,0:T(8,128)} %copy.89) | copy-start | bytes 1572868
  118.4 40.1 %collective-permute-start.8 = (f32[2,256,512]{2,1,0:T(8,128)}, f32[2,256,512]{2,1,0:T(8,128)}, u32[]{:S(2)}, u32[]{:S(2)}) collective-permute-start(f32[2,256,512]{2,1,0:T(8,128)} %collective-permute-done.6), channel_id=1, source_target_pairs={{0,12},{1,13},{2,14},{3,15},{4,0},{5,1},{6,2},{7,3},{8,4},{9,5},{1... | collective-permute-start | bytes 3145736 | tf_op jit(solution)/shard_map/ppermute | solution.py:33
  121.7 41.1 %collective-permute-start.13 = (f32[2,128,1024]{2,1,0:T(8,128)}, f32[2,128,1024]{2,1,0:T(8,128)}, u32[]{:S(2)}, u32[]{:S(2)}) collective-permute-start(f32[2,128,1024]{2,1,0:T(8,128)} %collective-permute-done.11), channel_id=1, source_target_pairs={{0,1},{1,0},{2,3},{3,2},{4,5},{5,4},{6,7},{7,6},{8,9},{9,8},{10,11... | collective-permute-start | bytes 3145736 | tf_op jit(solution)/shard_map/ppermute | solution.py:33
  131.5 35.1 %collective-permute-start.3 = (f32[2,256,512]{2,1,0:T(8,128)}, f32[2,256,512]{2,1,0:T(8,128)}, u32[]{:S(2)}, u32[]{:S(2)}) collective-permute-start(f32[2,256,512]{2,1,0:T(8,128)} %pad_maximum_fusion.1), channel_id=1, source_target_pairs={{0,4},{1,5},{2,6},{3,7},{4,8},{5,9},{6,10},{7,11},{8,12},{9,13},{1... | collective-permute-start | bytes 3145736 | tf_op jit(solution)/shard_map/ppermute | solution.py:33
  131.5 40.7 %collective-permute-start.4 = (f32[2,256,512]{2,1,0:T(8,128)}, f32[2,256,512]{2,1,0:T(8,128)}, u32[]{:S(2)}, u32[]{:S(2)}) collective-permute-start(f32[2,256,512]{2,1,0:T(8,128)} %pad_maximum_fusion.1), channel_id=1, source_target_pairs={{0,12},{1,13},{2,14},{3,15},{4,0},{5,1},{6,2},{7,3},{8,4},{9,5},{1... | collective-permute-start | bytes 3145736 | tf_op jit(solution)/shard_map/ppermute | solution.py:33
  143.9 4.5 %copy-start.16 = (f32[2,128,512]{1,2,0:T(8,128)S(1)}, f32[2,128,512]{1,2,0:T(8,128)}, u32[]{:S(2)}) copy-start(f32[2,128,512]{1,2,0:T(8,128)} %copy.90) | copy-start | bytes 1572868
  143.9 5.4 %copy-start.15 = (f32[2,128,512]{1,2,0:T(8,128)S(1)}, f32[2,128,512]{1,2,0:T(8,128)}, u32[]{:S(2)}) copy-start(f32[2,128,512]{1,2,0:T(8,128)} %copy.91) | copy-start | bytes 1572868
  154.5 3.1 %copy-start.14 = (f32[2,128,512]{1,2,0:T(8,128)S(1)}, f32[2,128,512]{1,2,0:T(8,128)}, u32[]{:S(2)}) copy-start(f32[2,128,512]{1,2,0:T(8,128)} %copy.92) | copy-start | bytes 1572868
  178.5 2.9 %copy-start.18 = (f32[2,128,512]{1,2,0:T(8,128)S(1)}, f32[2,128,512]{1,2,0:T(8,128)}, u32[]{:S(2)}) copy-start(f32[2,128,512]{1,2,0:T(8,128)} %copy.95) | copy-start | bytes 1572868
  178.5 3.8 %copy-start.17 = (f32[2,128,512]{1,2,0:T(8,128)S(1)}, f32[2,128,512]{1,2,0:T(8,128)}, u32[]{:S(2)}) copy-start(f32[2,128,512]{1,2,0:T(8,128)} %copy.96) | copy-start | bytes 1572868
  178.5 4.7 %copy-start.12 = (f32[2,128,512]{1,2,0:T(8,128)S(1)}, f32[2,128,512]{1,2,0:T(8,128)}, u32[]{:S(2)}) copy-start(f32[2,128,512]{1,2,0:T(8,128)} %copy.97) | copy-start | bytes 1572868
  180.6 3.6 %copy-start.11 = (f32[2,128,512]{1,2,0:T(8,128)S(1)}, f32[2,128,512]{1,2,0:T(8,128)}, u32[]{:S(2)}) copy-start(f32[2,128,512]{1,2,0:T(8,128)} %copy.98) | copy-start | bytes 1572868
  181.5 3.6 %copy-start.10 = (f32[2,128,512]{1,2,0:T(8,128)S(1)}, f32[2,128,512]{1,2,0:T(8,128)}, u32[]{:S(2)}) copy-start(f32[2,128,512]{1,2,0:T(8,128)} %copy.99) | copy-start | bytes 1572868
  182.4 3.6 %copy-start.9 = (f32[2,128,512]{1,2,0:T(8,128)S(1)}, f32[2,128,512]{1,2,0:T(8,128)}, u32[]{:S(2)}) copy-start(f32[2,128,512]{1,2,0:T(8,128)} %copy.100) | copy-start | bytes 1572868
  183.2 3.6 %copy-start.26 = (f32[2,256,128]{2,1,0:T(8,128)S(1)}, f32[2,256,128]{2,1,0:T(8,128)}, u32[]{:S(2)}) copy-start(f32[2,256,128]{2,1,0:T(8,128)} %get-tuple-element.15) | copy-start | bytes 786436
  183.3 3.6 %copy-start.27 = (f32[2,256,128]{2,1,0:T(8,128)S(1)}, f32[2,256,128]{2,1,0:T(8,128)}, u32[]{:S(2)}) copy-start(f32[2,256,128]{2,1,0:T(8,128)} %get-tuple-element.16) | copy-start | bytes 786436
  183.3 25.6 %collective-permute-start.7 = (f32[2,256,512]{2,1,0:T(8,128)}, f32[2,256,512]{2,1,0:T(8,128)S(1)}, u32[]{:S(2)}, u32[]{:S(2)}) collective-permute-start(f32[2,256,512]{2,1,0:T(8,128)} %collective-permute-done.3), channel_id=1, source_target_pairs={{0,4},{1,5},{2,6},{3,7},{4,8},{5,9},{6,10},{7,11},{8,12},{9,13},{1... | collective-permute-start | bytes 3145736 | tf_op jit(solution)/shard_map/ppermute | solution.py:33
  186.8 3.2 %copy-start.24 = (f32[2,256,128]{2,1,0:T(8,128)S(1)}, f32[2,256,128]{2,1,0:T(8,128)}, u32[]{:S(2)}) copy-start(f32[2,256,128]{2,1,0:T(8,128)} %get-tuple-element.17) | copy-start | bytes 786436
  186.8 3.2 %copy-start.25 = (f32[2,256,128]{2,1,0:T(8,128)S(1)}, f32[2,256,128]{2,1,0:T(8,128)}, u32[]{:S(2)}) copy-start(f32[2,256,128]{2,1,0:T(8,128)} %get-tuple-element.18) | copy-start | bytes 786436
  190.0 18.9 %copy-start.22 = (f32[2,256,128]{2,1,0:T(8,128)S(1)}, f32[2,256,128]{2,1,0:T(8,128)}, u32[]{:S(2)}) copy-start(f32[2,256,128]{2,1,0:T(8,128)} %get-tuple-element.9) | copy-start | bytes 786436
  190.0 18.9 %copy-start.23 = (f32[2,256,128]{2,1,0:T(8,128)S(1)}, f32[2,256,128]{2,1,0:T(8,128)}, u32[]{:S(2)}) copy-start(f32[2,256,128]{2,1,0:T(8,128)} %get-tuple-element.10) | copy-start | bytes 786436
  190.0 20.7 %copy-start.1 = (f32[2,512,2,256]{3,1,2,0:T(8,128)S(1)}, f32[2,512,2,256]{3,1,2,0:T(8,128)}, u32[]{:S(2)}) copy-start(f32[2,512,2,256]{3,1,2,0:T(8,128)} %fusion.24) | copy-start | bytes 6291460
  190.0 20.7 %copy-start.2 = (f32[2,512,2,256]{3,1,2,0:T(8,128)S(1)}, f32[2,512,2,256]{3,1,2,0:T(8,128)}, u32[]{:S(2)}) copy-start(f32[2,512,2,256]{3,1,2,0:T(8,128)} %fusion.32) | copy-start | bytes 6291460
  193.3 17.5 %copy-start = (f32[2,512,2,256]{3,1,2,0:T(8,128)S(1)}, f32[2,512,2,256]{3,1,2,0:T(8,128)}, u32[]{:S(2)}) copy-start(f32[2,512,2,256]{3,1,2,0:T(8,128)} %fusion.22) | copy-start | bytes 6291460
  193.3 17.5 %copy-start.21 = (f32[2,256,128]{2,1,0:T(8,128)S(1)}, f32[2,256,128]{2,1,0:T(8,128)}, u32[]{:S(2)}) copy-start(f32[2,256,128]{2,1,0:T(8,128)} %get-tuple-element.8) | copy-start | bytes 786436
  217.6 4.3 %copy-start.13 = (f32[2,128,512]{1,2,0:T(8,128)S(1)}, f32[2,128,512]{1,2,0:T(8,128)}, u32[]{:S(2)}) copy-start(f32[2,128,512]{1,2,0:T(8,128)} %copy.103) | copy-start | bytes 1572868
  218.8 5.0 %copy-start.4 = (f32[2,128,2048]{2,1,0:T(8,128)S(1)}, f32[2,128,2048]{2,1,0:T(8,128)}, u32[]{:S(2)}) copy-start(f32[2,128,2048]{2,1,0:T(8,128)} %slice_dynamic-update-slice_fusion) | copy-start | bytes 6291460
  218.8 20.4 %collective-permute-start.9 = (f32[2,128,512]{1,2,0:T(8,128)}, f32[2,128,512]{1,2,0:T(8,128)S(1)}, u32[]{:S(2)}, u32[]{:S(2)}) collective-permute-start(f32[2,128,512]{1,2,0:T(8,128)} %get-tuple-element.32), channel_id=1, source_target_pairs={{0,1},{1,0},{2,3},{3,2},{4,5},{5,4},{6,7},{7,6},{8,9},{9,8},{10,11... | collective-permute-start | bytes 1572872 | tf_op jit(solution)/shard_map/ppermute | solution.py:33
  223.7 6.1 %copy-start.6 = (f32[2,128,2048]{2,1,0:T(8,128)S(1)}, f32[2,128,2048]{2,1,0:T(8,128)}, u32[]{:S(2)}) copy-start(f32[2,128,2048]{2,1,0:T(8,128)} %slice_dynamic-update-slice_fusion.3) | copy-start | bytes 6291460
  235.8 26.4 %copy-start.20 = (f32[1,2,128,512]{2,3,1,0:T(8,128)S(1)}, f32[1,2,128,512]{2,3,1,0:T(8,128)}, u32[]{:S(2)}) copy-start(f32[1,2,128,512]{2,3,1,0:T(8,128)} %get-tuple-element.31) | copy-start | bytes 1572868
  237.3 13.6 %collective-permute-start.12 = (f32[2,128,512]{1,2,0:T(8,128)S(1)}, f32[2,128,512]{1,2,0:T(8,128)S(1)}, u32[]{:S(2)}, u32[]{:S(2)}) collective-permute-start(f32[2,128,512]{1,2,0:T(8,128)S(1)} %pad_maximum_fusion.5), channel_id=1, source_target_pairs={{0,2},{1,3},{2,0},{3,1},{4,6},{5,7},{6,4},{7,5},{8,10},{9,11},{10,... | collective-permute-start | bytes 1572872 | tf_op jit(solution)/shard_map/ppermute | solution.py:33
  238.3 24.0 %collective-permute-start.14 = (f32[2,128,512]{1,2,0:T(8,128)S(1)}, f32[2,128,512]{1,2,0:T(8,128)S(1)}, u32[]{:S(2)}, u32[]{:S(2)}) collective-permute-start(f32[2,128,512]{1,2,0:T(8,128)S(1)} %pad_maximum_fusion.6), channel_id=1, source_target_pairs={{0,3},{1,2},{2,1},{3,0},{4,7},{5,6},{6,5},{7,4},{8,11},{9,10},{10,... | collective-permute-start | bytes 1572872 | tf_op jit(solution)/shard_map/ppermute | solution.py:33

commit v7 on v5

--- a/solution.py
+++ b/solution.py
@@ -58,14 +58,24 @@
     q1 = send(own, xor_perm(nblk, 1))
     c2 = send(cols(own, p ^ 2), xor_perm(nblk, 2))
     c3 = send(cols(own, p ^ 3), xor_perm(nblk, 3))
-    rest = jnp.concatenate([cols(own, p ^ 2 ^ m) for m in range(1, GROUP)], axis=2)
+    rest = jnp.concatenate([cols(own, p), cols(own, p ^ 1)], axis=2)
     rest, _, _ = lax.optimization_barrier((rest, c2, c3))
     rest = send(rest, xor_perm(nblk, 2))
-    q2 = jnp.zeros_like(own)
-    q2 = lax.dynamic_update_slice_in_dim(q2, c2, p * cw, axis=2)
-    for m in range(1, GROUP):
-        q2 = lax.dynamic_update_slice_in_dim(q2, rest[:, :, (m - 1) * cw:m * cw], (p ^ m) * cw, axis=2)
-    q3 = send(q2, xor_perm(nblk, 1))
+    r_c = send(jnp.concatenate([c2, c3], axis=2), xor_perm(nblk, 1))
+    r_rest = send(rest, xor_perm(nblk, 1))
+
+    def assemble(blocks):
+        out = jnp.zeros_like(own)
+        for m, blk in blocks:
+            out = lax.dynamic_update_slice_in_dim(out, blk, (p ^ m) * cw, axis=2)
+        return out
+
+    q2 = assemble([
+        (0, c2), (1, r_c[:, :, cw:]), (2, rest[:, :, :cw]), (3, rest[:, :, cw:]),
+    ])
+    q3 = assemble([
+        (0, c3), (1, r_c[:, :, :cw]), (3, r_rest[:, :, :cw]), (2, r_rest[:, :, cw:]),
+    ])
 
     def mm(lhs, rhs):
         return jnp.einsum(

time: 208 us -> 233 us (1.12)
  waiting for transfers between devices: 85.7 us -> 111 us
    ppermute x14 -> x15, waiting for transfers between devices: 85.7 us -> 111 us  [send(): return lax.ppermute(x, 'blk', perm)]
    ppermute x14 -> x15, starting transfers between devices: 18 us -> 16.1 us  [send(): return lax.ppermute(x, 'blk', perm)]
  transfers between devices with their start and end apart: 14 -> 15, of which waited for: 8 -> 9; matrix products, arithmetic and copies ran while one was open for 16% -> 14% of each run, Pallas kernels for 0% -> 0%
where the time goes in v7:
time: 233 us; the launch traced here: 232 us
  waiting for transfers between devices  111 us (48%)
  blocking collectives  35.6 us (15%)
  local copies, waits for them, and re-layouts  31.8 us (14%)
  matrix products  28.7 us (12%)
  starting transfers between devices  16.1 us (7%)
  other arithmetic  8.61 us (4%)
    ppermute x15, waiting for transfers between devices, send(): return lax.ppermute(x, 'blk', perm)  111 us
    all_to_all x1, blocking collectives, on_device(): lax.all_to_all(projected, 'freq', split_axis=1, concat_axis=3, tiled=True)  35.6 us
    dot_general x9, matrix products, mm(): jnp.einsum('aik,bkj->abij', lhs, rhs, precision=lax.Precision.HIGH, prefe...  18.5 us
    ppermute x15, starting transfers between devices, send(): return lax.ppermute(x, 'blk', perm)  16.1 us
    dynamic_update_slice x14, local copies, waits for them, and re-layouts, on_device(): lax.dynamic_update_slice_in_dim(right, pc[:, i * rb:(i + 1) * rb], kblk(g...  12.9 us
    dot_general x1, matrix products, on_device(): jnp.einsum('srt,tc->csr', traces, table, preferred_element_type=jnp.float32)  10.2 us
  transfers between devices with their start and end apart: 15, of which 9 were waited for; matrix products, arithmetic and copies ran while one was open for 14% of the time, Pallas kernels for 0%

profile of v7, /device:TPU:1, one launch (start us, length us, event | category | flops | bytes accessed | tf_op | source)
XLA Modules:
  0.0 232.1 jit_solution(4219298550140719916)
XLA Ops:
  0.1 10.2 %convolution_bitcast_fusion = f32[2,8,128,256]{3,1,0,2:T(8,128)S(1)} fusion(bf16[128,256,256]{2,1,0:T(8,128)(2,1)} %param.2, bf16[256,8]{0,1:T(8,128)(2,1)S(1)} %get-tuple-element.50, bf16[256,8]{0,1:T(8,128)(2,1)S(1)} %get-tuple-element.49), kind=kOutput, calls=%fused_computation.21 | convolution fusion | flops 268451840 | bytes 18882560 | tf_op jit(solution)/shard_map/srt,tc->csr/dot_general | solution.py:43
  10.4 1.1 copy.10
  11.5 35.6 %all_to_all.15 = f32[2,8,128,256]{3,0,2,1:T(2,128)S(1)} all-to-all(f32[2,8,128,256]{3,0,2,1:T(2,128)S(1)} %copy.10), channel_id=1, replica_groups=mesh['freq'=8,'blk'=16] {'freq'}, dimensions={1} | all-to-all | bytes 4194304 | tf_op jit(solution)/shard_map/all_to_all | solution.py:45
  47.1 2.5 %copy.11 = f32[2,1,128,8,256]{4,3,2,0,1:T(8,128)} copy(f32[2,1,128,8,256]{4,0,2,3,1:T(2,128)S(1)} %bitcast.146) | data formatting | bytes 4194304 | tf_op jit(solution)/shard_map/all_to_all | solution.py:45
  49.6 1.7 squeeze.27
  51.3 1.8 collective-permute-start
  53.2 4.4 %broadcast_in_dim.8 = f32[2,2048,512]{2,1,0:T(8,128)} broadcast(f32[]{:T(128)} %constant.92.clone.1), dimensions={} | broadcast | bytes 8388612 | tf_op jit(solution)/shard_map/broadcast_in_dim | solution.py:118
  57.5 1.0 constant_dynamic-update-slice_fusion.5
  59.3 1.0 collective-permute-start.2
  60.2 1.1 pad_maximum_fusion.4
  61.3 10.6 %collective-permute-done.1 = f32[2,128,512]{2,1,0:T(8,128)S(1)} collective-permute-done((f32[2,128,512]{2,1,0:T(8,128)S(1)}, f32[2,128,512]{2,1,0:T(8,128)S(1)}, u32[]{:S(2)}, u32[]{:S(2)}) %collective-permute-start.1) | collective-permute-done | bytes 524320 | tf_op jit(solution)/shard_map/ppermute | solution.py:33
  72.0 11.5 %collective-permute-done.2 = f32[2,128,512]{2,1,0:T(8,128)S(1)} collective-permute-done((f32[2,128,512]{2,1,0:T(8,128)S(1)}, f32[2,128,512]{2,1,0:T(8,128)S(1)}, u32[]{:S(2)}, u32[]{:S(2)}) %collective-permute-start.2) | collective-permute-done | bytes 524320 | tf_op jit(solution)/shard_map/ppermute | solution.py:33
  84.2 1.1 pad_maximum_fusion.3
  86.4 21.9 %collective-permute-done.10 = f32[2,128,1024]{2,1,0:T(8,128)} collective-permute-done((f32[2,128,1024]{2,1,0:T(8,128)}, f32[2,128,1024]{2,1,0:T(8,128)}, u32[]{:S(2)}, u32[]{:S(2)}) %collective-permute-start.10) | collective-permute-done | bytes 1048608 | tf_op jit(solution)/shard_map/ppermute | solution.py:33
  108.3 1.0 collective-permute-start.11
  109.3 1.9 constant_dynamic-update-slice_fusion.4
  111.3 1.4 collective-permute-start.3
  112.7 1.5 collective-permute-start.4
  114.4 1.0 constant_dynamic-update-slice_fusion.9
  115.7 0.9 constant_dynamic-update-slice_fusion.8
  116.6 2.7 %collective-permute-start.6 = (f32[2,256,512]{2,1,0:T(8,128)S(1)}, f32[2,256,512]{2,1,0:T(8,128)S(1)}, u32[]{:S(2)}, u32[]{:S(2)}) collective-permute-start(f32[2,256,512]{2,1,0:T(8,128)S(1)} %get-tuple-element.43), channel_id=1, source_target_pairs={{0,12},{1,13},{2,14},{3,15},{4,0},{5,1},{6,2},{7,3},{8,4},{9,5},{1... | collective-permute-start | bytes 3145736 | tf_op jit(solution)/shard_map/ppermute | solution.py:33
  119.3 1.3 slice_dynamic-update-slice_fusion.5
  120.5 1.1 slice_dynamic-update-slice_fusion.4
  121.6 1.1 slice_dynamic-update-slice_fusion.3
  122.7 1.7 constant_dynamic-update-slice_fusion.6
  125.1 1.0 fusion.28
  126.1 1.0 fusion.30
  127.3 10.1 %collective-permute-done.3 = f32[2,256,512]{2,1,0:T(8,128)S(1)} collective-permute-done((f32[2,256,512]{2,1,0:T(8,128)S(1)}, f32[2,256,512]{2,1,0:T(8,128)S(1)}, u32[]{:S(2)}, u32[]{:S(2)}) %collective-permute-start.3) | collective-permute-done | bytes 1048608 | tf_op jit(solution)/shard_map/ppermute | solution.py:33
  140.7 19.1 %collective-permute-done.5 = f32[2,256,512]{2,1,0:T(8,128)S(1)} collective-permute-done((f32[2,256,512]{2,1,0:T(8,128)S(1)}, f32[2,256,512]{2,1,0:T(8,128)S(1)}, u32[]{:S(2)}, u32[]{:S(2)}) %collective-permute-start.5) | collective-permute-done | bytes 1048608 | tf_op jit(solution)/shard_map/ppermute | solution.py:33
  159.9 0.9 slice_dynamic-update-slice_fusion.13
  160.7 0.8 slice_dynamic-update-slice_fusion.12
  161.6 1.3 collective-permute-start.8
  162.9 1.0 fusion.20
  163.9 1.0 fusion.22
  165.8 1.0 fusion.24
  167.7 1.0 fusion.26
  168.7 13.6 %collective-permute-done.7 = f32[2,256,512]{2,1,0:T(8,128)S(1)} collective-permute-done((f32[2,256,512]{2,1,0:T(8,128)S(1)}, f32[2,256,512]{2,1,0:T(8,128)S(1)}, u32[]{:S(2)}, u32[]{:S(2)}) %collective-permute-start.7) | collective-permute-done | bytes 1048608 | tf_op jit(solution)/shard_map/ppermute | solution.py:33
  184.0 1.1 collective-permute-done.8
  186.7 9.3 %fusion.4 = f32[2,2,256,512]{3,2,0,1:T(8,128)S(1)} fusion(f32[2,128,2048]{2,1,0:T(8,128)S(1)} %slice_dynamic-update-slice_fusion, f32[2,128,2048]{2,1,0:T(8,128)S(1)} %slice_dynamic-update-slice_fusion.3, f32[2,2048,512]{2,1,0:T(8,128)} %slice_dynamic-update-slice_fusion.6), kind=kOutput, calls=%fused_computation.20 | convolution fusion | flops 6443499520 | bytes 14680064 | tf_op jit(solution)/shard_map/aik,bkj->abij/dot_general | solution.py:81
  196.0 1.0 fusion.18
  197.1 1.9 add_bitcast_fusion
  199.0 1.8 fusion.38
  200.8 1.5 fusion.34
  202.5 2.9 %collective-permute-start.14 = (f32[2,128,512]{2,1,0:T(8,128)S(1)}, f32[2,128,512]{2,1,0:T(8,128)S(1)}, u32[]{:S(2)}, u32[]{:S(2)}) collective-permute-start(f32[2,128,512]{2,1,0:T(8,128)S(1)} %get-tuple-element.36), channel_id=1, source_target_pairs={{0,3},{1,2},{2,1},{3,0},{4,7},{5,6},{6,5},{7,4},{8,11},{9,10},{10,... | collective-permute-start | bytes 1572872 | tf_op jit(solution)/shard_map/ppermute | solution.py:33
  206.0 11.8 %collective-permute-done.14 = f32[2,128,512]{2,1,0:T(8,128)S(1)} collective-permute-done((f32[2,128,512]{2,1,0:T(8,128)S(1)}, f32[2,128,512]{2,1,0:T(8,128)S(1)}, u32[]{:S(2)}, u32[]{:S(2)}) %collective-permute-start.14) | collective-permute-done | bytes 524320 | tf_op jit(solution)/shard_map/ppermute | solution.py:33
  217.8 11.3 %collective-permute-done.13 = f32[2,128,512]{2,1,0:T(8,128)S(1)} collective-permute-done((f32[2,128,512]{2,1,0:T(8,128)S(1)}, f32[2,128,512]{2,1,0:T(8,128)S(1)}, u32[]{:S(2)}, u32[]{:S(2)}) %collective-permute-start.13) | collective-permute-done | bytes 524320 | tf_op jit(solution)/shard_map/ppermute | solution.py:33
  229.1 1.3 pad_maximum_fusion
  230.6 1.5 maximum_bitcast_fusion.2
  (41 shorter events, 13.4 us)
Async XLA Ops:
  51.3 58.0 %collective-permute-start = (f32[2,128,2048]{2,1,0:T(8,128)S(1)}, f32[2,128,2048]{2,1,0:T(8,128)}, u32[]{:S(2)}, u32[]{:S(2)}) collective-permute-start(f32[2,128,2048]{2,1,0:T(8,128)S(1)} %squeeze.27), channel_id=1, source_target_pairs={{0,1},{1,0},{2,3},{3,2},{4,5},{5,4},{6,7},{7,6},{8,9},{9,8},{10,11... | collective-permute-start | bytes 6291464 | tf_op jit(solution)/shard_map/ppermute | solution.py:33
  58.5 13.4 %collective-permute-start.1 = (f32[2,128,512]{2,1,0:T(8,128)S(1)}, f32[2,128,512]{2,1,0:T(8,128)S(1)}, u32[]{:S(2)}, u32[]{:S(2)}) collective-permute-start(f32[2,128,512]{2,1,0:T(8,128)S(1)} %get-tuple-element.40), channel_id=1, source_target_pairs={{0,2},{1,3},{2,0},{3,1},{4,6},{5,7},{6,4},{7,5},{8,10},{9,11},{10,... | collective-permute-start | bytes 1572872 | tf_op jit(solution)/shard_map/ppermute | solution.py:33
  59.3 24.2 %collective-permute-start.2 = (f32[2,128,512]{2,1,0:T(8,128)S(1)}, f32[2,128,512]{2,1,0:T(8,128)S(1)}, u32[]{:S(2)}, u32[]{:S(2)}) collective-permute-start(f32[2,128,512]{2,1,0:T(8,128)S(1)} %get-tuple-element.39), channel_id=1, source_target_pairs={{0,3},{1,2},{2,1},{3,0},{4,7},{5,6},{6,5},{7,4},{8,11},{9,10},{10,... | collective-permute-start | bytes 1572872 | tf_op jit(solution)/shard_map/ppermute | solution.py:33
  60.2 25.4 %copy-start.2 = (f32[1,2]{1,0:T(1,128)S(1)}, f32[1,2]{1,0:T(1,128)}, u32[]{:S(2)}) copy-start(f32[1,2]{1,0:T(1,128)} %param.3) | copy-start | bytes 28
  71.9 12.2 %copy-start = (f32[2,128,512]{2,1,0:T(8,128)}, f32[2,128,512]{2,1,0:T(8,128)S(1)}, u32[]{:S(2)}) copy-start(f32[2,128,512]{2,1,0:T(8,128)S(1)} %collective-permute-done.1) | copy-start | bytes 1572868
  83.4 24.9 %collective-permute-start.10 = (f32[2,128,1024]{2,1,0:T(8,128)}, f32[2,128,1024]{2,1,0:T(8,128)}, u32[]{:S(2)}, u32[]{:S(2)}) collective-permute-start(f32[2,128,1024]{2,1,0:T(8,128)} %pad_maximum_fusion.4), channel_id=1, source_target_pairs={{0,2},{1,3},{2,0},{3,1},{4,6},{5,7},{6,4},{7,5},{8,10},{9,11},{10,... | collective-permute-start | bytes 3145736 | tf_op jit(solution)/shard_map/ppermute | solution.py:33
  85.2 31.4 %collective-permute-start.9 = (f32[2,128,1024]{2,1,0:T(8,128)}, f32[2,128,1024]{2,1,0:T(8,128)}, u32[]{:S(2)}, u32[]{:S(2)}) collective-permute-start(f32[2,128,1024]{2,1,0:T(8,128)} %pad_maximum_fusion.3), channel_id=1, source_target_pairs={{0,1},{1,0},{2,3},{3,2},{4,5},{5,4},{6,7},{7,6},{8,9},{9,8},{10,11... | collective-permute-start | bytes 3145736 | tf_op jit(solution)/shard_map/ppermute | solution.py:33
  108.3 18.9 %collective-permute-start.11 = (f32[2,128,1024]{2,1,0:T(8,128)}, f32[2,128,1024]{2,1,0:T(8,128)S(1)}, u32[]{:S(2)}, u32[]{:S(2)}) collective-permute-start(f32[2,128,1024]{2,1,0:T(8,128)} %collective-permute-done.10), channel_id=1, source_target_pairs={{0,1},{1,0},{2,3},{3,2},{4,5},{5,4},{6,7},{7,6},{8,9},{9,8},{10,11... | collective-permute-start | bytes 3145736 | tf_op jit(solution)/shard_map/ppermute | solution.py:33
  111.2 3.2 %copy-start.1 = (f32[2,128,512]{2,1,0:T(8,128)S(1)}, f32[2,128,512]{2,1,0:T(8,128)}, u32[]{:S(2)}) copy-start(f32[2,128,512]{2,1,0:T(8,128)} %copy-done) | copy-start | bytes 1572868
  111.3 26.1 %collective-permute-start.3 = (f32[2,256,512]{2,1,0:T(8,128)S(1)}, f32[2,256,512]{2,1,0:T(8,128)S(1)}, u32[]{:S(2)}, u32[]{:S(2)}) collective-permute-start(f32[2,256,512]{2,1,0:T(8,128)S(1)} %pad_maximum_fusion.2), channel_id=1, source_target_pairs={{0,4},{1,5},{2,6},{3,7},{4,8},{5,9},{6,10},{7,11},{8,12},{9,13},{1... | collective-permute-start | bytes 3145736 | tf_op jit(solution)/shard_map/ppermute | solution.py:33
  112.7 26.4 %collective-permute-start.4 = (f32[2,256,512]{2,1,0:T(8,128)S(1)}, f32[2,256,512]{2,1,0:T(8,128)S(1)}, u32[]{:S(2)}, u32[]{:S(2)}) collective-permute-start(f32[2,256,512]{2,1,0:T(8,128)S(1)} %pad_maximum_fusion.2), channel_id=1, source_target_pairs={{0,12},{1,13},{2,14},{3,15},{4,0},{5,1},{6,2},{7,3},{8,4},{9,5},{1... | collective-permute-start | bytes 3145736 | tf_op jit(solution)/shard_map/ppermute | solution.py:33
  116.6 43.3 %collective-permute-start.5 = (f32[2,256,512]{2,1,0:T(8,128)S(1)}, f32[2,256,512]{2,1,0:T(8,128)S(1)}, u32[]{:S(2)}, u32[]{:S(2)}) collective-permute-start(f32[2,256,512]{2,1,0:T(8,128)S(1)} %get-tuple-element.43), channel_id=1, source_target_pairs={{0,4},{1,5},{2,6},{3,7},{4,8},{5,9},{6,10},{7,11},{8,12},{9,13},{1... | collective-permute-start | bytes 3145736 | tf_op jit(solution)/shard_map/ppermute | solution.py:33
  116.6 45.0 %collective-permute-start.6 = (f32[2,256,512]{2,1,0:T(8,128)S(1)}, f32[2,256,512]{2,1,0:T(8,128)S(1)}, u32[]{:S(2)}, u32[]{:S(2)}) collective-permute-start(f32[2,256,512]{2,1,0:T(8,128)S(1)} %get-tuple-element.43), channel_id=1, source_target_pairs={{0,12},{1,13},{2,14},{3,15},{4,0},{5,1},{6,2},{7,3},{8,4},{9,5},{1... | collective-permute-start | bytes 3145736 | tf_op jit(solution)/shard_map/ppermute | solution.py:33
  137.4 44.9 %collective-permute-start.7 = (f32[2,256,512]{2,1,0:T(8,128)S(1)}, f32[2,256,512]{2,1,0:T(8,128)S(1)}, u32[]{:S(2)}, u32[]{:S(2)}) collective-permute-start(f32[2,256,512]{2,1,0:T(8,128)S(1)} %collective-permute-done.3), channel_id=1, source_target_pairs={{0,4},{1,5},{2,6},{3,7},{4,8},{5,9},{6,10},{7,11},{8,12},{9,13},{1... | collective-permute-start | bytes 3145736 | tf_op jit(solution)/shard_map/ppermute | solution.py:33
  161.6 23.5 %collective-permute-start.8 = (f32[2,256,512]{2,1,0:T(8,128)S(1)}, f32[2,256,512]{2,1,0:T(8,128)S(1)}, u32[]{:S(2)}, u32[]{:S(2)}) collective-permute-start(f32[2,256,512]{2,1,0:T(8,128)S(1)} %collective-permute-done.6), channel_id=1, source_target_pairs={{0,12},{1,13},{2,14},{3,15},{4,0},{5,1},{6,2},{7,3},{8,4},{9,5},{1... | collective-permute-start | bytes 3145736 | tf_op jit(solution)/shard_map/ppermute | solution.py:33
  202.5 15.3 %collective-permute-start.14 = (f32[2,128,512]{2,1,0:T(8,128)S(1)}, f32[2,128,512]{2,1,0:T(8,128)S(1)}, u32[]{:S(2)}, u32[]{:S(2)}) collective-permute-start(f32[2,128,512]{2,1,0:T(8,128)S(1)} %get-tuple-element.36), channel_id=1, source_target_pairs={{0,3},{1,2},{2,1},{3,0},{4,7},{5,6},{6,5},{7,4},{8,11},{9,10},{10,... | collective-permute-start | bytes 1572872 | tf_op jit(solution)/shard_map/ppermute | solution.py:33
  205.3 23.7 %collective-permute-start.13 = (f32[2,128,512]{2,1,0:T(8,128)S(1)}, f32[2,128,512]{2,1,0:T(8,128)S(1)}, u32[]{:S(2)}, u32[]{:S(2)}) collective-permute-start(f32[2,128,512]{2,1,0:T(8,128)S(1)} %get-tuple-element.37), channel_id=1, source_target_pairs={{0,2},{1,3},{2,0},{3,1},{4,6},{5,7},{6,4},{7,5},{8,10},{9,11},{10,... | collective-permute-start | bytes 1572872 | tf_op jit(solution)/shard_map/ppermute | solution.py:33
  206.0 23.1 %collective-permute-start.12 = (f32[2,128,512]{2,1,0:T(8,128)S(1)}, f32[2,128,512]{2,1,0:T(8,128)}, u32[]{:S(2)}, u32[]{:S(2)}) collective-permute-start(f32[2,128,512]{2,1,0:T(8,128)S(1)} %get-tuple-element.35), channel_id=1, source_target_pairs={{0,1},{1,0},{2,3},{3,2},{4,5},{5,4},{6,7},{7,6},{8,9},{9,8},{10,11... | collective-permute-start | bytes 1572872 | tf_op jit(solution)/shard_map/ppermute | solution.py:33

commit v8 on v7

--- a/solution.py
+++ b/solution.py
@@ -91,15 +91,17 @@
     da = send(part_a, dn)
     ub = send(part_b, up)
     db = send(part_b, dn)
-    fa = send(ua, up)
-    fb = send(db, dn)
+    fa0 = send(ua[:, :rb], up)
+    fa1 = send(da[:, rb:], dn)
+    fb0 = send(ub[:, :rb], up)
+    fb1 = send(db[:, rb:], dn)
 
-    half = GROUP // 2
     pieces = [
-        (y, 0, part_a), (y, 1, part_b),
-        ((y - 1) % ny, 0, ua), ((y + 1) % ny, 0, da),
-        ((y - 1) % ny, 1, ub), ((y + 1) % ny, 1, db),
-        ((y + 2) % ny, 0, fa), ((y + 2) % ny, 1, fb),
+        (y, (0, 1), part_a), (y, (2, 3), part_b),
+        ((y - 1) % ny, (0, 1), ua), ((y + 1) % ny, (0, 1), da),
+        ((y - 1) % ny, (2, 3), ub), ((y + 1) % ny, (2, 3), db),
+        ((y + 2) % ny, (0,), fa0), ((y + 2) % ny, (1,), fa1),
+        ((y + 2) % ny, (2,), fb0), ((y + 2) % ny, (3,), fb1),
     ]
 
     def kblk(g, m):
@@ -107,19 +109,18 @@
 
     early = jnp.concatenate([own, q1], axis=1)
     t_early = None
-    for g, h, pc in pieces:
+    for g, ms, pc in pieces:
         lhs = jnp.concatenate(
-            [lax.dynamic_slice_in_dim(early, kblk(g, half * h + i), rb, axis=2) for i in range(half)],
-            axis=2,
+            [lax.dynamic_slice_in_dim(early, kblk(g, m), rb, axis=2) for m in ms], axis=2
         )
         term = mm(lhs, pc)
         t_early = term if t_early is None else t_early + term
 
     right = jnp.zeros((2, n, cw), jnp.float32)
-    for g, h, pc in pieces:
-        for i in range(half):
+    for g, ms, pc in pieces:
+        for i, m in enumerate(ms):
             right = lax.dynamic_update_slice_in_dim(
-                right, pc[:, i * rb:(i + 1) * rb], kblk(g, half * h + i), axis=1
+                right, pc[:, i * rb:(i + 1) * rb], kblk(g, m), axis=1
             )
     late = jnp.concatenate([q2, q3], axis=1)
     t_late = mm(late, right)

time: 233 us -> 241 us (1.034)
  starting transfers between devices: 16.1 us -> 20.3 us
    ppermute x15 -> x17, starting transfers between devices: 16.1 us -> 20.3 us  [send(): return lax.ppermute(x, 'blk', perm)]
    slice x0 -> x4, local copies, waits for them, and re-layouts: none -> 3.51 us  [the longest x1 0.89 us: on_device(): fa0 = send(ua[:, :rb], up)]
    dynamic_update_slice x14 -> x10, local copies, waits for them, and re-layouts: 12.9 us -> 9.59 us  [on_device(): lax.dynamic_update_slice_in_dim(right, pc[:, i * rb:(i + 1) * rb], kblk(g...]
    dot_general x9 -> x11, matrix products: 18.5 us -> 20.6 us  [mm(): jnp.einsum('aik,bkj->abij', lhs, rhs, precision=lax.Precision.HIGH, prefe...]
    ppermute x15 -> x17, waiting for transfers between devices: 111 us -> 113 us  [send(): return lax.ppermute(x, 'blk', perm)]
  transfers between devices with their start and end apart: 15 -> 17, of which waited for: 9 -> 8; matrix products, arithmetic and copies ran while one was open for 14% -> 14% of each run, Pallas kernels for 0% -> 0%
where the time goes in v8:
time: 241 us
  waiting for transfers between devices  113 us (47%)
  blocking collectives  35.6 us (15%)
  local copies, waits for them, and re-layouts  31.9 us (13%)
  matrix products  30.8 us (13%)
  starting transfers between devices  20.3 us (8%)
  other arithmetic  8.87 us (4%)
    ppermute x17, waiting for transfers between devices, send(): return lax.ppermute(x, 'blk', perm)  113 us
    all_to_all x1, blocking collectives, on_device(): lax.all_to_all(projected, 'freq', split_axis=1, concat_axis=3, tiled=True)  35.6 us
    dot_general x11, matrix products, mm(): jnp.einsum('aik,bkj->abij', lhs, rhs, precision=lax.Precision.HIGH, prefe...  20.6 us
    ppermute x17, starting transfers between devices, send(): return lax.ppermute(x, 'blk', perm)  20.3 us
    dot_general x1, matrix products, on_device(): jnp.einsum('srt,tc->csr', traces, table, preferred_element_type=jnp.float32)  10.2 us
    dynamic_update_slice x10, local copies, waits for them, and re-layouts, on_device(): lax.dynamic_update_slice_in_dim(right, pc[:, i * rb:(i + 1) * rb], kblk(g...  9.59 us
  transfers between devices with their start and end apart: 17, of which 8 were waited for; matrix products, arithmetic and copies ran while one was open for 14% of the time, Pallas kernels for 0%

profile of v8, /device:TPU:1, one launch (start us, length us, event | category | flops | bytes accessed | tf_op | source)
XLA Modules:
  0.0 240.5 jit_solution(11225095265966788273)
XLA Ops:
  0.1 10.2 %convolution_bitcast_fusion = f32[2,8,128,256]{3,1,0,2:T(8,128)S(1)} fusion(bf16[128,256,256]{2,1,0:T(8,128)(2,1)} %param.2, bf16[256,8]{0,1:T(8,128)(2,1)S(1)} %get-tuple-element.54, bf16[256,8]{0,1:T(8,128)(2,1)S(1)} %get-tuple-element.53), kind=kOutput, calls=%fused_computation.21 | convolution fusion | flops 268451840 | bytes 18882560 | tf_op jit(solution)/shard_map/srt,tc->csr/dot_general | solution.py:43
  10.4 1.1 copy.10
  11.5 35.6 %all_to_all.15 = f32[2,8,128,256]{3,0,2,1:T(2,128)S(1)} all-to-all(f32[2,8,128,256]{3,0,2,1:T(2,128)S(1)} %copy.10), channel_id=1, replica_groups=mesh['freq'=8,'blk'=16] {'freq'}, dimensions={1} | all-to-all | bytes 4194304 | tf_op jit(solution)/shard_map/all_to_all | solution.py:45
  47.1 2.5 %copy.11 = f32[2,1,128,8,256]{4,3,2,0,1:T(8,128)} copy(f32[2,1,128,8,256]{4,0,2,3,1:T(2,128)S(1)} %bitcast.162) | data formatting | bytes 4194304 | tf_op jit(solution)/shard_map/all_to_all | solution.py:45
  49.6 1.7 squeeze.27
  51.3 1.8 collective-permute-start
  53.2 4.3 %broadcast_in_dim.8 = f32[2,2048,512]{2,1,0:T(8,128)} broadcast(f32[]{:T(128)} %constant.96.clone.1), dimensions={} | broadcast | bytes 8388612 | tf_op jit(solution)/shard_map/broadcast_in_dim | solution.py:119
  57.5 1.0 constant_dynamic-update-slice_fusion.13
  59.3 0.9 collective-permute-start.2
  60.2 1.1 pad_maximum_fusion.4
  61.3 10.7 %collective-permute-done.1 = f32[2,128,512]{2,1,0:T(8,128)S(1)} collective-permute-done((f32[2,128,512]{2,1,0:T(8,128)S(1)}, f32[2,128,512]{2,1,0:T(8,128)S(1)}, u32[]{:S(2)}, u32[]{:S(2)}) %collective-permute-start.1) | collective-permute-done | bytes 524320 | tf_op jit(solution)/shard_map/ppermute | solution.py:33
  72.0 11.4 %collective-permute-done.2 = f32[2,128,512]{2,1,0:T(8,128)S(1)} collective-permute-done((f32[2,128,512]{2,1,0:T(8,128)S(1)}, f32[2,128,512]{2,1,0:T(8,128)S(1)}, u32[]{:S(2)}, u32[]{:S(2)}) %collective-permute-start.2) | collective-permute-done | bytes 524320 | tf_op jit(solution)/shard_map/ppermute | solution.py:33
  84.2 1.1 pad_maximum_fusion.3
  86.5 21.8 %collective-permute-done.12 = f32[2,128,1024]{2,1,0:T(8,128)} collective-permute-done((f32[2,128,1024]{2,1,0:T(8,128)}, f32[2,128,1024]{2,1,0:T(8,128)}, u32[]{:S(2)}, u32[]{:S(2)}) %collective-permute-start.12) | collective-permute-done | bytes 1048608 | tf_op jit(solution)/shard_map/ppermute | solution.py:33
  108.3 1.0 collective-permute-start.13
  109.3 1.9 constant_dynamic-update-slice_fusion.12
  111.4 1.0 constant_dynamic-update-slice_fusion.17
  112.6 1.0 constant_dynamic-update-slice_fusion.16
  113.6 2.9 %collective-permute-start.6 = (f32[2,256,512]{2,1,0:T(8,128)S(1)}, f32[2,256,512]{2,1,0:T(8,128)S(1)}, u32[]{:S(2)}, u32[]{:S(2)}) collective-permute-start(f32[2,256,512]{2,1,0:T(8,128)S(1)} %get-tuple-element.47), channel_id=1, source_target_pairs={{0,12},{1,13},{2,14},{3,15},{4,0},{5,1},{6,2},{7,3},{8,4},{9,5},{1... | collective-permute-start | bytes 3145736 | tf_op jit(solution)/shard_map/ppermute | solution.py:33
  116.5 2.7 %collective-permute-start.4 = (f32[2,256,512]{2,1,0:T(8,128)S(1)}, f32[2,256,512]{2,1,0:T(8,128)S(1)}, u32[]{:S(2)}, u32[]{:S(2)}) collective-permute-start(f32[2,256,512]{2,1,0:T(8,128)S(1)} %pad_maximum_fusion.2), channel_id=1, source_target_pairs={{0,12},{1,13},{2,14},{3,15},{4,0},{5,1},{6,2},{7,3},{8,4},{9,5},{1... | collective-permute-start | bytes 3145736 | tf_op jit(solution)/shard_map/ppermute | solution.py:33
  119.3 1.3 slice_dynamic-update-slice_fusion.5
  120.5 1.1 slice_dynamic-update-slice_fusion.4
  121.6 1.1 slice_dynamic-update-slice_fusion.3
  122.7 1.7 constant_dynamic-update-slice_fusion.14
  124.9 1.0 fusion.22
  126.0 1.0 fusion.24
  127.1 37.4 %collective-permute-done.3 = f32[2,256,512]{2,1,0:T(8,128)S(1)} collective-permute-done((f32[2,256,512]{2,1,0:T(8,128)S(1)}, f32[2,256,512]{2,1,0:T(8,128)S(1)}, u32[]{:S(2)}, u32[]{:S(2)}) %collective-permute-start.3) | collective-permute-done | bytes 1048608 | tf_op jit(solution)/shard_map/ppermute | solution.py:33
  164.5 0.9 fusion.92
  168.0 2.7 %collective-permute-start.8 = (f32[2,128,512]{2,1,0:T(8,128)S(1)}, f32[2,128,512]{2,1,0:T(8,128)S(1)}, u32[]{:S(2)}, u32[]{:S(2)}) collective-permute-start(f32[2,128,512]{2,1,0:T(8,128)S(1)} %get-tuple-element.41), channel_id=1, source_target_pairs={{0,12},{1,13},{2,14},{3,15},{4,0},{5,1},{6,2},{7,3},{8,4},{9,5},{1... | collective-permute-start | bytes 1572872 | tf_op jit(solution)/shard_map/ppermute | solution.py:33
  171.5 0.9 slice_dynamic-update-slice_fusion.7
  174.1 2.6 %collective-permute-start.10 = (f32[2,128,512]{2,1,0:T(8,128)S(1)}, f32[2,128,512]{2,1,0:T(8,128)S(1)}, u32[]{:S(2)}, u32[]{:S(2)}) collective-permute-start(f32[2,128,512]{2,1,0:T(8,128)S(1)} %get-tuple-element.37), channel_id=1, source_target_pairs={{0,12},{1,13},{2,14},{3,15},{4,0},{5,1},{6,2},{7,3},{8,4},{9,5},{1... | collective-permute-start | bytes 1572872 | tf_op jit(solution)/shard_map/ppermute | solution.py:33
  176.7 1.0 fusion.14
  177.8 1.0 fusion.16
  178.8 1.0 fusion.18
  179.9 1.0 fusion.20
  182.6 7.6 %collective-permute-done.9 = f32[2,128,512]{2,1,0:T(8,128)S(1)} collective-permute-done((f32[2,128,512]{2,1,0:T(8,128)S(1)}, f32[2,128,512]{2,1,0:T(8,128)S(1)}, u32[]{:S(2)}, u32[]{:S(2)}) %collective-permute-start.9) | collective-permute-done | bytes 524320 | tf_op jit(solution)/shard_map/ppermute | solution.py:33
  192.5 9.3 %fusion.4 = f32[2,2,256,512]{3,2,0,1:T(8,128)S(1)} fusion(f32[2,128,2048]{2,1,0:T(8,128)S(1)} %slice_dynamic-update-slice_fusion, f32[2,128,2048]{2,1,0:T(8,128)S(1)} %slice_dynamic-update-slice_fusion.3, f32[2,2048,512]{2,1,0:T(8,128)} %constant_dynamic-update-slice_fusion.2), kind=kOutput, calls=%fused_computation.20 | convolution fusion | flops 6443499520 | bytes 14680064 | tf_op jit(solution)/shard_map/aik,bkj->abij/dot_general | solution.py:81
  201.9 1.0 fusion.53
  202.8 1.0 fusion.55
  203.8 1.0 fusion.57
  204.8 2.1 add_bitcast_fusion
  206.9 1.9 fusion.32
  208.9 1.6 fusion.28
  210.7 3.1 %collective-permute-start.16 = (f32[2,128,512]{2,1,0:T(8,128)S(1)}, f32[2,128,512]{2,1,0:T(8,128)S(1)}, u32[]{:S(2)}, u32[]{:S(2)}) collective-permute-start(f32[2,128,512]{2,1,0:T(8,128)S(1)} %get-tuple-element.32), channel_id=1, source_target_pairs={{0,3},{1,2},{2,1},{3,0},{4,7},{5,6},{6,5},{7,4},{8,11},{9,10},{10,... | collective-permute-start | bytes 1572872 | tf_op jit(solution)/shard_map/ppermute | solution.py:33
  214.4 11.8 %collective-permute-done.16 = f32[2,128,512]{2,1,0:T(8,128)S(1)} collective-permute-done((f32[2,128,512]{2,1,0:T(8,128)S(1)}, f32[2,128,512]{2,1,0:T(8,128)S(1)}, u32[]{:S(2)}, u32[]{:S(2)}) %collective-permute-start.16) | collective-permute-done | bytes 524320 | tf_op jit(solution)/shard_map/ppermute | solution.py:33
  226.2 11.3 %collective-permute-done.15 = f32[2,128,512]{2,1,0:T(8,128)S(1)} collective-permute-done((f32[2,128,512]{2,1,0:T(8,128)S(1)}, f32[2,128,512]{2,1,0:T(8,128)S(1)}, u32[]{:S(2)}, u32[]{:S(2)}) %collective-permute-start.15) | collective-permute-done | bytes 524320 | tf_op jit(solution)/shard_map/ppermute | solution.py:33
  237.5 1.2 pad_maximum_fusion
  239.0 1.5 maximum_bitcast_fusion.2
  (47 shorter events, 14.2 us)
Async XLA Ops:
  51.3 58.0 %collective-permute-start = (f32[2,128,2048]{2,1,0:T(8,128)S(1)}, f32[2,128,2048]{2,1,0:T(8,128)}, u32[]{:S(2)}, u32[]{:S(2)}) collective-permute-start(f32[2,128,2048]{2,1,0:T(8,128)S(1)} %squeeze.27), channel_id=1, source_target_pairs={{0,1},{1,0},{2,3},{3,2},{4,5},{5,4},{6,7},{7,6},{8,9},{9,8},{10,11... | collective-permute-start | bytes 6291464 | tf_op jit(solution)/shard_map/ppermute | solution.py:33
  58.5 13.4 %collective-permute-start.1 = (f32[2,128,512]{2,1,0:T(8,128)S(1)}, f32[2,128,512]{2,1,0:T(8,128)S(1)}, u32[]{:S(2)}, u32[]{:S(2)}) collective-permute-start(f32[2,128,512]{2,1,0:T(8,128)S(1)} %get-tuple-element.36), channel_id=1, source_target_pairs={{0,2},{1,3},{2,0},{3,1},{4,6},{5,7},{6,4},{7,5},{8,10},{9,11},{10,... | collective-permute-start | bytes 1572872 | tf_op jit(solution)/shard_map/ppermute | solution.py:33
  59.3 24.1 %collective-permute-start.2 = (f32[2,128,512]{2,1,0:T(8,128)S(1)}, f32[2,128,512]{2,1,0:T(8,128)S(1)}, u32[]{:S(2)}, u32[]{:S(2)}) collective-permute-start(f32[2,128,512]{2,1,0:T(8,128)S(1)} %get-tuple-element.35), channel_id=1, source_target_pairs={{0,3},{1,2},{2,1},{3,0},{4,7},{5,6},{6,5},{7,4},{8,11},{9,10},{10,... | collective-permute-start | bytes 1572872 | tf_op jit(solution)/shard_map/ppermute | solution.py:33
  60.2 25.5 %copy-start.2 = (f32[1,2]{1,0:T(1,128)S(1)}, f32[1,2]{1,0:T(1,128)}, u32[]{:S(2)}) copy-start(f32[1,2]{1,0:T(1,128)} %param.3) | copy-start | bytes 28
  72.0 12.2 %copy-start = (f32[2,128,512]{2,1,0:T(8,128)}, f32[2,128,512]{2,1,0:T(8,128)S(1)}, u32[]{:S(2)}) copy-start(f32[2,128,512]{2,1,0:T(8,128)S(1)} %collective-permute-done.1) | copy-start | bytes 1572868
  83.4 24.9 %collective-permute-start.12 = (f32[2,128,1024]{2,1,0:T(8,128)}, f32[2,128,1024]{2,1,0:T(8,128)}, u32[]{:S(2)}, u32[]{:S(2)}) collective-permute-start(f32[2,128,1024]{2,1,0:T(8,128)} %pad_maximum_fusion.4), channel_id=1, source_target_pairs={{0,2},{1,3},{2,0},{3,1},{4,6},{5,7},{6,4},{7,5},{8,10},{9,11},{10,... | collective-permute-start | bytes 3145736 | tf_op jit(solution)/shard_map/ppermute | solution.py:33
  85.2 34.0 %collective-permute-start.11 = (f32[2,128,1024]{2,1,0:T(8,128)}, f32[2,128,1024]{2,1,0:T(8,128)}, u32[]{:S(2)}, u32[]{:S(2)}) collective-permute-start(f32[2,128,1024]{2,1,0:T(8,128)} %pad_maximum_fusion.3), channel_id=1, source_target_pairs={{0,1},{1,0},{2,3},{3,2},{4,5},{5,4},{6,7},{7,6},{8,9},{9,8},{10,11... | collective-permute-start | bytes 3145736 | tf_op jit(solution)/shard_map/ppermute | solution.py:33
  86.5 24.9 %copy-start.1 = (f32[2,128,512]{2,1,0:T(8,128)S(1)}, f32[2,128,512]{2,1,0:T(8,128)}, u32[]{:S(2)}) copy-start(f32[2,128,512]{2,1,0:T(8,128)} %copy-done) | copy-start | bytes 1572868
  108.3 18.7 %collective-permute-start.13 = (f32[2,128,1024]{2,1,0:T(8,128)}, f32[2,128,1024]{2,1,0:T(8,128)S(1)}, u32[]{:S(2)}, u32[]{:S(2)}) collective-permute-start(f32[2,128,1024]{2,1,0:T(8,128)} %collective-permute-done.12), channel_id=1, source_target_pairs={{0,1},{1,0},{2,3},{3,2},{4,5},{5,4},{6,7},{7,6},{8,9},{9,8},{10,11... | collective-permute-start | bytes 3145736 | tf_op jit(solution)/shard_map/ppermute | solution.py:33
  113.6 58.8 %collective-permute-start.6 = (f32[2,256,512]{2,1,0:T(8,128)S(1)}, f32[2,256,512]{2,1,0:T(8,128)S(1)}, u32[]{:S(2)}, u32[]{:S(2)}) collective-permute-start(f32[2,256,512]{2,1,0:T(8,128)S(1)} %get-tuple-element.47), channel_id=1, source_target_pairs={{0,12},{1,13},{2,14},{3,15},{4,0},{5,1},{6,2},{7,3},{8,4},{9,5},{1... | collective-permute-start | bytes 3145736 | tf_op jit(solution)/shard_map/ppermute | solution.py:33
  116.4 54.2 %collective-permute-start.5 = (f32[2,256,512]{2,1,0:T(8,128)S(1)}, f32[2,256,512]{2,1,0:T(8,128)S(1)}, u32[]{:S(2)}, u32[]{:S(2)}) collective-permute-start(f32[2,256,512]{2,1,0:T(8,128)S(1)} %get-tuple-element.47), channel_id=1, source_target_pairs={{0,4},{1,5},{2,6},{3,7},{4,8},{5,9},{6,10},{7,11},{8,12},{9,13},{1... | collective-permute-start | bytes 3145736 | tf_op jit(solution)/shard_map/ppermute | solution.py:33
  116.5 49.8 %collective-permute-start.4 = (f32[2,256,512]{2,1,0:T(8,128)S(1)}, f32[2,256,512]{2,1,0:T(8,128)S(1)}, u32[]{:S(2)}, u32[]{:S(2)}) collective-permute-start(f32[2,256,512]{2,1,0:T(8,128)S(1)} %pad_maximum_fusion.2), channel_id=1, source_target_pairs={{0,12},{1,13},{2,14},{3,15},{4,0},{5,1},{6,2},{7,3},{8,4},{9,5},{1... | collective-permute-start | bytes 3145736 | tf_op jit(solution)/shard_map/ppermute | solution.py:33
  119.3 45.3 %collective-permute-start.3 = (f32[2,256,512]{2,1,0:T(8,128)S(1)}, f32[2,256,512]{2,1,0:T(8,128)S(1)}, u32[]{:S(2)}, u32[]{:S(2)}) collective-permute-start(f32[2,256,512]{2,1,0:T(8,128)S(1)} %pad_maximum_fusion.2), channel_id=1, source_target_pairs={{0,4},{1,5},{2,6},{3,7},{4,8},{5,9},{6,10},{7,11},{8,12},{9,13},{1... | collective-permute-start | bytes 3145736 | tf_op jit(solution)/shard_map/ppermute | solution.py:33
  165.4 15.5 %collective-permute-start.7 = (f32[2,128,512]{2,1,0:T(8,128)S(1)}, f32[2,128,512]{2,1,0:T(8,128)S(1)}, u32[]{:S(2)}, u32[]{:S(2)}) collective-permute-start(f32[2,128,512]{2,1,0:T(8,128)S(1)} %get-tuple-element.43), channel_id=1, source_target_pairs={{0,4},{1,5},{2,6},{3,7},{4,8},{5,9},{6,10},{7,11},{8,12},{9,13},{1... | collective-permute-start | bytes 1572872 | tf_op jit(solution)/shard_map/ppermute | solution.py:33
  168.0 13.8 %collective-permute-start.8 = (f32[2,128,512]{2,1,0:T(8,128)S(1)}, f32[2,128,512]{2,1,0:T(8,128)S(1)}, u32[]{:S(2)}, u32[]{:S(2)}) collective-permute-start(f32[2,128,512]{2,1,0:T(8,128)S(1)} %get-tuple-element.41), channel_id=1, source_target_pairs={{0,12},{1,13},{2,14},{3,15},{4,0},{5,1},{6,2},{7,3},{8,4},{9,5},{1... | collective-permute-start | bytes 1572872 | tf_op jit(solution)/shard_map/ppermute | solution.py:33
  171.5 18.7 %collective-permute-start.9 = (f32[2,128,512]{2,1,0:T(8,128)S(1)}, f32[2,128,512]{2,1,0:T(8,128)S(1)}, u32[]{:S(2)}, u32[]{:S(2)}) collective-permute-start(f32[2,128,512]{2,1,0:T(8,128)S(1)} %get-tuple-element.39), channel_id=1, source_target_pairs={{0,4},{1,5},{2,6},{3,7},{4,8},{5,9},{6,10},{7,11},{8,12},{9,13},{1... | collective-permute-start | bytes 1572872 | tf_op jit(solution)/shard_map/ppermute | solution.py:33
  174.1 17.6 %collective-permute-start.10 = (f32[2,128,512]{2,1,0:T(8,128)S(1)}, f32[2,128,512]{2,1,0:T(8,128)S(1)}, u32[]{:S(2)}, u32[]{:S(2)}) collective-permute-start(f32[2,128,512]{2,1,0:T(8,128)S(1)} %get-tuple-element.37), channel_id=1, source_target_pairs={{0,12},{1,13},{2,14},{3,15},{4,0},{5,1},{6,2},{7,3},{8,4},{9,5},{1... | collective-permute-start | bytes 1572872 | tf_op jit(solution)/shard_map/ppermute | solution.py:33
  210.7 15.5 %collective-permute-start.16 = (f32[2,128,512]{2,1,0:T(8,128)S(1)}, f32[2,128,512]{2,1,0:T(8,128)S(1)}, u32[]{:S(2)}, u32[]{:S(2)}) collective-permute-start(f32[2,128,512]{2,1,0:T(8,128)S(1)} %get-tuple-element.32), channel_id=1, source_target_pairs={{0,3},{1,2},{2,1},{3,0},{4,7},{5,6},{6,5},{7,4},{8,11},{9,10},{10,... | collective-permute-start | bytes 1572872 | tf_op jit(solution)/shard_map/ppermute | solution.py:33
  213.8 23.7 %collective-permute-start.15 = (f32[2,128,512]{2,1,0:T(8,128)S(1)}, f32[2,128,512]{2,1,0:T(8,128)S(1)}, u32[]{:S(2)}, u32[]{:S(2)}) collective-permute-start(f32[2,128,512]{2,1,0:T(8,128)S(1)} %get-tuple-element.33), channel_id=1, source_target_pairs={{0,2},{1,3},{2,0},{3,1},{4,6},{5,7},{6,4},{7,5},{8,10},{9,11},{10,... | collective-permute-start | bytes 1572872 | tf_op jit(solution)/shard_map/ppermute | solution.py:33
  214.4 23.1 %collective-permute-start.14 = (f32[2,128,512]{2,1,0:T(8,128)S(1)}, f32[2,128,512]{2,1,0:T(8,128)}, u32[]{:S(2)}, u32[]{:S(2)}) collective-permute-start(f32[2,128,512]{2,1,0:T(8,128)S(1)} %get-tuple-element.31), channel_id=1, source_target_pairs={{0,1},{1,0},{2,3},{3,2},{4,5},{5,4},{6,7},{7,6},{8,9},{9,8},{10,11... | collective-permute-start | bytes 1572872 | tf_op jit(solution)/shard_map/ppermute | solution.py:33

commit v9 on v5

--- a/solution.py
+++ b/solution.py
@@ -40,10 +40,11 @@
     ny = nblk // GROUP
     assert ny == 4 and nblk % GROUP == 0
     table = make_table(freqs, samples)
+    table = table.reshape(samples, 2, freqs).transpose(0, 2, 1).reshape(samples, 2 * freqs)
     projected = jnp.einsum("srt,tc->csr", traces, table, preferred_element_type=jnp.float32)
-    projected = projected.reshape(2, freqs, src_rows, rec_cols)
-    spectra = lax.all_to_all(projected, "freq", split_axis=1, concat_axis=3, tiled=True)
-    own = spectra[:, 0]
+    projected = projected.reshape(freqs, 2, src_rows, rec_cols)
+    spectra = lax.all_to_all(projected, "freq", split_axis=0, concat_axis=3, tiled=True)
+    own = spectra[0]
     n = own.shape[2]
     rb = src_rows
     cw = n // GROUP

time: 208 us -> 208 us (level)
  no operation moved by 1% of the time
where the time goes in v9:
time: 208 us; the launch traced here: 207 us
  waiting for transfers between devices  85.7 us (41%)
  blocking collectives  35.6 us (17%)
  local copies, waits for them, and re-layouts  31.2 us (15%)
  matrix products  28.8 us (14%)
  starting transfers between devices  18 us (9%)
  other arithmetic  7.6 us (4%)
    ppermute x14, waiting for transfers between devices, send(): return lax.ppermute(x, 'blk', perm)  85.7 us
    all_to_all x1, blocking collectives, on_device(): lax.all_to_all(projected, 'freq', split_axis=0, concat_axis=3, tiled=True)  35.6 us
    dot_general x9, matrix products, mm(): jnp.einsum('aik,bkj->abij', lhs, rhs, precision=lax.Precision.HIGH, prefe...  18.6 us
    ppermute x14, starting transfers between devices, send(): return lax.ppermute(x, 'blk', perm)  18 us
    dynamic_update_slice x14, local copies, waits for them, and re-layouts, on_device(): lax.dynamic_update_slice_in_dim(right, pc[:, i * rb:(i + 1) * rb], kblk(g...  13.1 us
    dot_general x1, matrix products, on_device(): jnp.einsum('srt,tc->csr', traces, table, preferred_element_type=jnp.float32)  10.2 us
    broadcast_in_dim x1, local copies, waits for them, and re-layouts, on_device(): right = jnp.zeros((2, n, cw), jnp.float32)  4.35 us
  transfers between devices with their start and end apart: 14, of which 8 were waited for; matrix products, arithmetic and copies ran while one was open for 16% of the time, Pallas kernels for 0%

profile of v9, /device:TPU:1, one launch (start us, length us, event | category | flops | bytes accessed | tf_op | source)
XLA Modules:
  0.0 207.1 jit_solution(13477636555155044063)
XLA Ops:
  0.2 10.2 %fusion = f32[8,2,128,256]{3,0,2,1:T(8,128)S(1)} fusion(bf16[128,256,256]{2,1,0:T(8,128)(2,1)} %param.2, bf16[8,2,256,1]{2,1,0,3:T(2,128)(2,1)S(1)} %bitcast.150), kind=kOutput, calls=%fused_computation | convolution fusion | flops 268435456 | bytes 18882560 | tf_op jit(solution)/shard_map/srt,tc->csr/dot_general | solution.py:44
  11.1 35.6 %all_to_all.15 = f32[8,2,128,256]{3,2,1,0:T(8,128)S(1)} all-to-all(f32[8,2,128,256]{3,2,1,0:T(8,128)S(1)} %copy.27), channel_id=1, replica_groups=mesh['freq'=8,'blk'=16] {'freq'}, dimensions={0} | all-to-all | bytes 4194304 | tf_op jit(solution)/shard_map/all_to_all | solution.py:46
  46.7 2.5 %copy.28 = f32[1,2,128,8,256]{4,3,2,1,0:T(8,128)} copy(f32[1,2,128,8,256]{4,2,1,3,0:T(8,128)S(1)} %bitcast.147) | data formatting | bytes 4194304 | tf_op jit(solution)/shard_map/all_to_all | solution.py:46
  49.2 1.7 squeeze.27
  50.9 1.8 collective-permute-start
  52.8 4.3 %broadcast_in_dim.11 = f32[2,2048,512]{2,1,0:T(8,128)} broadcast(f32[]{:T(128)} %constant.92.clone.1), dimensions={} | broadcast | bytes 8388612 | tf_op jit(solution)/shard_map/broadcast_in_dim | solution.py:109
  57.1 1.2 constant_dynamic-update-slice_fusion.4
  59.0 1.0 collective-permute-start.2
  60.0 1.2 pad_maximum_fusion.1
  61.3 10.4 %collective-permute-done.1 = f32[2,128,512]{2,1,0:T(8,128)S(1)} collective-permute-done((f32[2,128,512]{2,1,0:T(8,128)S(1)}, f32[2,128,512]{2,1,0:T(8,128)S(1)}, u32[]{:S(2)}, u32[]{:S(2)}) %collective-permute-start.1) | collective-permute-done | bytes 524320 | tf_op jit(solution)/shard_map/ppermute | solution.py:33
  71.7 11.5 %collective-permute-done.2 = f32[2,128,512]{2,1,0:T(8,128)S(1)} collective-permute-done((f32[2,128,512]{2,1,0:T(8,128)S(1)}, f32[2,128,512]{2,1,0:T(8,128)S(1)}, u32[]{:S(2)}, u32[]{:S(2)}) %collective-permute-start.2) | collective-permute-done | bytes 524320 | tf_op jit(solution)/shard_map/ppermute | solution.py:33
  84.7 2.0 constant_dynamic-update-slice_fusion.3
  86.7 1.4 collective-permute-start.3
  88.1 1.6 collective-permute-start.4
  89.9 1.0 constant_dynamic-update-slice_fusion.8
  90.9 0.9 constant_dynamic-update-slice_fusion.7
  91.8 2.7 %collective-permute-start.6 = (f32[2,256,512]{2,1,0:T(8,128)S(1)}, f32[2,256,512]{2,1,0:T(8,128)S(1)}, u32[]{:S(2)}, u32[]{:S(2)}) collective-permute-start(f32[2,256,512]{2,1,0:T(8,128)S(1)} %get-tuple-element.43), channel_id=1, source_target_pairs={{0,12},{1,13},{2,14},{3,15},{4,0},{5,1},{6,2},{7,3},{8,4},{9,5},{1... | collective-permute-start | bytes 3145736 | tf_op jit(solution)/shard_map/ppermute | solution.py:33
  94.5 24.8 %collective-permute-done.9 = f32[2,128,1536]{2,1,0:T(8,128)} collective-permute-done((f32[2,128,1536]{2,1,0:T(8,128)}, f32[2,128,1536]{2,1,0:T(8,128)}, u32[]{:S(2)}, u32[]{:S(2)}) %collective-permute-start.9) | collective-permute-done | bytes 1572896 | tf_op jit(solution)/shard_map/ppermute | solution.py:33
  119.3 1.1 slice_dynamic-update-slice_fusion.2
  120.4 1.1 slice_dynamic-update-slice_fusion.1
  121.5 1.1 slice_dynamic-update-slice_fusion
  122.6 1.3 collective-permute-start.10
  123.8 1.7 constant_dynamic-update-slice_fusion.5
  126.2 1.0 fusion.30
  127.2 1.0 fusion.32
  128.3 1.4 collective-permute-start.7
  131.3 0.8 slice_dynamic-update-slice_fusion.12
  133.0 2.0 collective-permute-done.5
  135.0 0.9 slice_dynamic-update-slice_fusion.10
  135.9 0.9 slice_dynamic-update-slice_fusion.9
  136.8 1.2 collective-permute-start.8
  138.0 1.0 fusion.22
  139.0 1.0 fusion.24
  140.1 0.8 slice_dynamic-update-slice_fusion.8
  140.9 1.0 fusion.26
  142.7 1.0 fusion.28
  143.8 13.7 %collective-permute-done.7 = f32[2,256,512]{2,1,0:T(8,128)S(1)} collective-permute-done((f32[2,256,512]{2,1,0:T(8,128)S(1)}, f32[2,256,512]{2,1,0:T(8,128)S(1)}, u32[]{:S(2)}, u32[]{:S(2)}) %collective-permute-start.7) | collective-permute-done | bytes 1048608 | tf_op jit(solution)/shard_map/ppermute | solution.py:33
  161.2 9.3 %fusion.6 = f32[2,2,256,512]{3,2,0,1:T(8,128)S(1)} fusion(f32[2,128,2048]{2,1,0:T(8,128)S(1)} %collective-permute-done.10, f32[2,128,2048]{2,1,0:T(8,128)S(1)} %slice_dynamic-update-slice_fusion, f32[2,2048,512]{2,1,0:T(8,128)} %slice_dynamic-update-slice_fusion.3), kind=kOutput, calls=%fused_computation.22 | convolution fusion | flops 6443499520 | bytes 14680064 | tf_op jit(solution)/shard_map/aik,bkj->abij/dot_general | solution.py:72
  170.5 1.0 fusion.20
  171.5 2.0 add_bitcast_fusion
  173.6 1.8 fusion.40
  175.4 1.4 fusion.36
  177.0 3.3 %collective-permute-start.13 = (f32[2,128,512]{2,1,0:T(8,128)S(1)}, f32[2,128,512]{2,1,0:T(8,128)S(1)}, u32[]{:S(2)}, u32[]{:S(2)}) collective-permute-start(f32[2,128,512]{2,1,0:T(8,128)S(1)} %get-tuple-element.36), channel_id=1, source_target_pairs={{0,3},{1,2},{2,1},{3,0},{4,7},{5,6},{6,5},{7,4},{8,11},{9,10},{10,... | collective-permute-start | bytes 1572872 | tf_op jit(solution)/shard_map/ppermute | solution.py:33
  180.3 0.9 collective-permute-start.12
  181.3 11.2 %collective-permute-done.13 = f32[2,128,512]{2,1,0:T(8,128)S(1)} collective-permute-done((f32[2,128,512]{2,1,0:T(8,128)S(1)}, f32[2,128,512]{2,1,0:T(8,128)S(1)}, u32[]{:S(2)}, u32[]{:S(2)}) %collective-permute-start.13) | collective-permute-done | bytes 524320 | tf_op jit(solution)/shard_map/ppermute | solution.py:33
  192.5 11.6 %collective-permute-done.12 = f32[2,128,512]{2,1,0:T(8,128)S(1)} collective-permute-done((f32[2,128,512]{2,1,0:T(8,128)S(1)}, f32[2,128,512]{2,1,0:T(8,128)S(1)}, u32[]{:S(2)}, u32[]{:S(2)}) %collective-permute-start.12) | collective-permute-done | bytes 524320 | tf_op jit(solution)/shard_map/ppermute | solution.py:33
  204.1 1.2 pad_maximum_fusion
  205.6 1.5 maximum_bitcast_fusion.2
  (39 shorter events, 11.5 us)
Async XLA Ops:
  50.9 33.7 %collective-permute-start = (f32[2,128,2048]{2,1,0:T(8,128)S(1)}, f32[2,128,2048]{2,1,0:T(8,128)}, u32[]{:S(2)}, u32[]{:S(2)}) collective-permute-start(f32[2,128,2048]{2,1,0:T(8,128)S(1)} %squeeze.27), channel_id=1, source_target_pairs={{0,1},{1,0},{2,3},{3,2},{4,5},{5,4},{6,7},{7,6},{8,9},{9,8},{10,11... | collective-permute-start | bytes 6291464 | tf_op jit(solution)/shard_map/ppermute | solution.py:33
  58.3 25.6 %copy-start.2 = (f32[1,2]{1,0:T(1,128)S(1)}, f32[1,2]{1,0:T(1,128)}, u32[]{:S(2)}) copy-start(f32[1,2]{1,0:T(1,128)} %param.3) | copy-start | bytes 28
  58.3 13.4 %collective-permute-start.1 = (f32[2,128,512]{2,1,0:T(8,128)S(1)}, f32[2,128,512]{2,1,0:T(8,128)S(1)}, u32[]{:S(2)}, u32[]{:S(2)}) collective-permute-start(f32[2,128,512]{2,1,0:T(8,128)S(1)} %get-tuple-element.42), channel_id=1, source_target_pairs={{0,2},{1,3},{2,0},{3,1},{4,6},{5,7},{6,4},{7,5},{8,10},{9,11},{10,... | collective-permute-start | bytes 1572872 | tf_op jit(solution)/shard_map/ppermute | solution.py:33
  59.0 24.1 %collective-permute-start.2 = (f32[2,128,512]{2,1,0:T(8,128)S(1)}, f32[2,128,512]{2,1,0:T(8,128)S(1)}, u32[]{:S(2)}, u32[]{:S(2)}) collective-permute-start(f32[2,128,512]{2,1,0:T(8,128)S(1)} %get-tuple-element.41), channel_id=1, source_target_pairs={{0,3},{1,2},{2,1},{3,0},{4,7},{5,6},{6,5},{7,4},{8,11},{9,10},{10,... | collective-permute-start | bytes 1572872 | tf_op jit(solution)/shard_map/ppermute | solution.py:33
  71.7 11.5 %copy-start = (f32[2,128,512]{2,1,0:T(8,128)}, f32[2,128,512]{2,1,0:T(8,128)S(1)}, u32[]{:S(2)}) copy-start(f32[2,128,512]{2,1,0:T(8,128)S(1)} %collective-permute-done.1) | copy-start | bytes 1572868
  83.2 36.1 %collective-permute-start.9 = (f32[2,128,1536]{2,1,0:T(8,128)}, f32[2,128,1536]{2,1,0:T(8,128)}, u32[]{:S(2)}, u32[]{:S(2)}) collective-permute-start(f32[2,128,1536]{2,1,0:T(8,128)} %pad_maximum_fusion.1), channel_id=1, source_target_pairs={{0,2},{1,3},{2,0},{3,1},{4,6},{5,7},{6,4},{7,5},{8,10},{9,11},{10,... | collective-permute-start | bytes 4718600 | tf_op jit(solution)/shard_map/ppermute | solution.py:33
  86.6 3.3 %copy-start.1 = (f32[2,128,512]{2,1,0:T(8,128)S(1)}, f32[2,128,512]{2,1,0:T(8,128)}, u32[]{:S(2)}) copy-start(f32[2,128,512]{2,1,0:T(8,128)} %copy-done) | copy-start | bytes 1572868
  86.7 41.6 %collective-permute-start.3 = (f32[2,256,512]{2,1,0:T(8,128)S(1)}, f32[2,256,512]{2,1,0:T(8,128)S(1)}, u32[]{:S(2)}, u32[]{:S(2)}) collective-permute-start(f32[2,256,512]{2,1,0:T(8,128)S(1)} %pad_maximum_fusion.3), channel_id=1, source_target_pairs={{0,4},{1,5},{2,6},{3,7},{4,8},{5,9},{6,10},{7,11},{8,12},{9,13},{1... | collective-permute-start | bytes 3145736 | tf_op jit(solution)/shard_map/ppermute | solution.py:33
  88.1 43.2 %collective-permute-start.4 = (f32[2,256,512]{2,1,0:T(8,128)S(1)}, f32[2,256,512]{2,1,0:T(8,128)S(1)}, u32[]{:S(2)}, u32[]{:S(2)}) collective-permute-start(f32[2,256,512]{2,1,0:T(8,128)S(1)} %pad_maximum_fusion.3), channel_id=1, source_target_pairs={{0,12},{1,13},{2,14},{3,15},{4,0},{5,1},{6,2},{7,3},{8,4},{9,5},{1... | collective-permute-start | bytes 3145736 | tf_op jit(solution)/shard_map/ppermute | solution.py:33
  91.8 43.2 %collective-permute-start.5 = (f32[2,256,512]{2,1,0:T(8,128)S(1)}, f32[2,256,512]{2,1,0:T(8,128)S(1)}, u32[]{:S(2)}, u32[]{:S(2)}) collective-permute-start(f32[2,256,512]{2,1,0:T(8,128)S(1)} %get-tuple-element.43), channel_id=1, source_target_pairs={{0,4},{1,5},{2,6},{3,7},{4,8},{5,9},{6,10},{7,11},{8,12},{9,13},{1... | collective-permute-start | bytes 3145736 | tf_op jit(solution)/shard_map/ppermute | solution.py:33
  91.8 44.9 %collective-permute-start.6 = (f32[2,256,512]{2,1,0:T(8,128)S(1)}, f32[2,256,512]{2,1,0:T(8,128)S(1)}, u32[]{:S(2)}, u32[]{:S(2)}) collective-permute-start(f32[2,256,512]{2,1,0:T(8,128)S(1)} %get-tuple-element.43), channel_id=1, source_target_pairs={{0,12},{1,13},{2,14},{3,15},{4,0},{5,1},{6,2},{7,3},{8,4},{9,5},{1... | collective-permute-start | bytes 3145736 | tf_op jit(solution)/shard_map/ppermute | solution.py:33
  122.6 38.6 %collective-permute-start.10 = (f32[2,128,2048]{2,1,0:T(8,128)S(1)}, f32[2,128,2048]{2,1,0:T(8,128)S(1)}, u32[]{:S(2)}, u32[]{:S(2)}) collective-permute-start(f32[2,128,2048]{2,1,0:T(8,128)S(1)} %slice_dynamic-update-slice_fusion), channel_id=1, source_target_pairs={{0,1},{1,0},{2,3},{3,2},{4,5},{5,4},{6,7},{7,6},{8,9},{9,8},{10,11... | collective-permute-start | bytes 6291464 | tf_op jit(solution)/shard_map/ppermute | solution.py:33
  128.3 29.2 %collective-permute-start.7 = (f32[2,256,512]{2,1,0:T(8,128)S(1)}, f32[2,256,512]{2,1,0:T(8,128)S(1)}, u32[]{:S(2)}, u32[]{:S(2)}) collective-permute-start(f32[2,256,512]{2,1,0:T(8,128)S(1)} %collective-permute-done.3), channel_id=1, source_target_pairs={{0,4},{1,5},{2,6},{3,7},{4,8},{5,9},{6,10},{7,11},{8,12},{9,13},{1... | collective-permute-start | bytes 3145736 | tf_op jit(solution)/shard_map/ppermute | solution.py:33
  136.8 22.8 %collective-permute-start.8 = (f32[2,256,512]{2,1,0:T(8,128)S(1)}, f32[2,256,512]{2,1,0:T(8,128)S(1)}, u32[]{:S(2)}, u32[]{:S(2)}) collective-permute-start(f32[2,256,512]{2,1,0:T(8,128)S(1)} %collective-permute-done.6), channel_id=1, source_target_pairs={{0,12},{1,13},{2,14},{3,15},{4,0},{5,1},{6,2},{7,3},{8,4},{9,5},{1... | collective-permute-start | bytes 3145736 | tf_op jit(solution)/shard_map/ppermute | solution.py:33
  177.0 15.5 %collective-permute-start.13 = (f32[2,128,512]{2,1,0:T(8,128)S(1)}, f32[2,128,512]{2,1,0:T(8,128)S(1)}, u32[]{:S(2)}, u32[]{:S(2)}) collective-permute-start(f32[2,128,512]{2,1,0:T(8,128)S(1)} %get-tuple-element.36), channel_id=1, source_target_pairs={{0,3},{1,2},{2,1},{3,0},{4,7},{5,6},{6,5},{7,4},{8,11},{9,10},{10,... | collective-permute-start | bytes 1572872 | tf_op jit(solution)/shard_map/ppermute | solution.py:33
  180.3 23.7 %collective-permute-start.12 = (f32[2,128,512]{2,1,0:T(8,128)S(1)}, f32[2,128,512]{2,1,0:T(8,128)S(1)}, u32[]{:S(2)}, u32[]{:S(2)}) collective-permute-start(f32[2,128,512]{2,1,0:T(8,128)S(1)} %get-tuple-element.37), channel_id=1, source_target_pairs={{0,2},{1,3},{2,0},{3,1},{4,6},{5,7},{6,4},{7,5},{8,10},{9,11},{10,... | collective-permute-start | bytes 1572872 | tf_op jit(solution)/shard_map/ppermute | solution.py:33
  181.3 22.8 %collective-permute-start.11 = (f32[2,128,512]{2,1,0:T(8,128)S(1)}, f32[2,128,512]{2,1,0:T(8,128)}, u32[]{:S(2)}, u32[]{:S(2)}) collective-permute-start(f32[2,128,512]{2,1,0:T(8,128)S(1)} %get-tuple-element.35), channel_id=1, source_target_pairs={{0,1},{1,0},{2,3},{3,2},{4,5},{5,4},{6,7},{7,6},{8,9},{9,8},{10,11... | collective-permute-start | bytes 1572872 | tf_op jit(solution)/shard_map/ppermute | solution.py:33

commit v10 on v9

--- a/solution.py
+++ b/solution.py
@@ -43,8 +43,15 @@
     table = table.reshape(samples, 2, freqs).transpose(0, 2, 1).reshape(samples, 2 * freqs)
     projected = jnp.einsum("srt,tc->csr", traces, table, preferred_element_type=jnp.float32)
     projected = projected.reshape(freqs, 2, src_rows, rec_cols)
-    spectra = lax.all_to_all(projected, "freq", split_axis=0, concat_axis=3, tiled=True)
-    own = spectra[0]
+    f = lax.axis_index("freq")
+    own = jnp.zeros((2, src_rows, freqs * rec_cols), jnp.float32)
+    own = lax.dynamic_update_slice_in_dim(
+        own, lax.dynamic_index_in_dim(projected, f, 0, keepdims=False), f * rec_cols, axis=2
+    )
+    for k in range(1, freqs):
+        chunk = lax.dynamic_index_in_dim(projected, (f + k) % freqs, 0, keepdims=False)
+        got = lax.ppermute(chunk, "freq", shift_perm(freqs, k))
+        own = lax.dynamic_update_slice_in_dim(own, got, ((f - k) % freqs) * rec_cols, axis=2)
     n = own.shape[2]
     rb = src_rows
     cw = n // GROUP

time: 208 us -> 206 us (level)
  blocking collectives: 35.6 us -> 0 us
  starting transfers between devices: 18 us -> 33 us
  waiting for transfers between devices: 85.7 us -> 97 us
  other arithmetic: 7.6 us -> 12.6 us
    all_to_all x1 -> x0, blocking collectives: 35.6 us -> none  [on_device(): lax.all_to_all(projected, 'freq', split_axis=0, concat_axis=3, tiled=True)]
    ppermute x0 -> x7, starting transfers between devices: none -> 15 us  [on_device(): got = lax.ppermute(chunk, 'freq', shift_perm(freqs, k))]
    ppermute x0 -> x7, waiting for transfers between devices: none -> 12.5 us  [on_device(): got = lax.ppermute(chunk, 'freq', shift_perm(freqs, k))]
    unnamed x8 -> x14, local copies, waits for them, and re-layouts: 1.15 us -> 5.3 us
    concatenate x0 -> x3, other arithmetic: none -> 3.99 us  [on_device(): early = jnp.concatenate([own, q1], axis=1)]
    dynamic_update_slice x0 -> x8, local copies, waits for them, and re-layouts: none -> 3.04 us  [the longest x7 3.01 us: on_device(): lax.dynamic_update_slice_in_dim(own, got, (f - k) % freqs * rec_cols, axi...]
    all_to_all x1 -> x0, local copies, waits for them, and re-layouts: 2.54 us -> none  [on_device(): lax.all_to_all(projected, 'freq', split_axis=0, concat_axis=3, tiled=True)]
  transfers between devices with their start and end apart: 14 -> 21, of which waited for: 8 -> 13; matrix products, arithmetic and copies ran while one was open for 16% -> 20% of each run, Pallas kernels for 0% -> 0%
where the time goes in v10:
time: 206 us; the launch traced here: 205 us
  waiting for transfers between devices  97 us (47%)
  starting transfers between devices  33 us (16%)
  local copies, waits for them, and re-layouts  32.9 us (16%)
  matrix products  29.2 us (14%)
  other arithmetic  12.6 us (6%)
    ppermute x14, waiting for transfers between devices, send(): return lax.ppermute(x, 'blk', perm)  84.5 us
    dot_general x9, matrix products, mm(): jnp.einsum('aik,bkj->abij', lhs, rhs, precision=lax.Precision.HIGH, prefe...  19 us
    ppermute x14, starting transfers between devices, send(): return lax.ppermute(x, 'blk', perm)  18 us
    ppermute x7, starting transfers between devices, on_device(): got = lax.ppermute(chunk, 'freq', shift_perm(freqs, k))  15 us
    dynamic_update_slice x14, local copies, waits for them, and re-layouts, on_device(): lax.dynamic_update_slice_in_dim(right, pc[:, i * rb:(i + 1) * rb], kblk(g...  13.2 us
    ppermute x7, waiting for transfers between devices, on_device(): got = lax.ppermute(chunk, 'freq', shift_perm(freqs, k))  12.5 us
    dot_general x1, matrix products, on_device(): jnp.einsum('srt,tc->csr', traces, table, preferred_element_type=jnp.float32)  10.2 us
    unnamed x14, local copies, waits for them, and re-layouts  5.3 us
  transfers between devices with their start and end apart: 21, of which 13 were waited for; matrix products, arithmetic and copies ran while one was open for 20% of the time, Pallas kernels for 0%

profile of v10, /device:TPU:1, one launch (start us, length us, event | category | flops | bytes accessed | tf_op | source)
XLA Modules:
  0.0 205.3 jit_solution(5047379372018069947)
XLA Ops:
  0.2 10.2 %fusion = f32[8,2,128,256]{3,0,2,1:T(8,128)S(1)} fusion(bf16[128,256,256]{2,1,0:T(8,128)(2,1)} %param.2, bf16[8,2,256,1]{2,1,0,3:T(2,128)(2,1)S(1)} %bitcast.168), kind=kOutput, calls=%fused_computation | convolution fusion | flops 268435456 | bytes 18882560 | tf_op jit(solution)/shard_map/srt,tc->csr/dot_general | solution.py:44
  10.4 1.7 constant_dynamic-slice_fusion.7
  12.8 2.0 collective-permute-start
  15.5 2.5 %collective-permute-start.1 = (f32[2,128,256]{2,1,0:T(8,128)}, f32[2,128,256]{2,1,0:T(8,128)}, u32[]{:S(2)}, u32[]{:S(2)}) collective-permute-start(f32[2,128,256]{2,1,0:T(8,128)} %bitcast.163), channel_id=1, source_target_pairs={{0,32},{16,48},{32,64},{48,80},{64,96},{80,112},{96,0},{112,16},{1... | collective-permute-start | bytes 786440 | tf_op jit(solution)/shard_map/ppermute | solution.py:53
  18.7 4.5 %collective-permute-start.2 = (f32[2,128,256]{2,1,0:T(8,128)}, f32[2,128,256]{2,1,0:T(8,128)}, u32[]{:S(2)}, u32[]{:S(2)}) collective-permute-start(f32[2,128,256]{2,1,0:T(8,128)} %bitcast.162), channel_id=1, source_target_pairs={{0,48},{16,64},{32,80},{48,96},{64,112},{80,0},{96,16},{112,32},{1... | collective-permute-start | bytes 786440 | tf_op jit(solution)/shard_map/ppermute | solution.py:53
  24.6 3.0 %collective-permute-start.4 = (f32[2,128,256]{2,1,0:T(8,128)}, f32[2,128,256]{2,1,0:T(8,128)S(1)}, u32[]{:S(2)}, u32[]{:S(2)}) collective-permute-start(f32[2,128,256]{2,1,0:T(8,128)} %bitcast.160), channel_id=1, source_target_pairs={{0,80},{16,96},{32,112},{48,0},{64,16},{80,32},{96,48},{112,64},{1... | collective-permute-start | bytes 786440 | tf_op jit(solution)/shard_map/ppermute | solution.py:53
  28.8 3.0 %collective-permute-start.5 = (f32[2,128,256]{2,1,0:T(8,128)}, f32[2,128,256]{2,1,0:T(8,128)S(1)}, u32[]{:S(2)}, u32[]{:S(2)}) collective-permute-start(f32[2,128,256]{2,1,0:T(8,128)} %bitcast.167), channel_id=1, source_target_pairs={{0,96},{16,112},{32,0},{48,16},{64,32},{80,48},{96,64},{112,80},{1... | collective-permute-start | bytes 786440 | tf_op jit(solution)/shard_map/ppermute | solution.py:53
  32.8 1.5 collective-permute-done.1
  35.3 1.3 collective-permute-done.2
  37.6 5.8 %collective-permute-done.3 = f32[2,128,256]{2,1,0:T(8,128)S(1)} collective-permute-done((f32[2,128,256]{2,1,0:T(8,128)}, f32[2,128,256]{2,1,0:T(8,128)S(1)}, u32[]{:S(2)}, u32[]{:S(2)}) %collective-permute-start.3) | collective-permute-done | bytes 262176 | tf_op jit(solution)/shard_map/ppermute | solution.py:53
  43.7 3.7 %collective-permute-done.6 = f32[2,128,256]{2,1,0:T(8,128)S(1)} collective-permute-done((f32[2,128,256]{2,1,0:T(8,128)S(1)}, f32[2,128,256]{2,1,0:T(8,128)S(1)}, u32[]{:S(2)}, u32[]{:S(2)}) %collective-permute-start.6) | collective-permute-done | bytes 262176 | tf_op jit(solution)/shard_map/ppermute | solution.py:53
  47.4 1.9 collective-permute-start.7
  49.3 4.4 %broadcast_in_dim.8 = f32[2,2048,512]{2,1,0:T(8,128)} broadcast(f32[]{:T(128)} %constant.169.clone.1), dimensions={} | broadcast | bytes 8388612 | tf_op jit(solution)/shard_map/broadcast_in_dim | solution.py:116
  53.7 1.2 constant_dynamic-update-slice_fusion.4
  56.6 1.2 pad_maximum_fusion.1
  57.8 10.4 %collective-permute-done.8 = f32[2,128,512]{2,1,0:T(8,128)S(1)} collective-permute-done((f32[2,128,512]{2,1,0:T(8,128)S(1)}, f32[2,128,512]{2,1,0:T(8,128)S(1)}, u32[]{:S(2)}, u32[]{:S(2)}) %collective-permute-start.8) | collective-permute-done | bytes 524320 | tf_op jit(solution)/shard_map/ppermute | solution.py:33
  68.3 11.5 %collective-permute-done.9 = f32[2,128,512]{2,1,0:T(8,128)S(1)} collective-permute-done((f32[2,128,512]{2,1,0:T(8,128)S(1)}, f32[2,128,512]{2,1,0:T(8,128)S(1)}, u32[]{:S(2)}, u32[]{:S(2)}) %collective-permute-start.9) | collective-permute-done | bytes 524320 | tf_op jit(solution)/shard_map/ppermute | solution.py:33
  81.2 1.9 constant_dynamic-update-slice_fusion.3
  83.2 1.4 collective-permute-start.10
  84.5 1.6 collective-permute-start.11
  88.1 2.7 %collective-permute-start.13 = (f32[2,256,512]{2,1,0:T(8,128)S(1)}, f32[2,256,512]{2,1,0:T(8,128)S(1)}, u32[]{:S(2)}, u32[]{:S(2)}) collective-permute-start(f32[2,256,512]{2,1,0:T(8,128)S(1)} %get-tuple-element.51), channel_id=1, source_target_pairs={{0,12},{1,13},{2,14},{3,15},{4,0},{5,1},{6,2},{7,3},{8,4},{9,5},{1... | collective-permute-start | bytes 3145736 | tf_op jit(solution)/shard_map/ppermute | solution.py:33
  90.8 25.1 %collective-permute-done.16 = f32[2,128,1536]{2,1,0:T(8,128)} collective-permute-done((f32[2,128,1536]{2,1,0:T(8,128)}, f32[2,128,1536]{2,1,0:T(8,128)}, u32[]{:S(2)}, u32[]{:S(2)}) %collective-permute-start.16) | collective-permute-done | bytes 1572896 | tf_op jit(solution)/shard_map/ppermute | solution.py:33
  115.9 1.1 slice_dynamic-update-slice_fusion.2
  117.0 1.1 slice_dynamic-update-slice_fusion.1
  118.0 1.1 slice_dynamic-update-slice_fusion
  119.1 1.3 collective-permute-start.17
  120.4 1.4 fusion.76
  121.8 1.0 fusion.32
  122.8 1.4 fusion.61
  124.2 1.0 fusion.30
  125.3 1.2 fusion.72
  126.5 1.4 collective-permute-start.14
  133.2 1.2 collective-permute-start.15
  135.4 1.0 fusion.24
  137.3 1.0 fusion.26
  139.2 1.0 fusion.28
  140.2 13.6 %collective-permute-done.14 = f32[2,256,512]{2,1,0:T(8,128)S(1)} collective-permute-done((f32[2,256,512]{2,1,0:T(8,128)S(1)}, f32[2,256,512]{2,1,0:T(8,128)S(1)}, u32[]{:S(2)}, u32[]{:S(2)}) %collective-permute-start.14) | collective-permute-done | bytes 1048608 | tf_op jit(solution)/shard_map/ppermute | solution.py:33
  157.5 9.6 %fusion.6 = f32[2,2,256,512]{3,2,0,1:T(8,128)S(1)} fusion(f32[2,128,2048]{2,1,0:T(8,128)S(1)} %collective-permute-done.17, f32[2,128,2048]{2,1,0:T(8,128)S(1)} %slice_dynamic-update-slice_fusion, f32[2,2048,512]{2,1,0:T(8,128)} %slice_dynamic-update-slice_fusion.3), kind=kOutput, calls=%fused_computation.54 | convolution fusion | flops 6443499520 | bytes 14680064 | tf_op jit(solution)/shard_map/aik,bkj->abij/dot_general | solution.py:79
  167.1 1.0 fusion.20
  168.2 2.1 %add_bitcast_fusion = f32[2,2,256,512]{3,2,0,1:T(8,128)S(1)} fusion(f32[2,512,2,256]{1,3,2,0:T(8,128)S(1)} %fusion.20, f32[2,512,2,256]{1,3,2,0:T(8,128)S(1)} %fusion.22, f32[2,512,2,256]{1,3,2,0:T(8,128)S(1)} %fusion.24, f32[2,512,2,256]{1,3,2,0:T(8,128)S(1)} %fusion.26, f32[2,512,2,256]{1,3,2,0:T(8,128)S(1)} %fusion.28, ...), kind=kOutput, calls=%fused_computation.53 | convolution fusion | flops 809107456 | bytes 18350080 | tf_op jit(solution)/shard_map/aik,bkj->abij/dot_general | solution.py:79
  170.3 1.7 fusion.40
  172.0 1.5 fusion.36
  173.5 1.0 fusion.43
  174.6 3.5 %collective-permute-start.20 = (f32[2,128,512]{2,1,0:T(8,128)}, f32[2,128,512]{2,1,0:T(8,128)S(1)}, u32[]{:S(2)}, u32[]{:S(2)}) collective-permute-start(f32[2,128,512]{2,1,0:T(8,128)} %get-tuple-element.36), channel_id=1, source_target_pairs={{0,3},{1,2},{2,1},{3,0},{4,7},{5,6},{6,5},{7,4},{8,11},{9,10},{10,... | collective-permute-start | bytes 1572872 | tf_op jit(solution)/shard_map/ppermute | solution.py:33
  178.8 11.9 %collective-permute-done.20 = f32[2,128,512]{2,1,0:T(8,128)S(1)} collective-permute-done((f32[2,128,512]{2,1,0:T(8,128)}, f32[2,128,512]{2,1,0:T(8,128)S(1)}, u32[]{:S(2)}, u32[]{:S(2)}) %collective-permute-start.20) | collective-permute-done | bytes 524320 | tf_op jit(solution)/shard_map/ppermute | solution.py:33
  190.7 11.4 %collective-permute-done.19 = f32[2,128,512]{2,1,0:T(8,128)} collective-permute-done((f32[2,128,512]{2,1,0:T(8,128)S(1)}, f32[2,128,512]{2,1,0:T(8,128)}, u32[]{:S(2)}, u32[]{:S(2)}) %collective-permute-start.19) | collective-permute-done | bytes 524320 | tf_op jit(solution)/shard_map/ppermute | solution.py:33
  202.1 1.4 pad_maximum_fusion
  203.8 1.5 maximum_bitcast_fusion.2
  (66 shorter events, 25.9 us)
Async XLA Ops:
  12.8 16.0 %collective-permute-start = (f32[2,128,256]{2,1,0:T(8,128)}, f32[2,128,256]{2,1,0:T(8,128)}, u32[]{:S(2)}, u32[]{:S(2)}) collective-permute-start(f32[2,128,256]{2,1,0:T(8,128)} %bitcast.164), channel_id=1, source_target_pairs={{0,16},{16,32},{32,48},{48,64},{64,80},{80,96},{96,112},{112,0},{1... | collective-permute-start | bytes 786440 | tf_op jit(solution)/shard_map/ppermute | solution.py:53
  15.5 18.7 %collective-permute-start.1 = (f32[2,128,256]{2,1,0:T(8,128)}, f32[2,128,256]{2,1,0:T(8,128)}, u32[]{:S(2)}, u32[]{:S(2)}) collective-permute-start(f32[2,128,256]{2,1,0:T(8,128)} %bitcast.163), channel_id=1, source_target_pairs={{0,32},{16,48},{32,64},{48,80},{64,96},{80,112},{96,0},{112,16},{1... | collective-permute-start | bytes 786440 | tf_op jit(solution)/shard_map/ppermute | solution.py:53
  18.7 17.9 %collective-permute-start.2 = (f32[2,128,256]{2,1,0:T(8,128)}, f32[2,128,256]{2,1,0:T(8,128)}, u32[]{:S(2)}, u32[]{:S(2)}) collective-permute-start(f32[2,128,256]{2,1,0:T(8,128)} %bitcast.162), channel_id=1, source_target_pairs={{0,48},{16,64},{32,80},{48,96},{64,112},{80,0},{96,16},{112,32},{1... | collective-permute-start | bytes 786440 | tf_op jit(solution)/shard_map/ppermute | solution.py:53
  23.9 19.4 %collective-permute-start.3 = (f32[2,128,256]{2,1,0:T(8,128)}, f32[2,128,256]{2,1,0:T(8,128)S(1)}, u32[]{:S(2)}, u32[]{:S(2)}) collective-permute-start(f32[2,128,256]{2,1,0:T(8,128)} %bitcast.161), channel_id=1, source_target_pairs={{0,64},{16,80},{32,96},{48,112},{64,0},{80,16},{96,32},{112,48},{1... | collective-permute-start | bytes 786440 | tf_op jit(solution)/shard_map/ppermute | solution.py:53
  24.6 19.0 %collective-permute-start.4 = (f32[2,128,256]{2,1,0:T(8,128)}, f32[2,128,256]{2,1,0:T(8,128)S(1)}, u32[]{:S(2)}, u32[]{:S(2)}) collective-permute-start(f32[2,128,256]{2,1,0:T(8,128)} %bitcast.160), channel_id=1, source_target_pairs={{0,80},{16,96},{32,112},{48,0},{64,16},{80,32},{96,48},{112,64},{1... | collective-permute-start | bytes 786440 | tf_op jit(solution)/shard_map/ppermute | solution.py:53
  28.8 14.9 %collective-permute-start.5 = (f32[2,128,256]{2,1,0:T(8,128)}, f32[2,128,256]{2,1,0:T(8,128)S(1)}, u32[]{:S(2)}, u32[]{:S(2)}) collective-permute-start(f32[2,128,256]{2,1,0:T(8,128)} %bitcast.167), channel_id=1, source_target_pairs={{0,96},{16,112},{32,0},{48,16},{64,32},{80,48},{96,64},{112,80},{1... | collective-permute-start | bytes 786440 | tf_op jit(solution)/shard_map/ppermute | solution.py:53
  34.3 13.1 %collective-permute-start.6 = (f32[2,128,256]{2,1,0:T(8,128)S(1)}, f32[2,128,256]{2,1,0:T(8,128)S(1)}, u32[]{:S(2)}, u32[]{:S(2)}) collective-permute-start(f32[2,128,256]{2,1,0:T(8,128)S(1)} %bitcast.166), channel_id=1, source_target_pairs={{0,112},{16,0},{32,16},{48,32},{64,48},{80,64},{96,80},{112,96},{1... | collective-permute-start | bytes 786440 | tf_op jit(solution)/shard_map/ppermute | solution.py:53
  47.4 33.7 %collective-permute-start.7 = (f32[2,128,2048]{2,1,0:T(8,128)S(1)}, f32[2,128,2048]{2,1,0:T(8,128)}, u32[]{:S(2)}, u32[]{:S(2)}) collective-permute-start(f32[2,128,2048]{2,1,0:T(8,128)S(1)} %constant_dynamic-update-slice_fusion.5), channel_id=1, source_target_pairs={{0,1},{1,0},{2,3},{3,2},{4,5},{5,4},{6,7},{7,6},{8,9},{9,8},{10,11... | collective-permute-start | bytes 6291464 | tf_op jit(solution)/shard_map/ppermute | solution.py:33
  54.9 25.7 %copy-start.2 = (f32[1,2]{1,0:T(1,128)S(1)}, f32[1,2]{1,0:T(1,128)}, u32[]{:S(2)}) copy-start(f32[1,2]{1,0:T(1,128)} %param.3) | copy-start | bytes 28
  54.9 13.4 %collective-permute-start.8 = (f32[2,128,512]{2,1,0:T(8,128)S(1)}, f32[2,128,512]{2,1,0:T(8,128)S(1)}, u32[]{:S(2)}, u32[]{:S(2)}) collective-permute-start(f32[2,128,512]{2,1,0:T(8,128)S(1)} %get-tuple-element.42), channel_id=1, source_target_pairs={{0,2},{1,3},{2,0},{3,1},{4,6},{5,7},{6,4},{7,5},{8,10},{9,11},{10,... | collective-permute-start | bytes 1572872 | tf_op jit(solution)/shard_map/ppermute | solution.py:33
  55.6 24.1 %collective-permute-start.9 = (f32[2,128,512]{2,1,0:T(8,128)S(1)}, f32[2,128,512]{2,1,0:T(8,128)S(1)}, u32[]{:S(2)}, u32[]{:S(2)}) collective-permute-start(f32[2,128,512]{2,1,0:T(8,128)S(1)} %get-tuple-element.41), channel_id=1, source_target_pairs={{0,3},{1,2},{2,1},{3,0},{4,7},{5,6},{6,5},{7,4},{8,11},{9,10},{10,... | collective-permute-start | bytes 1572872 | tf_op jit(solution)/shard_map/ppermute | solution.py:33
  68.3 11.5 %copy-start = (f32[2,128,512]{2,1,0:T(8,128)}, f32[2,128,512]{2,1,0:T(8,128)S(1)}, u32[]{:S(2)}) copy-start(f32[2,128,512]{2,1,0:T(8,128)S(1)} %collective-permute-done.8) | copy-start | bytes 1572868
  79.8 36.1 %collective-permute-start.16 = (f32[2,128,1536]{2,1,0:T(8,128)}, f32[2,128,1536]{2,1,0:T(8,128)}, u32[]{:S(2)}, u32[]{:S(2)}) collective-permute-start(f32[2,128,1536]{2,1,0:T(8,128)} %pad_maximum_fusion.1), channel_id=1, source_target_pairs={{0,2},{1,3},{2,0},{3,1},{4,6},{5,7},{6,4},{7,5},{8,10},{9,11},{10,... | collective-permute-start | bytes 4718600 | tf_op jit(solution)/shard_map/ppermute | solution.py:33
  83.1 3.2 %copy-start.1 = (f32[2,128,512]{2,1,0:T(8,128)S(1)}, f32[2,128,512]{2,1,0:T(8,128)}, u32[]{:S(2)}) copy-start(f32[2,128,512]{2,1,0:T(8,128)} %copy-done) | copy-start | bytes 1572868
  83.2 43.3 %collective-permute-start.10 = (f32[2,256,512]{2,1,0:T(8,128)S(1)}, f32[2,256,512]{2,1,0:T(8,128)S(1)}, u32[]{:S(2)}, u32[]{:S(2)}) collective-permute-start(f32[2,256,512]{2,1,0:T(8,128)S(1)} %pad_maximum_fusion.3), channel_id=1, source_target_pairs={{0,4},{1,5},{2,6},{3,7},{4,8},{5,9},{6,10},{7,11},{8,12},{9,13},{1... | collective-permute-start | bytes 3145736 | tf_op jit(solution)/shard_map/ppermute | solution.py:33
  84.5 45.0 %collective-permute-start.11 = (f32[2,256,512]{2,1,0:T(8,128)S(1)}, f32[2,256,512]{2,1,0:T(8,128)S(1)}, u32[]{:S(2)}, u32[]{:S(2)}) collective-permute-start(f32[2,256,512]{2,1,0:T(8,128)S(1)} %pad_maximum_fusion.3), channel_id=1, source_target_pairs={{0,12},{1,13},{2,14},{3,15},{4,0},{5,1},{6,2},{7,3},{8,4},{9,5},{1... | collective-permute-start | bytes 3145736 | tf_op jit(solution)/shard_map/ppermute | solution.py:33
  88.1 43.3 %collective-permute-start.12 = (f32[2,256,512]{2,1,0:T(8,128)S(1)}, f32[2,256,512]{2,1,0:T(8,128)S(1)}, u32[]{:S(2)}, u32[]{:S(2)}) collective-permute-start(f32[2,256,512]{2,1,0:T(8,128)S(1)} %get-tuple-element.51), channel_id=1, source_target_pairs={{0,4},{1,5},{2,6},{3,7},{4,8},{5,9},{6,10},{7,11},{8,12},{9,13},{1... | collective-permute-start | bytes 3145736 | tf_op jit(solution)/shard_map/ppermute | solution.py:33
  88.1 45.0 %collective-permute-start.13 = (f32[2,256,512]{2,1,0:T(8,128)S(1)}, f32[2,256,512]{2,1,0:T(8,128)S(1)}, u32[]{:S(2)}, u32[]{:S(2)}) collective-permute-start(f32[2,256,512]{2,1,0:T(8,128)S(1)} %get-tuple-element.51), channel_id=1, source_target_pairs={{0,12},{1,13},{2,14},{3,15},{4,0},{5,1},{6,2},{7,3},{8,4},{9,5},{1... | collective-permute-start | bytes 3145736 | tf_op jit(solution)/shard_map/ppermute | solution.py:33
  119.1 38.4 %collective-permute-start.17 = (f32[2,128,2048]{2,1,0:T(8,128)S(1)}, f32[2,128,2048]{2,1,0:T(8,128)S(1)}, u32[]{:S(2)}, u32[]{:S(2)}) collective-permute-start(f32[2,128,2048]{2,1,0:T(8,128)S(1)} %slice_dynamic-update-slice_fusion), channel_id=1, source_target_pairs={{0,1},{1,0},{2,3},{3,2},{4,5},{5,4},{6,7},{7,6},{8,9},{9,8},{10,11... | collective-permute-start | bytes 6291464 | tf_op jit(solution)/shard_map/ppermute | solution.py:33
  126.5 27.3 %collective-permute-start.14 = (f32[2,256,512]{2,1,0:T(8,128)S(1)}, f32[2,256,512]{2,1,0:T(8,128)S(1)}, u32[]{:S(2)}, u32[]{:S(2)}) collective-permute-start(f32[2,256,512]{2,1,0:T(8,128)S(1)} %collective-permute-done.10), channel_id=1, source_target_pairs={{0,4},{1,5},{2,6},{3,7},{4,8},{5,9},{6,10},{7,11},{8,12},{9,13},{1... | collective-permute-start | bytes 3145736 | tf_op jit(solution)/shard_map/ppermute | solution.py:33
  133.2 22.7 %collective-permute-start.15 = (f32[2,256,512]{2,1,0:T(8,128)S(1)}, f32[2,256,512]{2,1,0:T(8,128)S(1)}, u32[]{:S(2)}, u32[]{:S(2)}) collective-permute-start(f32[2,256,512]{2,1,0:T(8,128)S(1)} %collective-permute-done.13), channel_id=1, source_target_pairs={{0,12},{1,13},{2,14},{3,15},{4,0},{5,1},{6,2},{7,3},{8,4},{9,5},{1... | collective-permute-start | bytes 3145736 | tf_op jit(solution)/shard_map/ppermute | solution.py:33
  174.6 16.1 %collective-permute-start.20 = (f32[2,128,512]{2,1,0:T(8,128)}, f32[2,128,512]{2,1,0:T(8,128)S(1)}, u32[]{:S(2)}, u32[]{:S(2)}) collective-permute-start(f32[2,128,512]{2,1,0:T(8,128)} %get-tuple-element.36), channel_id=1, source_target_pairs={{0,3},{1,2},{2,1},{3,0},{4,7},{5,6},{6,5},{7,4},{8,11},{9,10},{10,... | collective-permute-start | bytes 1572872 | tf_op jit(solution)/shard_map/ppermute | solution.py:33
  178.1 24.0 %collective-permute-start.19 = (f32[2,128,512]{2,1,0:T(8,128)S(1)}, f32[2,128,512]{2,1,0:T(8,128)}, u32[]{:S(2)}, u32[]{:S(2)}) collective-permute-start(f32[2,128,512]{2,1,0:T(8,128)S(1)} %get-tuple-element.37), channel_id=1, source_target_pairs={{0,2},{1,3},{2,0},{3,1},{4,6},{5,7},{6,4},{7,5},{8,10},{9,11},{10,... | collective-permute-start | bytes 1572872 | tf_op jit(solution)/shard_map/ppermute | solution.py:33
  178.8 23.4 %collective-permute-start.18 = (f32[2,128,512]{2,1,0:T(8,128)S(1)}, f32[2,128,512]{2,1,0:T(8,128)}, u32[]{:S(2)}, u32[]{:S(2)}) collective-permute-start(f32[2,128,512]{2,1,0:T(8,128)S(1)} %get-tuple-element.35), channel_id=1, source_target_pairs={{0,1},{1,0},{2,3},{3,2},{4,5},{5,4},{6,7},{7,6},{8,9},{9,8},{10,11... | collective-permute-start | bytes 1572872 | tf_op jit(solution)/shard_map/ppermute | solution.py:33

commit v11 on v10

--- a/solution.py
+++ b/solution.py
@@ -11,8 +11,8 @@
 GROUP = 4
 
 
-def make_table(freqs, samples):
-    bins = BIN0 + BINSTEP * jnp.arange(freqs, dtype=jnp.int32)
+def make_table(freqs, samples, first=0):
+    bins = BIN0 + BINSTEP * ((first + jnp.arange(freqs, dtype=jnp.int32)) % freqs)
     steps = jnp.arange(samples, dtype=jnp.int32)
     phase = steps[:, None] * bins[None, :] % samples
     angle = phase.astype(jnp.float32) * (2.0 * math.pi / samples)
@@ -39,17 +39,15 @@
     nblk = lax.axis_size("blk")
     ny = nblk // GROUP
     assert ny == 4 and nblk % GROUP == 0
-    table = make_table(freqs, samples)
+    f = lax.axis_index("freq")
+    table = make_table(freqs, samples, f)
     table = table.reshape(samples, 2, freqs).transpose(0, 2, 1).reshape(samples, 2 * freqs)
     projected = jnp.einsum("srt,tc->csr", traces, table, preferred_element_type=jnp.float32)
     projected = projected.reshape(freqs, 2, src_rows, rec_cols)
-    f = lax.axis_index("freq")
     own = jnp.zeros((2, src_rows, freqs * rec_cols), jnp.float32)
-    own = lax.dynamic_update_slice_in_dim(
-        own, lax.dynamic_index_in_dim(projected, f, 0, keepdims=False), f * rec_cols, axis=2
-    )
+    own = lax.dynamic_update_slice_in_dim(own, projected[0], f * rec_cols, axis=2)
     for k in range(1, freqs):
-        chunk = lax.dynamic_index_in_dim(projected, (f + k) % freqs, 0, keepdims=False)
+        chunk = projected[k]
         got = lax.ppermute(chunk, "freq", shift_perm(freqs, k))
         own = lax.dynamic_update_slice_in_dim(own, got, ((f - k) % freqs) * rec_cols, axis=2)
     n = own.shape[2]

time: 206 us -> 203 us (0.985)
  local copies, waits for them, and re-layouts: 32.9 us -> 30.4 us
    unnamed x14 -> x7, local copies, waits for them, and re-layouts: 5.3 us -> 0.91 us
where the time goes in v11:
time: 203 us
  waiting for transfers between devices  98.6 us (49%)
  starting transfers between devices  32.5 us (16%)
  local copies, waits for them, and re-layouts  30.4 us (15%)
  matrix products  29.2 us (14%)
  other arithmetic  11.6 us (6%)
    ppermute x14, waiting for transfers between devices, send(): return lax.ppermute(x, 'blk', perm)  84.2 us
    dot_general x9, matrix products, mm(): jnp.einsum('aik,bkj->abij', lhs, rhs, precision=lax.Precision.HIGH, prefe...  18.9 us
    ppermute x14, starting transfers between devices, send(): return lax.ppermute(x, 'blk', perm)  18.1 us
    ppermute x7, starting transfers between devices, on_device(): got = lax.ppermute(chunk, 'freq', shift_perm(freqs, k))  14.4 us
    ppermute x7, waiting for transfers between devices, on_device(): got = lax.ppermute(chunk, 'freq', shift_perm(freqs, k))  14.4 us
    dynamic_update_slice x14, local copies, waits for them, and re-layouts, on_device(): lax.dynamic_update_slice_in_dim(right, pc[:, i * rb:(i + 1) * rb], kblk(g...  13.2 us
    dot_general x1, matrix products, on_device(): jnp.einsum('srt,tc->csr', traces, table, preferred_element_type=jnp.float32)  10.2 us
    dynamic_update_slice x7, local copies, waits for them, and re-layouts, on_device(): lax.dynamic_update_slice_in_dim(own, got, (f - k) % freqs * rec_cols, axi...  4.92 us
  transfers between devices with their start and end apart: 21, of which 13 were waited for; matrix products, arithmetic and copies ran while one was open for 20% of the time, Pallas kernels for 0%

profile of v11, /device:TPU:1, one launch (start us, length us, event | category | flops | bytes accessed | tf_op | source)
XLA Modules:
  0.0 202.8 jit_solution(13445203730771942783)
XLA Ops:
  0.2 10.2 %fusion.97 = f32[16,128,256]{2,0,1:T(8,128)S(1)} fusion(bf16[256,16,1]{0,1,2:T(8,128)(2,1)S(1)} %reshape.205, bf16[128,256,256]{2,1,0:T(8,128)(2,1)} %param.2), kind=kOutput, calls=%fused_computation.203 | convolution fusion | flops 268435456 | bytes 18882560 | tf_op jit(solution)/shard_map/srt,tc->csr/dot_general | solution.py:45
  10.4 1.6 fusion.95
  12.0 2.0 %collective-permute-start = (f32[2,128,256]{2,0,1:T(2,128)}, f32[2,128,256]{2,0,1:T(2,128)}, u32[]{:S(2)}, u32[]{:S(2)}) collective-permute-start(f32[2,128,256]{2,0,1:T(2,128)} %get-tuple-element.49), channel_id=1, source_target_pairs={{0,16},{16,32},{32,48},{48,64},{64,80},{80,96},{96,112},{112,0},{1... | collective-permute-start | bytes 786440 | tf_op jit(solution)/shard_map/ppermute | solution.py:51
  14.0 2.5 %collective-permute-start.1 = (f32[2,128,256]{2,0,1:T(2,128)}, f32[2,128,256]{2,0,1:T(2,128)}, u32[]{:S(2)}, u32[]{:S(2)}) collective-permute-start(f32[2,128,256]{2,0,1:T(2,128)} %get-tuple-element.48), channel_id=1, source_target_pairs={{0,32},{16,48},{32,64},{48,80},{64,96},{80,112},{96,0},{112,16},{1... | collective-permute-start | bytes 786440 | tf_op jit(solution)/shard_map/ppermute | solution.py:51
  16.5 4.5 %collective-permute-start.2 = (f32[2,128,256]{2,0,1:T(2,128)}, f32[2,128,256]{2,0,1:T(2,128)}, u32[]{:S(2)}, u32[]{:S(2)}) collective-permute-start(f32[2,128,256]{2,0,1:T(2,128)} %get-tuple-element.47), channel_id=1, source_target_pairs={{0,48},{16,64},{32,80},{48,96},{64,112},{80,0},{96,16},{112,32},{1... | collective-permute-start | bytes 786440 | tf_op jit(solution)/shard_map/ppermute | solution.py:51
  20.9 3.0 %collective-permute-start.4 = (f32[2,128,256]{2,0,1:T(2,128)S(1)}, f32[2,128,256]{2,0,1:T(2,128)}, u32[]{:S(2)}, u32[]{:S(2)}) collective-permute-start(f32[2,128,256]{2,0,1:T(2,128)S(1)} %get-tuple-element.45), channel_id=1, source_target_pairs={{0,80},{16,96},{32,112},{48,0},{64,16},{80,32},{96,48},{112,64},{1... | collective-permute-start | bytes 786440 | tf_op jit(solution)/shard_map/ppermute | solution.py:51
  24.9 2.4 %collective-permute-start.5 = (f32[2,128,256]{2,0,1:T(2,128)S(1)}, f32[2,128,256]{2,0,1:T(2,128)S(1)}, u32[]{:S(2)}, u32[]{:S(2)}) collective-permute-start(f32[2,128,256]{2,0,1:T(2,128)S(1)} %get-tuple-element.44), channel_id=1, source_target_pairs={{0,96},{16,112},{32,0},{48,16},{64,32},{80,48},{96,64},{112,80},{1... | collective-permute-start | bytes 786440 | tf_op jit(solution)/shard_map/ppermute | solution.py:51
  28.3 5.5 %collective-permute-done.1 = f32[2,128,256]{2,0,1:T(2,128)} collective-permute-done((f32[2,128,256]{2,0,1:T(2,128)}, f32[2,128,256]{2,0,1:T(2,128)}, u32[]{:S(2)}, u32[]{:S(2)}) %collective-permute-start.1) | collective-permute-done | bytes 262176 | tf_op jit(solution)/shard_map/ppermute | solution.py:51
  36.6 5.9 %collective-permute-done.3 = f32[2,128,256]{2,0,1:T(2,128)} collective-permute-done((f32[2,128,256]{2,0,1:T(2,128)S(1)}, f32[2,128,256]{2,0,1:T(2,128)}, u32[]{:S(2)}, u32[]{:S(2)}) %collective-permute-start.3) | collective-permute-done | bytes 262176 | tf_op jit(solution)/shard_map/ppermute | solution.py:51
  43.5 1.0 copy_dynamic-update-slice_fusion.2
  44.6 1.6 collective-permute-done.6
  46.2 1.9 collective-permute-start.7
  48.0 4.4 %broadcast_in_dim.8 = f32[2,2048,512]{2,1,0:T(8,128)} broadcast(f32[]{:T(128)} %constant.131.clone.1), dimensions={} | broadcast | bytes 8388612 | tf_op jit(solution)/shard_map/broadcast_in_dim | solution.py:114
  52.4 1.2 constant_dynamic-update-slice_fusion.4
  55.3 1.3 pad_maximum_fusion.1
  56.5 10.4 %collective-permute-done.8 = f32[2,128,512]{2,1,0:T(8,128)S(1)} collective-permute-done((f32[2,128,512]{2,1,0:T(8,128)S(1)}, f32[2,128,512]{2,1,0:T(8,128)S(1)}, u32[]{:S(2)}, u32[]{:S(2)}) %collective-permute-start.8) | collective-permute-done | bytes 524320 | tf_op jit(solution)/shard_map/ppermute | solution.py:33
  67.0 11.5 %collective-permute-done.9 = f32[2,128,512]{2,1,0:T(8,128)S(1)} collective-permute-done((f32[2,128,512]{2,1,0:T(8,128)S(1)}, f32[2,128,512]{2,1,0:T(8,128)S(1)}, u32[]{:S(2)}, u32[]{:S(2)}) %collective-permute-start.9) | collective-permute-done | bytes 524320 | tf_op jit(solution)/shard_map/ppermute | solution.py:33
  79.9 1.9 constant_dynamic-update-slice_fusion.3
  81.9 1.4 collective-permute-start.10
  83.3 1.6 collective-permute-start.11
  86.8 2.7 %collective-permute-start.13 = (f32[2,256,512]{2,1,0:T(8,128)S(1)}, f32[2,256,512]{2,1,0:T(8,128)S(1)}, u32[]{:S(2)}, u32[]{:S(2)}) collective-permute-start(f32[2,256,512]{2,1,0:T(8,128)S(1)} %get-tuple-element.51), channel_id=1, source_target_pairs={{0,12},{1,13},{2,14},{3,15},{4,0},{5,1},{6,2},{7,3},{8,4},{9,5},{1... | collective-permute-start | bytes 3145736 | tf_op jit(solution)/shard_map/ppermute | solution.py:33
  89.5 25.1 %collective-permute-done.16 = f32[2,128,1536]{2,1,0:T(8,128)} collective-permute-done((f32[2,128,1536]{2,1,0:T(8,128)}, f32[2,128,1536]{2,1,0:T(8,128)}, u32[]{:S(2)}, u32[]{:S(2)}) %collective-permute-start.16) | collective-permute-done | bytes 1572896 | tf_op jit(solution)/shard_map/ppermute | solution.py:33
  114.6 1.1 slice_dynamic-update-slice_fusion.2
  115.7 1.1 slice_dynamic-update-slice_fusion.1
  116.8 1.1 slice_dynamic-update-slice_fusion
  117.8 1.3 collective-permute-start.17
  119.1 1.4 fusion.74
  120.5 1.0 fusion.30
  121.5 1.4 fusion.59
  122.9 1.0 fusion.28
  124.0 1.2 fusion.70
  125.2 1.4 collective-permute-start.14
  131.9 1.2 collective-permute-start.15
  133.1 1.0 fusion.20
  134.2 1.0 fusion.22
  136.1 1.0 fusion.24
  137.9 1.0 fusion.26
  139.0 13.6 %collective-permute-done.14 = f32[2,256,512]{2,1,0:T(8,128)S(1)} collective-permute-done((f32[2,256,512]{2,1,0:T(8,128)S(1)}, f32[2,256,512]{2,1,0:T(8,128)S(1)}, u32[]{:S(2)}, u32[]{:S(2)}) %collective-permute-start.14) | collective-permute-done | bytes 1048608 | tf_op jit(solution)/shard_map/ppermute | solution.py:33
  156.3 9.6 %fusion.4 = f32[2,2,256,512]{3,2,0,1:T(8,128)S(1)} fusion(f32[2,128,2048]{2,1,0:T(8,128)S(1)} %collective-permute-done.17, f32[2,128,2048]{2,1,0:T(8,128)S(1)} %slice_dynamic-update-slice_fusion, f32[2,2048,512]{2,1,0:T(8,128)} %slice_dynamic-update-slice_fusion.3), kind=kOutput, calls=%fused_computation.52 | convolution fusion | flops 6443499520 | bytes 14680064 | tf_op jit(solution)/shard_map/aik,bkj->abij/dot_general | solution.py:77
  165.9 1.0 fusion.18
  166.9 2.1 %add_bitcast_fusion = f32[2,2,256,512]{3,2,0,1:T(8,128)S(1)} fusion(f32[2,512,2,256]{1,3,2,0:T(8,128)S(1)} %fusion.18, f32[2,512,2,256]{1,3,2,0:T(8,128)S(1)} %fusion.20, f32[2,512,2,256]{1,3,2,0:T(8,128)S(1)} %fusion.22, f32[2,512,2,256]{1,3,2,0:T(8,128)S(1)} %fusion.24, f32[2,512,2,256]{1,3,2,0:T(8,128)S(1)} %fusion.26, ...), kind=kOutput, calls=%fused_computation.51 | convolution fusion | flops 809107456 | bytes 18350080 | tf_op jit(solution)/shard_map/aik,bkj->abij/dot_general | solution.py:77
  169.0 1.7 fusion.38
  170.8 1.5 fusion.34
  172.5 3.6 %collective-permute-start.20 = (f32[2,128,512]{2,1,0:T(8,128)S(1)}, f32[2,128,512]{2,1,0:T(8,128)S(1)}, u32[]{:S(2)}, u32[]{:S(2)}) collective-permute-start(f32[2,128,512]{2,1,0:T(8,128)S(1)} %get-tuple-element.36), channel_id=1, source_target_pairs={{0,3},{1,2},{2,1},{3,0},{4,7},{5,6},{6,5},{7,4},{8,11},{9,10},{10,... | collective-permute-start | bytes 1572872 | tf_op jit(solution)/shard_map/ppermute | solution.py:33
  176.8 11.7 %collective-permute-done.20 = f32[2,128,512]{2,1,0:T(8,128)S(1)} collective-permute-done((f32[2,128,512]{2,1,0:T(8,128)S(1)}, f32[2,128,512]{2,1,0:T(8,128)S(1)}, u32[]{:S(2)}, u32[]{:S(2)}) %collective-permute-start.20) | collective-permute-done | bytes 524320 | tf_op jit(solution)/shard_map/ppermute | solution.py:33
  188.4 11.3 %collective-permute-done.19 = f32[2,128,512]{2,1,0:T(8,128)S(1)} collective-permute-done((f32[2,128,512]{2,1,0:T(8,128)S(1)}, f32[2,128,512]{2,1,0:T(8,128)S(1)}, u32[]{:S(2)}, u32[]{:S(2)}) %collective-permute-start.19) | collective-permute-done | bytes 524320 | tf_op jit(solution)/shard_map/ppermute | solution.py:33
  199.8 1.2 pad_maximum_fusion
  201.3 1.5 maximum_bitcast_fusion.2
  (58 shorter events, 22.9 us)
Async XLA Ops:
  12.0 12.9 %collective-permute-start = (f32[2,128,256]{2,0,1:T(2,128)}, f32[2,128,256]{2,0,1:T(2,128)}, u32[]{:S(2)}, u32[]{:S(2)}) collective-permute-start(f32[2,128,256]{2,0,1:T(2,128)} %get-tuple-element.49), channel_id=1, source_target_pairs={{0,16},{16,32},{32,48},{48,64},{64,80},{80,96},{96,112},{112,0},{1... | collective-permute-start | bytes 786440 | tf_op jit(solution)/shard_map/ppermute | solution.py:51
  14.0 19.8 %collective-permute-start.1 = (f32[2,128,256]{2,0,1:T(2,128)}, f32[2,128,256]{2,0,1:T(2,128)}, u32[]{:S(2)}, u32[]{:S(2)}) collective-permute-start(f32[2,128,256]{2,0,1:T(2,128)} %get-tuple-element.48), channel_id=1, source_target_pairs={{0,32},{16,48},{32,64},{48,80},{64,96},{80,112},{96,0},{112,16},{1... | collective-permute-start | bytes 786440 | tf_op jit(solution)/shard_map/ppermute | solution.py:51
  16.5 19.2 %collective-permute-start.2 = (f32[2,128,256]{2,0,1:T(2,128)}, f32[2,128,256]{2,0,1:T(2,128)}, u32[]{:S(2)}, u32[]{:S(2)}) collective-permute-start(f32[2,128,256]{2,0,1:T(2,128)} %get-tuple-element.47), channel_id=1, source_target_pairs={{0,48},{16,64},{32,80},{48,96},{64,112},{80,0},{96,16},{112,32},{1... | collective-permute-start | bytes 786440 | tf_op jit(solution)/shard_map/ppermute | solution.py:51
  20.9 21.6 %collective-permute-start.3 = (f32[2,128,256]{2,0,1:T(2,128)S(1)}, f32[2,128,256]{2,0,1:T(2,128)}, u32[]{:S(2)}, u32[]{:S(2)}) collective-permute-start(f32[2,128,256]{2,0,1:T(2,128)S(1)} %get-tuple-element.46), channel_id=1, source_target_pairs={{0,64},{16,80},{32,96},{48,112},{64,0},{80,16},{96,32},{112,48},{1... | collective-permute-start | bytes 786440 | tf_op jit(solution)/shard_map/ppermute | solution.py:51
  20.9 22.6 %collective-permute-start.4 = (f32[2,128,256]{2,0,1:T(2,128)S(1)}, f32[2,128,256]{2,0,1:T(2,128)}, u32[]{:S(2)}, u32[]{:S(2)}) collective-permute-start(f32[2,128,256]{2,0,1:T(2,128)S(1)} %get-tuple-element.45), channel_id=1, source_target_pairs={{0,80},{16,96},{32,112},{48,0},{64,16},{80,32},{96,48},{112,64},{1... | collective-permute-start | bytes 786440 | tf_op jit(solution)/shard_map/ppermute | solution.py:51
  24.9 19.6 %collective-permute-start.5 = (f32[2,128,256]{2,0,1:T(2,128)S(1)}, f32[2,128,256]{2,0,1:T(2,128)S(1)}, u32[]{:S(2)}, u32[]{:S(2)}) collective-permute-start(f32[2,128,256]{2,0,1:T(2,128)S(1)} %get-tuple-element.44), channel_id=1, source_target_pairs={{0,96},{16,112},{32,0},{48,16},{64,32},{80,48},{96,64},{112,80},{1... | collective-permute-start | bytes 786440 | tf_op jit(solution)/shard_map/ppermute | solution.py:51
  33.8 12.3 %collective-permute-start.6 = (f32[2,128,256]{2,0,1:T(2,128)S(1)}, f32[2,128,256]{2,0,1:T(2,128)S(1)}, u32[]{:S(2)}, u32[]{:S(2)}) collective-permute-start(f32[2,128,256]{2,0,1:T(2,128)S(1)} %get-tuple-element.43), channel_id=1, source_target_pairs={{0,112},{16,0},{32,16},{48,32},{64,48},{80,64},{96,80},{112,96},{1... | collective-permute-start | bytes 786440 | tf_op jit(solution)/shard_map/ppermute | solution.py:51
  46.2 33.8 %collective-permute-start.7 = (f32[2,128,2048]{2,1,0:T(8,128)S(1)}, f32[2,128,2048]{2,1,0:T(8,128)}, u32[]{:S(2)}, u32[]{:S(2)}) collective-permute-start(f32[2,128,2048]{2,1,0:T(8,128)S(1)} %copy_dynamic-update-slice_fusion), channel_id=1, source_target_pairs={{0,1},{1,0},{2,3},{3,2},{4,5},{5,4},{6,7},{7,6},{8,9},{9,8},{10,11... | collective-permute-start | bytes 6291464 | tf_op jit(solution)/shard_map/ppermute | solution.py:33
  53.6 25.7 %copy-start.2 = (f32[1,2]{1,0:T(1,128)S(1)}, f32[1,2]{1,0:T(1,128)}, u32[]{:S(2)}) copy-start(f32[1,2]{1,0:T(1,128)} %param.3) | copy-start | bytes 28
  53.6 13.4 %collective-permute-start.8 = (f32[2,128,512]{2,1,0:T(8,128)S(1)}, f32[2,128,512]{2,1,0:T(8,128)S(1)}, u32[]{:S(2)}, u32[]{:S(2)}) collective-permute-start(f32[2,128,512]{2,1,0:T(8,128)S(1)} %get-tuple-element.42), channel_id=1, source_target_pairs={{0,2},{1,3},{2,0},{3,1},{4,6},{5,7},{6,4},{7,5},{8,10},{9,11},{10,... | collective-permute-start | bytes 1572872 | tf_op jit(solution)/shard_map/ppermute | solution.py:33
  54.4 24.1 %collective-permute-start.9 = (f32[2,128,512]{2,1,0:T(8,128)S(1)}, f32[2,128,512]{2,1,0:T(8,128)S(1)}, u32[]{:S(2)}, u32[]{:S(2)}) collective-permute-start(f32[2,128,512]{2,1,0:T(8,128)S(1)} %get-tuple-element.41), channel_id=1, source_target_pairs={{0,3},{1,2},{2,1},{3,0},{4,7},{5,6},{6,5},{7,4},{8,11},{9,10},{10,... | collective-permute-start | bytes 1572872 | tf_op jit(solution)/shard_map/ppermute | solution.py:33
  67.0 11.5 %copy-start = (f32[2,128,512]{2,1,0:T(8,128)}, f32[2,128,512]{2,1,0:T(8,128)S(1)}, u32[]{:S(2)}) copy-start(f32[2,128,512]{2,1,0:T(8,128)S(1)} %collective-permute-done.8) | copy-start | bytes 1572868
  78.5 36.1 %collective-permute-start.16 = (f32[2,128,1536]{2,1,0:T(8,128)}, f32[2,128,1536]{2,1,0:T(8,128)}, u32[]{:S(2)}, u32[]{:S(2)}) collective-permute-start(f32[2,128,1536]{2,1,0:T(8,128)} %pad_maximum_fusion.1), channel_id=1, source_target_pairs={{0,2},{1,3},{2,0},{3,1},{4,6},{5,7},{6,4},{7,5},{8,10},{9,11},{10,... | collective-permute-start | bytes 4718600 | tf_op jit(solution)/shard_map/ppermute | solution.py:33
  81.8 3.2 %copy-start.1 = (f32[2,128,512]{2,1,0:T(8,128)S(1)}, f32[2,128,512]{2,1,0:T(8,128)}, u32[]{:S(2)}) copy-start(f32[2,128,512]{2,1,0:T(8,128)} %copy-done) | copy-start | bytes 1572868
  81.9 43.3 %collective-permute-start.10 = (f32[2,256,512]{2,1,0:T(8,128)S(1)}, f32[2,256,512]{2,1,0:T(8,128)S(1)}, u32[]{:S(2)}, u32[]{:S(2)}) collective-permute-start(f32[2,256,512]{2,1,0:T(8,128)S(1)} %pad_maximum_fusion.3), channel_id=1, source_target_pairs={{0,4},{1,5},{2,6},{3,7},{4,8},{5,9},{6,10},{7,11},{8,12},{9,13},{1... | collective-permute-start | bytes 3145736 | tf_op jit(solution)/shard_map/ppermute | solution.py:33
  83.3 45.0 %collective-permute-start.11 = (f32[2,256,512]{2,1,0:T(8,128)S(1)}, f32[2,256,512]{2,1,0:T(8,128)S(1)}, u32[]{:S(2)}, u32[]{:S(2)}) collective-permute-start(f32[2,256,512]{2,1,0:T(8,128)S(1)} %pad_maximum_fusion.3), channel_id=1, source_target_pairs={{0,12},{1,13},{2,14},{3,15},{4,0},{5,1},{6,2},{7,3},{8,4},{9,5},{1... | collective-permute-start | bytes 3145736 | tf_op jit(solution)/shard_map/ppermute | solution.py:33
  86.8 43.3 %collective-permute-start.12 = (f32[2,256,512]{2,1,0:T(8,128)S(1)}, f32[2,256,512]{2,1,0:T(8,128)S(1)}, u32[]{:S(2)}, u32[]{:S(2)}) collective-permute-start(f32[2,256,512]{2,1,0:T(8,128)S(1)} %get-tuple-element.51), channel_id=1, source_target_pairs={{0,4},{1,5},{2,6},{3,7},{4,8},{5,9},{6,10},{7,11},{8,12},{9,13},{1... | collective-permute-start | bytes 3145736 | tf_op jit(solution)/shard_map/ppermute | solution.py:33
  86.8 45.1 %collective-permute-start.13 = (f32[2,256,512]{2,1,0:T(8,128)S(1)}, f32[2,256,512]{2,1,0:T(8,128)S(1)}, u32[]{:S(2)}, u32[]{:S(2)}) collective-permute-start(f32[2,256,512]{2,1,0:T(8,128)S(1)} %get-tuple-element.51), channel_id=1, source_target_pairs={{0,12},{1,13},{2,14},{3,15},{4,0},{5,1},{6,2},{7,3},{8,4},{9,5},{1... | collective-permute-start | bytes 3145736 | tf_op jit(solution)/shard_map/ppermute | solution.py:33
  117.8 38.4 %collective-permute-start.17 = (f32[2,128,2048]{2,1,0:T(8,128)S(1)}, f32[2,128,2048]{2,1,0:T(8,128)S(1)}, u32[]{:S(2)}, u32[]{:S(2)}) collective-permute-start(f32[2,128,2048]{2,1,0:T(8,128)S(1)} %slice_dynamic-update-slice_fusion), channel_id=1, source_target_pairs={{0,1},{1,0},{2,3},{3,2},{4,5},{5,4},{6,7},{7,6},{8,9},{9,8},{10,11... | collective-permute-start | bytes 6291464 | tf_op jit(solution)/shard_map/ppermute | solution.py:33
  125.2 27.4 %collective-permute-start.14 = (f32[2,256,512]{2,1,0:T(8,128)S(1)}, f32[2,256,512]{2,1,0:T(8,128)S(1)}, u32[]{:S(2)}, u32[]{:S(2)}) collective-permute-start(f32[2,256,512]{2,1,0:T(8,128)S(1)} %collective-permute-done.10), channel_id=1, source_target_pairs={{0,4},{1,5},{2,6},{3,7},{4,8},{5,9},{6,10},{7,11},{8,12},{9,13},{1... | collective-permute-start | bytes 3145736 | tf_op jit(solution)/shard_map/ppermute | solution.py:33
  131.9 22.7 %collective-permute-start.15 = (f32[2,256,512]{2,1,0:T(8,128)S(1)}, f32[2,256,512]{2,1,0:T(8,128)S(1)}, u32[]{:S(2)}, u32[]{:S(2)}) collective-permute-start(f32[2,256,512]{2,1,0:T(8,128)S(1)} %collective-permute-done.13), channel_id=1, source_target_pairs={{0,12},{1,13},{2,14},{3,15},{4,0},{5,1},{6,2},{7,3},{8,4},{9,5},{1... | collective-permute-start | bytes 3145736 | tf_op jit(solution)/shard_map/ppermute | solution.py:33
  172.5 15.9 %collective-permute-start.20 = (f32[2,128,512]{2,1,0:T(8,128)S(1)}, f32[2,128,512]{2,1,0:T(8,128)S(1)}, u32[]{:S(2)}, u32[]{:S(2)}) collective-permute-start(f32[2,128,512]{2,1,0:T(8,128)S(1)} %get-tuple-element.36), channel_id=1, source_target_pairs={{0,3},{1,2},{2,1},{3,0},{4,7},{5,6},{6,5},{7,4},{8,11},{9,10},{10,... | collective-permute-start | bytes 1572872 | tf_op jit(solution)/shard_map/ppermute | solution.py:33
  176.1 23.7 %collective-permute-start.19 = (f32[2,128,512]{2,1,0:T(8,128)S(1)}, f32[2,128,512]{2,1,0:T(8,128)S(1)}, u32[]{:S(2)}, u32[]{:S(2)}) collective-permute-start(f32[2,128,512]{2,1,0:T(8,128)S(1)} %get-tuple-element.37), channel_id=1, source_target_pairs={{0,2},{1,3},{2,0},{3,1},{4,6},{5,7},{6,4},{7,5},{8,10},{9,11},{10,... | collective-permute-start | bytes 1572872 | tf_op jit(solution)/shard_map/ppermute | solution.py:33
  176.8 23.0 %collective-permute-start.18 = (f32[2,128,512]{2,1,0:T(8,128)S(1)}, f32[2,128,512]{2,1,0:T(8,128)}, u32[]{:S(2)}, u32[]{:S(2)}) collective-permute-start(f32[2,128,512]{2,1,0:T(8,128)S(1)} %get-tuple-element.35), channel_id=1, source_target_pairs={{0,1},{1,0},{2,3},{3,2},{4,5},{5,4},{6,7},{7,6},{8,9},{9,8},{10,11... | collective-permute-start | bytes 1572872 | tf_op jit(solution)/shard_map/ppermute | solution.py:33

commit v12 on v11

--- a/solution.py
+++ b/solution.py
@@ -61,6 +61,7 @@
     def cols(x, i):
         return lax.dynamic_slice_in_dim(x, i * cw, cw, axis=2)
 
+    q1c = send(cols(own, p ^ 1), xor_perm(nblk, 1))
     q1 = send(own, xor_perm(nblk, 1))
     c2 = send(cols(own, p ^ 2), xor_perm(nblk, 2))
     c3 = send(cols(own, p ^ 3), xor_perm(nblk, 3))
@@ -79,7 +80,7 @@
             precision=lax.Precision.HIGH, preferred_element_type=jnp.float32,
         )
 
-    part_a = jnp.concatenate([cols(own, p), cols(q1, p)], axis=1)
+    part_a = jnp.concatenate([cols(own, p), q1c], axis=1)
     part_b = jnp.concatenate([c2, c3], axis=1)
     up = shift_perm(nblk, GROUP)
     dn = shift_perm(nblk, -GROUP)
@@ -130,12 +131,10 @@
     out_im = -(w_re * prod_im + w_im * prod_re) * scale
     blk_out = jnp.stack([out_re, out_im], axis=0)
 
-    parts = [blk_out[:, :rb]]
+    out = lax.dynamic_update_slice_in_dim(jnp.zeros_like(own), blk_out[:, :rb], p * cw, axis=2)
     for m in range(1, GROUP):
-        parts.append(send(blk_out[:, m * rb:(m + 1) * rb], xor_perm(nblk, m)))
-    stacked = jnp.stack(parts, axis=0)
-    ordered = [lax.dynamic_index_in_dim(stacked, p ^ i, 0, keepdims=False) for i in range(GROUP)]
-    out = jnp.concatenate(ordered, axis=2)
+        got = send(blk_out[:, m * rb:(m + 1) * rb], xor_perm(nblk, m))
+        out = lax.dynamic_update_slice_in_dim(out, got, (p ^ m) * cw, axis=2)
     return out[None]
 
 

time: 203 us -> 185 us (0.911)
  waiting for transfers between devices: 98.6 us -> 70.3 us
  local copies, waits for them, and re-layouts: 30.4 us -> 40.3 us
  matrix products: 29.2 us -> 34.6 us
  other arithmetic: 11.6 us -> 6.85 us
    ppermute x14 -> x15, waiting for transfers between devices: 84.2 us -> 56.1 us  [send(): return lax.ppermute(x, 'blk', perm)]
    dot_general x9, matrix products: 18.9 us -> 24.4 us  [mm(): jnp.einsum('aik,bkj->abij', lhs, rhs, precision=lax.Precision.HIGH, prefe...]
    dynamic_update_slice x14 -> x13, local copies, waits for them, and re-layouts: 13.2 us -> 17.1 us  [on_device(): lax.dynamic_update_slice_in_dim(right, pc[:, i * rb:(i + 1) * rb], kblk(g...]
    concatenate x3, other arithmetic: 3.98 us -> 0.57 us  [on_device(): early = jnp.concatenate([own, q1], axis=1)]
    ppermute x14 -> x15, starting transfers between devices: 18.1 us -> 16.9 us  [send(): return lax.ppermute(x, 'blk', perm)]
  transfers between devices with their start and end apart: 21 -> 22, of which waited for: 13 -> 11; matrix products, arithmetic and copies ran while one was open for 20% -> 27% of each run, Pallas kernels for 0% -> 0%
where the time goes in v12:
time: 185 us; the launch traced here: 184 us
  waiting for transfers between devices  70.3 us (38%)
  local copies, waits for them, and re-layouts  40.3 us (22%)
  matrix products  34.6 us (19%)
  starting transfers between devices  31.4 us (17%)
  other arithmetic  6.85 us (4%)
    ppermute x15, waiting for transfers between devices, send(): return lax.ppermute(x, 'blk', perm)  56.1 us
    dot_general x9, matrix products, mm(): jnp.einsum('aik,bkj->abij', lhs, rhs, precision=lax.Precision.HIGH, prefe...  24.4 us
    dynamic_update_slice x13, local copies, waits for them, and re-layouts, on_device(): lax.dynamic_update_slice_in_dim(right, pc[:, i * rb:(i + 1) * rb], kblk(g...  17.1 us
    ppermute x15, starting transfers between devices, send(): return lax.ppermute(x, 'blk', perm)  16.9 us
    ppermute x7, starting transfers between devices, on_device(): got = lax.ppermute(chunk, 'freq', shift_perm(freqs, k))  14.5 us
    ppermute x7, waiting for transfers between devices, on_device(): got = lax.ppermute(chunk, 'freq', shift_perm(freqs, k))  14.2 us
    dot_general x1, matrix products, on_device(): jnp.einsum('srt,tc->csr', traces, table, preferred_element_type=jnp.float32)  10.2 us
    dynamic_update_slice x7, local copies, waits for them, and re-layouts, on_device(): lax.dynamic_update_slice_in_dim(own, got, (f - k) % freqs * rec_cols, axi...  4.92 us
  transfers between devices with their start and end apart: 22, of which 11 were waited for; matrix products, arithmetic and copies ran while one was open for 27% of the time, Pallas kernels for 0%

profile of v12, /device:TPU:1, one launch (start us, length us, event | category | flops | bytes accessed | tf_op | source)
XLA Modules:
  0.0 184.0 jit_solution(9234040128399776496)
XLA Ops:
  0.2 10.2 %fusion.98 = f32[16,128,256]{2,0,1:T(8,128)S(1)} fusion(bf16[256,16,1]{0,1,2:T(8,128)(2,1)S(1)} %reshape.213, bf16[128,256,256]{2,1,0:T(8,128)(2,1)} %param.2), kind=kOutput, calls=%fused_computation.201 | convolution fusion | flops 268435456 | bytes 18882560 | tf_op jit(solution)/shard_map/srt,tc->csr/dot_general | solution.py:45
  10.4 1.6 fusion.96
  12.0 2.0 %collective-permute-start = (f32[2,128,256]{2,0,1:T(2,128)}, f32[2,128,256]{2,0,1:T(2,128)}, u32[]{:S(2)}, u32[]{:S(2)}) collective-permute-start(f32[2,128,256]{2,0,1:T(2,128)} %get-tuple-element.45), channel_id=1, source_target_pairs={{0,16},{16,32},{32,48},{48,64},{64,80},{80,96},{96,112},{112,0},{1... | collective-permute-start | bytes 786440 | tf_op jit(solution)/shard_map/ppermute | solution.py:51
  14.0 2.5 %collective-permute-start.1 = (f32[2,128,256]{2,0,1:T(2,128)}, f32[2,128,256]{2,0,1:T(2,128)}, u32[]{:S(2)}, u32[]{:S(2)}) collective-permute-start(f32[2,128,256]{2,0,1:T(2,128)} %get-tuple-element.44), channel_id=1, source_target_pairs={{0,32},{16,48},{32,64},{48,80},{64,96},{80,112},{96,0},{112,16},{1... | collective-permute-start | bytes 786440 | tf_op jit(solution)/shard_map/ppermute | solution.py:51
  16.5 4.5 %collective-permute-start.2 = (f32[2,128,256]{2,0,1:T(2,128)}, f32[2,128,256]{2,0,1:T(2,128)}, u32[]{:S(2)}, u32[]{:S(2)}) collective-permute-start(f32[2,128,256]{2,0,1:T(2,128)} %get-tuple-element.43), channel_id=1, source_target_pairs={{0,48},{16,64},{32,80},{48,96},{64,112},{80,0},{96,16},{112,32},{1... | collective-permute-start | bytes 786440 | tf_op jit(solution)/shard_map/ppermute | solution.py:51
  20.9 3.0 %collective-permute-start.4 = (f32[2,128,256]{2,0,1:T(2,128)S(1)}, f32[2,128,256]{2,0,1:T(2,128)}, u32[]{:S(2)}, u32[]{:S(2)}) collective-permute-start(f32[2,128,256]{2,0,1:T(2,128)S(1)} %get-tuple-element.41), channel_id=1, source_target_pairs={{0,80},{16,96},{32,112},{48,0},{64,16},{80,32},{96,48},{112,64},{1... | collective-permute-start | bytes 786440 | tf_op jit(solution)/shard_map/ppermute | solution.py:51
  24.9 2.5 %collective-permute-start.5 = (f32[2,128,256]{2,0,1:T(2,128)S(1)}, f32[2,128,256]{2,0,1:T(2,128)S(1)}, u32[]{:S(2)}, u32[]{:S(2)}) collective-permute-start(f32[2,128,256]{2,0,1:T(2,128)S(1)} %get-tuple-element.40), channel_id=1, source_target_pairs={{0,96},{16,112},{32,0},{48,16},{64,32},{80,48},{96,64},{112,80},{1... | collective-permute-start | bytes 786440 | tf_op jit(solution)/shard_map/ppermute | solution.py:51
  28.4 5.4 %collective-permute-done.1 = f32[2,128,256]{2,0,1:T(2,128)} collective-permute-done((f32[2,128,256]{2,0,1:T(2,128)}, f32[2,128,256]{2,0,1:T(2,128)}, u32[]{:S(2)}, u32[]{:S(2)}) %collective-permute-start.1) | collective-permute-done | bytes 262176 | tf_op jit(solution)/shard_map/ppermute | solution.py:51
  36.6 5.9 %collective-permute-done.3 = f32[2,128,256]{2,0,1:T(2,128)} collective-permute-done((f32[2,128,256]{2,0,1:T(2,128)S(1)}, f32[2,128,256]{2,0,1:T(2,128)}, u32[]{:S(2)}, u32[]{:S(2)}) %collective-permute-start.3) | collective-permute-done | bytes 262176 | tf_op jit(solution)/shard_map/ppermute | solution.py:51
  43.5 1.0 copy_dynamic-update-slice_fusion.2
  44.6 1.6 collective-permute-done.6
  46.2 4.3 %broadcast_in_dim.17 = f32[2,2048,512]{2,1,0:T(8,128)} broadcast(f32[]{:T(128)} %constant.125.clone.1), dimensions={} | broadcast | bytes 8388612 | tf_op jit(solution)/shard_map/broadcast_in_dim | solution.py:115
  50.5 1.8 constant_dynamic-slice_fusion.5
  52.3 1.8 collective-permute-start.7
  55.7 1.1 pad_maximum_fusion.2
  56.8 1.3 collective-permute-start.11
  58.1 1.4 collective-permute-start.12
  60.3 7.5 %collective-permute-done.9 = f32[2,128,512]{2,1,0:T(8,128)} collective-permute-done((f32[2,128,512]{2,1,0:T(8,128)}, f32[2,128,512]{2,1,0:T(8,128)}, u32[]{:S(2)}, u32[]{:S(2)}) %collective-permute-start.9) | collective-permute-done | bytes 524320 | tf_op jit(solution)/shard_map/ppermute | solution.py:33
  67.9 1.6 broadcast.198
  69.4 2.4 %constant_dynamic-update-slice_fusion.6 = (f32[2,256,512]{2,1,0:T(8,128)}, f32[2,128,2048]{2,1,0:T(8,128)}, f32[2,2048,512]{2,1,0:T(8,128)}) fusion(f32[2,128,512]{2,1,0:T(8,128)} %collective-permute-done.9, f32[2,128,2048]{2,1,0:T(8,128)} %broadcast.198, s32[]{:T(128)S(6)} %select_n.216, f32[2,2048,512]{2,1,0:T(8,128)} %constant_dynamic-update-slice_fusion.3, ...), kind=kLoop, calls=%fused_computation.183 | loop fusion | bytes 2097160
  71.8 7.7 %collective-permute-done.10 = f32[2,128,512]{2,1,0:T(8,128)} collective-permute-done((f32[2,128,512]{2,1,0:T(8,128)}, f32[2,128,512]{2,1,0:T(8,128)}, u32[]{:S(2)}, u32[]{:S(2)}) %collective-permute-start.10) | collective-permute-done | bytes 524320 | tf_op jit(solution)/shard_map/ppermute | solution.py:33
  79.6 2.1 %constant_dynamic-update-slice_fusion.5 = (f32[2,256,512]{2,1,0:T(8,128)}, f32[2,2048,512]{2,1,0:T(8,128)}) fusion(f32[2,256,512]{2,1,0:T(8,128)} %get-tuple-element.49, f32[2,128,512]{2,1,0:T(8,128)} %collective-permute-done.10, f32[2,2048,512]{2,1,0:T(8,128)} %get-tuple-element.51, s32[]{:T(128)S(6)} %select_n.224), kind=kLoop, calls=%fused_computation.182 | loop fusion | bytes 1572868 | tf_op jit(solution)/shard_map/concatenate | solution.py:84
  81.7 2.8 %collective-permute-start.14 = (f32[2,256,512]{2,1,0:T(8,128)}, f32[2,256,512]{2,1,0:T(8,128)}, u32[]{:S(2)}, u32[]{:S(2)}) collective-permute-start(f32[2,256,512]{2,1,0:T(8,128)} %get-tuple-element.47), channel_id=1, source_target_pairs={{0,12},{1,13},{2,14},{3,15},{4,0},{5,1},{6,2},{7,3},{8,4},{9,5},{1... | collective-permute-start | bytes 3145736 | tf_op jit(solution)/shard_map/ppermute | solution.py:33
  85.3 1.5 pad_maximum_fusion
  87.7 1.9 %slice_dynamic-update-slice_fusion.14 = f32[2,2048,512]{2,1,0:T(8,128)} fusion(f32[2,2048,512]{2,1,0:T(8,128)} %get-tuple-element.48, s32[]{:T(128)S(6)} %select_n.226, f32[2,256,512]{2,1,0:T(8,128)} %collective-permute-done.11), kind=kLoop, calls=%fused_computation.106 | loop fusion | bytes 1048580 | tf_op jit(solution)/shard_map/dynamic_update_slice | solution.py:118
  89.6 1.9 %slice_dynamic-update-slice_fusion.13 = f32[2,2048,512]{2,1,0:T(8,128)} fusion(f32[2,2048,512]{2,1,0:T(8,128)} %slice_dynamic-update-slice_fusion.14, s32[]{:T(128)S(6)} %select_n.227, f32[2,256,512]{2,1,0:T(8,128)} %collective-permute-done.11), kind=kLoop, calls=%fused_computation.105 | loop fusion | bytes 1048580 | tf_op jit(solution)/shard_map/dynamic_update_slice | solution.py:118
  91.5 15.9 %collective-permute-done.14 = f32[2,256,512]{2,1,0:T(8,128)} collective-permute-done((f32[2,256,512]{2,1,0:T(8,128)}, f32[2,256,512]{2,1,0:T(8,128)}, u32[]{:S(2)}, u32[]{:S(2)}) %collective-permute-start.14) | collective-permute-done | bytes 1048608 | tf_op jit(solution)/shard_map/ppermute | solution.py:33
  107.4 3.4 %collective-permute-start.16 = (f32[2,256,512]{2,1,0:T(8,128)}, f32[2,256,512]{2,1,0:T(8,128)S(1)}, u32[]{:S(2)}, u32[]{:S(2)}) collective-permute-start(f32[2,256,512]{2,1,0:T(8,128)} %collective-permute-done.14), channel_id=1, source_target_pairs={{0,12},{1,13},{2,14},{3,15},{4,0},{5,1},{6,2},{7,3},{8,4},{9,5},{1... | collective-permute-start | bytes 3145736 | tf_op jit(solution)/shard_map/ppermute | solution.py:33
  110.9 1.9 %slice_dynamic-update-slice_fusion.12 = f32[2,2048,512]{2,1,0:T(8,128)} fusion(f32[2,2048,512]{2,1,0:T(8,128)} %slice_dynamic-update-slice_fusion.13, s32[]{:T(128)S(6)} %select_n.229, f32[2,256,512]{2,1,0:T(8,128)} %collective-permute-done.12), kind=kLoop, calls=%fused_computation.104 | loop fusion | bytes 1048580 | tf_op jit(solution)/shard_map/dynamic_update_slice | solution.py:118
  112.7 1.9 %slice_dynamic-update-slice_fusion.11 = f32[2,2048,512]{2,1,0:T(8,128)} fusion(f32[2,2048,512]{2,1,0:T(8,128)} %slice_dynamic-update-slice_fusion.12, s32[]{:T(128)S(6)} %select_n.230, f32[2,256,512]{2,1,0:T(8,128)} %collective-permute-done.12), kind=kLoop, calls=%fused_computation.103 | loop fusion | bytes 1048580 | tf_op jit(solution)/shard_map/dynamic_update_slice | solution.py:118
  116.3 1.9 %slice_dynamic-update-slice_fusion.8 = f32[2,2048,512]{2,1,0:T(8,128)} fusion(f32[2,2048,512]{2,1,0:T(8,128)} %slice_dynamic-update-slice_fusion.9, s32[]{:T(128)S(6)} %select_n.233, f32[2,256,512]{2,1,0:T(8,128)} %collective-permute-done.14), kind=kLoop, calls=%fused_computation.100 | loop fusion | bytes 1048580 | tf_op jit(solution)/shard_map/dynamic_update_slice | solution.py:118
  118.2 1.9 %slice_dynamic-update-slice_fusion.7 = f32[2,2048,512]{2,1,0:T(8,128)} fusion(f32[2,2048,512]{2,1,0:T(8,128)} %slice_dynamic-update-slice_fusion.8, s32[]{:T(128)S(6)} %select_n.234, f32[2,256,512]{2,1,0:T(8,128)} %collective-permute-done.14), kind=kLoop, calls=%fused_computation.99 | loop fusion | bytes 1048580 | tf_op jit(solution)/shard_map/dynamic_update_slice | solution.py:118
  120.1 2.5 %collective-permute-done.17 = f32[2,128,1536]{2,1,0:T(8,128)S(1)} collective-permute-done((f32[2,128,1536]{2,1,0:T(8,128)S(1)}, f32[2,128,1536]{2,1,0:T(8,128)S(1)}, u32[]{:S(2)}, u32[]{:S(2)}) %collective-permute-start.17) | collective-permute-done | bytes 1572896 | tf_op jit(solution)/shard_map/ppermute | solution.py:33
  125.1 1.2 collective-permute-start.18
  126.4 2.2 %fusion.28 = f32[2,512,2,256]{1,3,2,0:T(8,128)S(1)} fusion(f32[2,256,512]{2,1,0:T(8,128)} %get-tuple-element.47, f32[2,256,128]{2,1,0:T(8,128)S(1)} %get-tuple-element.16, f32[2,256,128]{2,1,0:T(8,128)S(1)} %get-tuple-element.15), kind=kOutput, calls=%fused_computation.73 | convolution fusion | flops 805437440 | bytes 3670016 | tf_op jit(solution)/shard_map/aik,bkj->abij/dot_general | solution.py:78
  129.1 2.2 %fusion.20 = f32[2,512,2,256]{1,3,2,0:T(8,128)S(1)} fusion(f32[2,256,512]{2,1,0:T(8,128)} %collective-permute-done.14, f32[2,256,128]{2,1,0:T(8,128)S(1)} %get-tuple-element.25, f32[2,256,128]{2,1,0:T(8,128)S(1)} %get-tuple-element.24), kind=kOutput, calls=%fused_computation.65 | convolution fusion | flops 805437440 | bytes 3670016 | tf_op jit(solution)/shard_map/aik,bkj->abij/dot_general | solution.py:78
  131.3 1.0 fusion.22
  132.3 2.2 %fusion.24 = f32[2,512,2,256]{1,3,2,0:T(8,128)S(1)} fusion(f32[2,256,512]{2,1,0:T(8,128)} %collective-permute-done.12, f32[2,256,128]{2,1,0:T(8,128)S(1)} %get-tuple-element.21, f32[2,256,128]{2,1,0:T(8,128)S(1)} %get-tuple-element.20), kind=kOutput, calls=%fused_computation.69 | convolution fusion | flops 805437440 | bytes 3670016 | tf_op jit(solution)/shard_map/aik,bkj->abij/dot_general | solution.py:78
  134.6 2.2 %fusion.26 = f32[2,512,2,256]{1,3,2,0:T(8,128)S(1)} fusion(f32[2,256,512]{2,1,0:T(8,128)} %collective-permute-done.11, f32[2,256,128]{2,1,0:T(8,128)S(1)} %get-tuple-element.19, f32[2,256,128]{2,1,0:T(8,128)S(1)} %get-tuple-element.17), kind=kOutput, calls=%fused_computation.71 | convolution fusion | flops 805437440 | bytes 3670016 | tf_op jit(solution)/shard_map/aik,bkj->abij/dot_general | solution.py:78
  136.8 1.0 fusion.30
  141.2 1.0 fusion.18
  142.2 2.0 %add_bitcast_fusion = f32[2,2,256,512]{3,2,0,1:T(8,128)S(1)} fusion(f32[2,512,2,256]{1,3,2,0:T(8,128)S(1)} %fusion.18, f32[2,512,2,256]{1,3,2,0:T(8,128)S(1)} %fusion.20, f32[2,512,2,256]{1,3,2,0:T(8,128)S(1)} %fusion.22, f32[2,512,2,256]{1,3,2,0:T(8,128)S(1)} %fusion.24, f32[2,512,2,256]{1,3,2,0:T(8,128)S(1)} %fusion.26, ...), kind=kOutput, calls=%fused_computation.49 | convolution fusion | flops 809107456 | bytes 18350080 | tf_op jit(solution)/shard_map/aik,bkj->abij/dot_general | solution.py:78
  144.3 10.3 %fusion.4 = f32[2,2,256,512]{3,2,0,1:T(8,128)S(1)} fusion(f32[2,128,2048]{2,1,0:T(8,128)S(1)} %collective-permute-done.18, f32[2,128,2048]{2,1,0:T(8,128)} %slice_dynamic-update-slice_fusion, f32[2,2048,512]{2,1,0:T(8,128)} %slice_dynamic-update-slice_fusion.3), kind=kOutput, calls=%fused_computation.50 | convolution fusion | flops 6443499520 | bytes 14680064 | tf_op jit(solution)/shard_map/aik,bkj->abij/dot_general | solution.py:78
  154.6 1.8 fusion.34
  156.4 1.5 fusion.38
  159.1 1.2 collective-permute-start.21
  160.7 10.7 %collective-permute-done.20 = f32[2,128,512]{2,1,0:T(8,128)S(1)} collective-permute-done((f32[2,128,512]{2,1,0:T(8,128)S(1)}, f32[2,128,512]{2,1,0:T(8,128)S(1)}, u32[]{:S(2)}, u32[]{:S(2)}) %collective-permute-start.20) | collective-permute-done | bytes 524320 | tf_op jit(solution)/shard_map/ppermute | solution.py:33
  171.5 11.8 %collective-permute-done.21 = f32[2,128,512]{2,1,0:T(8,128)S(1)} collective-permute-done((f32[2,128,512]{2,1,0:T(8,128)S(1)}, f32[2,128,512]{2,1,0:T(8,128)S(1)}, u32[]{:S(2)}, u32[]{:S(2)}) %collective-permute-start.21) | collective-permute-done | bytes 524320 | tf_op jit(solution)/shard_map/ppermute | solution.py:33
  (60 shorter events, 20.4 us)
Async XLA Ops:
  12.0 12.9 %collective-permute-start = (f32[2,128,256]{2,0,1:T(2,128)}, f32[2,128,256]{2,0,1:T(2,128)}, u32[]{:S(2)}, u32[]{:S(2)}) collective-permute-start(f32[2,128,256]{2,0,1:T(2,128)} %get-tuple-element.45), channel_id=1, source_target_pairs={{0,16},{16,32},{32,48},{48,64},{64,80},{80,96},{96,112},{112,0},{1... | collective-permute-start | bytes 786440 | tf_op jit(solution)/shard_map/ppermute | solution.py:51
  14.0 19.8 %collective-permute-start.1 = (f32[2,128,256]{2,0,1:T(2,128)}, f32[2,128,256]{2,0,1:T(2,128)}, u32[]{:S(2)}, u32[]{:S(2)}) collective-permute-start(f32[2,128,256]{2,0,1:T(2,128)} %get-tuple-element.44), channel_id=1, source_target_pairs={{0,32},{16,48},{32,64},{48,80},{64,96},{80,112},{96,0},{112,16},{1... | collective-permute-start | bytes 786440 | tf_op jit(solution)/shard_map/ppermute | solution.py:51
  16.5 19.2 %collective-permute-start.2 = (f32[2,128,256]{2,0,1:T(2,128)}, f32[2,128,256]{2,0,1:T(2,128)}, u32[]{:S(2)}, u32[]{:S(2)}) collective-permute-start(f32[2,128,256]{2,0,1:T(2,128)} %get-tuple-element.43), channel_id=1, source_target_pairs={{0,48},{16,64},{32,80},{48,96},{64,112},{80,0},{96,16},{112,32},{1... | collective-permute-start | bytes 786440 | tf_op jit(solution)/shard_map/ppermute | solution.py:51
  20.9 21.6 %collective-permute-start.3 = (f32[2,128,256]{2,0,1:T(2,128)S(1)}, f32[2,128,256]{2,0,1:T(2,128)}, u32[]{:S(2)}, u32[]{:S(2)}) collective-permute-start(f32[2,128,256]{2,0,1:T(2,128)S(1)} %get-tuple-element.42), channel_id=1, source_target_pairs={{0,64},{16,80},{32,96},{48,112},{64,0},{80,16},{96,32},{112,48},{1... | collective-permute-start | bytes 786440 | tf_op jit(solution)/shard_map/ppermute | solution.py:51
  20.9 22.6 %collective-permute-start.4 = (f32[2,128,256]{2,0,1:T(2,128)S(1)}, f32[2,128,256]{2,0,1:T(2,128)}, u32[]{:S(2)}, u32[]{:S(2)}) collective-permute-start(f32[2,128,256]{2,0,1:T(2,128)S(1)} %get-tuple-element.41), channel_id=1, source_target_pairs={{0,80},{16,96},{32,112},{48,0},{64,16},{80,32},{96,48},{112,64},{1... | collective-permute-start | bytes 786440 | tf_op jit(solution)/shard_map/ppermute | solution.py:51
  24.9 19.6 %collective-permute-start.5 = (f32[2,128,256]{2,0,1:T(2,128)S(1)}, f32[2,128,256]{2,0,1:T(2,128)S(1)}, u32[]{:S(2)}, u32[]{:S(2)}) collective-permute-start(f32[2,128,256]{2,0,1:T(2,128)S(1)} %get-tuple-element.40), channel_id=1, source_target_pairs={{0,96},{16,112},{32,0},{48,16},{64,32},{80,48},{96,64},{112,80},{1... | collective-permute-start | bytes 786440 | tf_op jit(solution)/shard_map/ppermute | solution.py:51
  33.8 12.3 %collective-permute-start.6 = (f32[2,128,256]{2,0,1:T(2,128)S(1)}, f32[2,128,256]{2,0,1:T(2,128)S(1)}, u32[]{:S(2)}, u32[]{:S(2)}) collective-permute-start(f32[2,128,256]{2,0,1:T(2,128)S(1)} %get-tuple-element.39), channel_id=1, source_target_pairs={{0,112},{16,0},{32,16},{48,32},{64,48},{80,64},{96,80},{112,96},{1... | collective-permute-start | bytes 786440 | tf_op jit(solution)/shard_map/ppermute | solution.py:51
  52.3 3.4 %collective-permute-start.7 = (f32[2,128,512]{2,1,0:T(8,128)S(1)}, f32[2,128,512]{2,1,0:T(8,128)S(1)}, u32[]{:S(2)}, u32[]{:S(2)}) collective-permute-start(f32[2,128,512]{2,1,0:T(8,128)S(1)} %get-tuple-element.31), channel_id=1, source_target_pairs={{0,1},{1,0},{2,3},{3,2},{4,5},{5,4},{6,7},{7,6},{8,9},{9,8},{10,11... | collective-permute-start | bytes 1572872 | tf_op jit(solution)/shard_map/ppermute | solution.py:33
  54.1 13.8 %collective-permute-start.9 = (f32[2,128,512]{2,1,0:T(8,128)}, f32[2,128,512]{2,1,0:T(8,128)}, u32[]{:S(2)}, u32[]{:S(2)}) collective-permute-start(f32[2,128,512]{2,1,0:T(8,128)} %get-tuple-element.36), channel_id=1, source_target_pairs={{0,2},{1,3},{2,0},{3,1},{4,6},{5,7},{6,4},{7,5},{8,10},{9,11},{10,... | collective-permute-start | bytes 1572872 | tf_op jit(solution)/shard_map/ppermute | solution.py:33
  54.9 24.6 %collective-permute-start.10 = (f32[2,128,512]{2,1,0:T(8,128)}, f32[2,128,512]{2,1,0:T(8,128)}, u32[]{:S(2)}, u32[]{:S(2)}) collective-permute-start(f32[2,128,512]{2,1,0:T(8,128)} %get-tuple-element.35), channel_id=1, source_target_pairs={{0,3},{1,2},{2,1},{3,0},{4,7},{5,6},{6,5},{7,4},{8,11},{9,10},{10,... | collective-permute-start | bytes 1572872 | tf_op jit(solution)/shard_map/ppermute | solution.py:33
  56.8 30.1 %collective-permute-start.11 = (f32[2,256,512]{2,1,0:T(8,128)}, f32[2,256,512]{2,1,0:T(8,128)}, u32[]{:S(2)}, u32[]{:S(2)}) collective-permute-start(f32[2,256,512]{2,1,0:T(8,128)} %pad_maximum_fusion.2), channel_id=1, source_target_pairs={{0,4},{1,5},{2,6},{3,7},{4,8},{5,9},{6,10},{7,11},{8,12},{9,13},{1... | collective-permute-start | bytes 3145736 | tf_op jit(solution)/shard_map/ppermute | solution.py:33
  58.1 33.4 %collective-permute-start.12 = (f32[2,256,512]{2,1,0:T(8,128)}, f32[2,256,512]{2,1,0:T(8,128)}, u32[]{:S(2)}, u32[]{:S(2)}) collective-permute-start(f32[2,256,512]{2,1,0:T(8,128)} %pad_maximum_fusion.2), channel_id=1, source_target_pairs={{0,12},{1,13},{2,14},{3,15},{4,0},{5,1},{6,2},{7,3},{8,4},{9,5},{1... | collective-permute-start | bytes 3145736 | tf_op jit(solution)/shard_map/ppermute | solution.py:33
  69.4 15.1 %copy-start.1 = (f32[1,2]{1,0:T(1,128)S(1)}, f32[1,2]{1,0:T(1,128)}, u32[]{:S(2)}) copy-start(f32[1,2]{1,0:T(1,128)} %param.3) | copy-start | bytes 28
  81.7 25.7 %collective-permute-start.14 = (f32[2,256,512]{2,1,0:T(8,128)}, f32[2,256,512]{2,1,0:T(8,128)}, u32[]{:S(2)}, u32[]{:S(2)}) collective-permute-start(f32[2,256,512]{2,1,0:T(8,128)} %get-tuple-element.47), channel_id=1, source_target_pairs={{0,12},{1,13},{2,14},{3,15},{4,0},{5,1},{6,2},{7,3},{8,4},{9,5},{1... | collective-permute-start | bytes 3145736 | tf_op jit(solution)/shard_map/ppermute | solution.py:33
  85.1 41.1 %collective-permute-start.8 = (f32[2,128,2048]{2,1,0:T(8,128)S(1)}, f32[2,128,2048]{2,1,0:T(8,128)S(1)}, u32[]{:S(2)}, u32[]{:S(2)}) collective-permute-start(f32[2,128,2048]{2,1,0:T(8,128)S(1)} %copy_dynamic-update-slice_fusion), channel_id=1, source_target_pairs={{0,1},{1,0},{2,3},{3,2},{4,5},{5,4},{6,7},{7,6},{8,9},{9,8},{10,11... | collective-permute-start | bytes 6291464 | tf_op jit(solution)/shard_map/ppermute | solution.py:33
  85.3 29.3 %collective-permute-start.13 = (f32[2,256,512]{2,1,0:T(8,128)}, f32[2,256,512]{2,1,0:T(8,128)S(1)}, u32[]{:S(2)}, u32[]{:S(2)}) collective-permute-start(f32[2,256,512]{2,1,0:T(8,128)} %get-tuple-element.47), channel_id=1, source_target_pairs={{0,4},{1,5},{2,6},{3,7},{4,8},{5,9},{6,10},{7,11},{8,12},{9,13},{1... | collective-permute-start | bytes 3145736 | tf_op jit(solution)/shard_map/ppermute | solution.py:33
  86.8 35.7 %collective-permute-start.17 = (f32[2,128,1536]{2,1,0:T(8,128)S(1)}, f32[2,128,1536]{2,1,0:T(8,128)S(1)}, u32[]{:S(2)}, u32[]{:S(2)}) collective-permute-start(f32[2,128,1536]{2,1,0:T(8,128)S(1)} %pad_maximum_fusion), channel_id=1, source_target_pairs={{0,2},{1,3},{2,0},{3,1},{4,6},{5,7},{6,4},{7,5},{8,10},{9,11},{10,... | collective-permute-start | bytes 4718600 | tf_op jit(solution)/shard_map/ppermute | solution.py:33
  91.5 46.4 %collective-permute-start.15 = (f32[2,256,512]{2,1,0:T(8,128)}, f32[2,256,512]{2,1,0:T(8,128)S(1)}, u32[]{:S(2)}, u32[]{:S(2)}) collective-permute-start(f32[2,256,512]{2,1,0:T(8,128)} %collective-permute-done.11), channel_id=1, source_target_pairs={{0,4},{1,5},{2,6},{3,7},{4,8},{5,9},{6,10},{7,11},{8,12},{9,13},{1... | collective-permute-start | bytes 3145736 | tf_op jit(solution)/shard_map/ppermute | solution.py:33
  107.4 32.1 %collective-permute-start.16 = (f32[2,256,512]{2,1,0:T(8,128)}, f32[2,256,512]{2,1,0:T(8,128)S(1)}, u32[]{:S(2)}, u32[]{:S(2)}) collective-permute-start(f32[2,256,512]{2,1,0:T(8,128)} %collective-permute-done.14), channel_id=1, source_target_pairs={{0,12},{1,13},{2,14},{3,15},{4,0},{5,1},{6,2},{7,3},{8,4},{9,5},{1... | collective-permute-start | bytes 3145736 | tf_op jit(solution)/shard_map/ppermute | solution.py:33
  125.1 19.2 %collective-permute-start.18 = (f32[2,128,2048]{2,1,0:T(8,128)}, f32[2,128,2048]{2,1,0:T(8,128)S(1)}, u32[]{:S(2)}, u32[]{:S(2)}) collective-permute-start(f32[2,128,2048]{2,1,0:T(8,128)} %slice_dynamic-update-slice_fusion), channel_id=1, source_target_pairs={{0,1},{1,0},{2,3},{3,2},{4,5},{5,4},{6,7},{7,6},{8,9},{9,8},{10,11... | collective-permute-start | bytes 6291464 | tf_op jit(solution)/shard_map/ppermute | solution.py:33
  158.2 2.5 %collective-permute-start.19 = (f32[2,128,512]{2,1,0:T(8,128)S(1)}, f32[2,128,512]{2,1,0:T(8,128)S(1)}, u32[]{:S(2)}, u32[]{:S(2)}) collective-permute-start(f32[2,128,512]{2,1,0:T(8,128)S(1)} %get-tuple-element.29), channel_id=1, source_target_pairs={{0,1},{1,0},{2,3},{3,2},{4,5},{5,4},{6,7},{7,6},{8,9},{9,8},{10,11... | collective-permute-start | bytes 1572872 | tf_op jit(solution)/shard_map/ppermute | solution.py:33
  158.2 13.1 %collective-permute-start.20 = (f32[2,128,512]{2,1,0:T(8,128)S(1)}, f32[2,128,512]{2,1,0:T(8,128)S(1)}, u32[]{:S(2)}, u32[]{:S(2)}) collective-permute-start(f32[2,128,512]{2,1,0:T(8,128)S(1)} %get-tuple-element.30), channel_id=1, source_target_pairs={{0,2},{1,3},{2,0},{3,1},{4,6},{5,7},{6,4},{7,5},{8,10},{9,11},{10,... | collective-permute-start | bytes 1572872 | tf_op jit(solution)/shard_map/ppermute | solution.py:33
  159.1 24.1 %collective-permute-start.21 = (f32[2,128,512]{2,1,0:T(8,128)S(1)}, f32[2,128,512]{2,1,0:T(8,128)S(1)}, u32[]{:S(2)}, u32[]{:S(2)}) collective-permute-start(f32[2,128,512]{2,1,0:T(8,128)S(1)} %get-tuple-element.28), channel_id=1, source_target_pairs={{0,3},{1,2},{2,1},{3,0},{4,7},{5,6},{6,5},{7,4},{8,11},{9,10},{10,... | collective-permute-start | bytes 1572872 | tf_op jit(solution)/shard_map/ppermute | solution.py:33
  171.4 11.8 %copy-start = (f32[1,2,128,2048]{3,2,1,0:T(8,128)}, f32[1,2,128,2048]{3,2,1,0:T(8,128)S(1)}, u32[]{:S(2)}) copy-start(f32[1,2,128,2048]{3,2,1,0:T(8,128)S(1)} %bitcast_dynamic-update-slice_fusion.1) | copy-start | bytes 6291460
